TPU v7x, 128 devices: a whole 4x4x4 slice. The times are simulated.
128 devices in a mesh: hot: 4 (over z), dom: 32 (over y, x, core).
Axes of the slice: x: 4, y: 4, z: 4, core: 2. Of those that a mesh axis runs over, the one named last changes fastest.
Arguments:
- macro_adjoint: float32 [16, 6], P('hot'), may hold values from -6 to 6
- slip_code: int32 [32, 64, 4096], P('hot', 'dom'), may hold values from 0 to 4095
- grain_id: int32 [32, 64, 4096], P('hot', 'dom'), may hold values from 0 to 63
- grain_modulus: float32 [64], replicated, may hold values from 0.5 to 4
- slip_softening: float32 [64, 12], replicated, may hold values from 0.1 to 1.5
- rve_spot: int32 [32], P('hot'), may hold values from 0 to 15, as said below
Outputs:
- sensitivity: float32 [16, 6], P('hot')
- adjoint_field: float32 [32, 3, 64, 4096], P('hot', None, 'dom')
Inputs may be any that keep to these rules, and one draw needn't show every extreme that they name: `rve_spot`: every hot-spot is named by exactly 2 RVEs.
All inputs are finite; a program needn't handle non-finite values.
Results may differ from a plain program's by a relative error of at most 0.0003.
Values sent between devices are 32-bit elements; how exact they have to be, the bound alone decides.
No kernel may reach another device: no remote copies, remote signals or barrier semaphores. Data moves between devices by JAX's collectives and lax.ppermute only.
A program may use at most 64 MiB of HBM per device.

v0:
```python
import jax
import jax.numpy as jnp
from jax import lax
from jax.experimental import pallas as pl
from jax.sharding import Mesh, PartitionSpec as P

RES = 64
SLIPS = 12
GRAINS = 64
ITERS = 8
RVES = 32


mass_term = 0.02


def padded_2(value, sides, width):
    for axis, dim in sides:
        devices, length = (lax.axis_size(axis), value.shape[dim])
        up = [(i, (i + 1) % devices) for i in range(devices - 1)]
        down = [(j, i) for i, j in up]
        last = lax.slice_in_dim(value, length - width, length, axis=dim)
        leading = lax.slice_in_dim(value, 0, width, axis=dim)
        before = lax.ppermute(last, axis, up)
        after = lax.ppermute(leading, axis, down)
        value = jnp.concatenate([before, value, after], axis=dim)
    return value


def xor_groups(size):
    bits = size.bit_length() - 1
    if size != 1 << bits:
        return None
    groups = [(0, 1)] if bits % 2 else []
    lo = bits % 2
    while lo < bits:
        groups.append((lo, 2))
        lo += 2
    return groups


def tree_sum(vals, nb):
    cur = dict(vals)
    for level in range(nb):
        cur = {o: v + cur[o | (1 << level)] for o, v in cur.items() if not o & (1 << level)}
    return cur[0]


def axis_sum(value, axis):
    size = lax.axis_size(axis)
    groups = xor_groups(size)
    if groups is None:
        return lax.psum(value, axis)
    for lo, nb in groups:
        vals = {0: value}
        for o in range(1, 1 << nb):
            mask = o << lo
            vals[o] = lax.ppermute(value, axis, [(i, i ^ mask) for i in range(size)])
        value = tree_sum(vals, nb)
    return value


def axis_gather(value, axis):
    size = lax.axis_size(axis)
    if xor_groups(size) is None:
        return [lax.all_gather(value, axis, axis=0, tiled=True)], None
    parts = [value] + [
        lax.ppermute(value, axis, [(i, i ^ o) for i in range(size)]) for o in range(1, size)
    ]
    return parts, lax.axis_index(axis)


def axis_reduce_scatter(value, axis):
    size = lax.axis_size(axis)
    if xor_groups(size) is None:
        return lax.psum_scatter(value, axis, scatter_dimension=0, tiled=True)
    me = lax.axis_index(axis)
    block = value.shape[0] // size
    nb = size.bit_length() - 1
    vals = {0: lax.dynamic_slice_in_dim(value, me * block, block, 0)}
    for o in range(1, size):
        wanted = lax.dynamic_slice_in_dim(value, (me ^ o) * block, block, 0)
        vals[o] = lax.ppermute(wanted, axis, [(i, i ^ o) for i in range(size)])
    return tree_sum(vals, nb)


CHUNK = 512


def stiffness_kernel(pieces_ref, codes_ref, grains_ref, out_ref):
    rows = pieces_ref.shape[1]

    def chunk(c, carry):
        at = pl.multiple_of(c * CHUNK, CHUNK)
        for plane in range(codes_ref.shape[1]):
            grains = grains_ref[0, plane : plane + 1, pl.ds(at, CHUNK)]
            codes = codes_ref[0, plane : plane + 1, pl.ds(at, CHUNK)]
            onehot = (lax.broadcasted_iota(jnp.int32, (GRAINS, CHUNK), 0) == grains).astype(jnp.bfloat16)
            looked = jnp.dot(pieces_ref[0], onehot, preferred_element_type=jnp.float32)
            looked = looked + jnp.dot(pieces_ref[1], onehot, preferred_element_type=jnp.float32)
            looked = looked + jnp.dot(pieces_ref[2], onehot, preferred_element_type=jnp.float32)
            softening = jnp.zeros((1, CHUNK), jnp.float32)
            for slip in range(SLIPS):
                active = ((codes >> slip) & 1).astype(jnp.float32)
                softening = softening + active * looked[1 + slip : 2 + slip, :]
            out_ref[0, plane : plane + 1, pl.ds(at, CHUNK)] = looked[0:1, :] / (1.0 + softening)
        return carry

    lax.fori_loop(0, codes_ref.shape[2] // CHUNK, chunk, 0)
    del rows


def stiffness(table, slip_code, grain_id):
    high = lax.reduce_precision(table, exponent_bits=8, mantissa_bits=7)
    rest = table - high
    middle = lax.reduce_precision(rest, exponent_bits=8, mantissa_bits=7)
    low = rest - middle
    pieces = jnp.stack([high, middle, low]).astype(jnp.bfloat16)
    pieces = jnp.pad(pieces, ((0, 0), (0, 16 - table.shape[0]), (0, 0)))
    rves, planes, cells = slip_code.shape
    block = pl.BlockSpec((1, planes, cells), lambda r: (r, 0, 0))
    return pl.pallas_call(
        stiffness_kernel,
        grid=(rves,),
        in_specs=[pl.BlockSpec(pieces.shape, lambda r: (0, 0, 0)), block, block],
        out_specs=block,
        out_shape=jax.ShapeDtypeStruct(slip_code.shape, jnp.float32),
    )(pieces, slip_code, grain_id)


def shift_cells(field, step):
    filler = jnp.zeros(field.shape[:-1] + (abs(step),), field.dtype)
    if step > 0:
        return jnp.concatenate([field[..., step:], filler], -1)
    return jnp.concatenate([filler, field[..., :step]], -1)


def local_dot(first, second):
    return jnp.sum(first * second, axis=(1, 2, 3))


def shards(macro_adjoint, slip_code, grain_id, grain_modulus, slip_softening, rve_spot):
    rve_count = slip_code.shape[0]
    cells = slip_code.shape[2]
    spot_count = macro_adjoint.shape[0] * lax.axis_size("hot")
    column = jnp.arange(cells) % RES
    upper_mask = (column != RES - 1).astype(jnp.float32)
    lower_mask = (column != 0).astype(jnp.float32)
    table = jnp.concatenate([grain_modulus[None, :], slip_softening.T], 0)

    def stiff_one(inputs):
        codes, grain_cells = inputs
        flat_codes = codes.reshape(-1)
        flat_grains = grain_cells.reshape(-1)
        onehot = (jnp.arange(GRAINS)[:, None] == flat_grains[None, :]).astype(jnp.float32)
        looked = jnp.dot(
            table, onehot, precision=lax.Precision.HIGHEST, preferred_element_type=jnp.float32
        )
        softening = jnp.zeros(flat_codes.shape, jnp.float32)
        for slip in range(SLIPS):
            active = (flat_codes // 2**slip % 2).astype(jnp.float32)
            softening = softening + active * looked[1 + slip]
        return (looked[0] / (1.0 + softening)).reshape(codes.shape)

    spot_onehot = (rve_spot[:, None] == jnp.arange(spot_count)[None, :]).astype(jnp.float32)
    parts, hot_me = axis_gather(macro_adjoint, "hot")
    if hot_me is None:
        all_strains = parts[0]
    else:
        local = macro_adjoint.shape[0]
        ordered = []
        for j in range(len(parts)):
            pick = [(hot_me ^ o) == j for o in range(len(parts))]
            block = parts[0]
            for o in range(1, len(parts)):
                block = jnp.where(pick[o], parts[o], block)
            ordered.append(block)
        all_strains = jnp.concatenate(ordered, 0)
    strains = jnp.dot(
        spot_onehot,
        all_strains,
        precision=lax.Precision.HIGHEST,
        preferred_element_type=jnp.float32,
    )
    stiff_slabs = stiffness(table, slip_code, grain_id)
    stiff = lax.all_to_all(stiff_slabs, "xc", 0, 1, tiled=True)
    mine = lax.axis_index("xc")
    strains = lax.dynamic_slice_in_dim(strains, mine, 1, 0)
    padded = padded_2(stiff, (("yb", 1),), 1)

    def squares(residual):
        return axis_sum(local_dot(residual, residual), "yb")

    near_xup = padded[:, 2:]
    near_xdn = padded[:, :-2]
    near_yup = shift_cells(stiff, RES)
    near_ydn = shift_cells(stiff, -RES)
    near_zup = shift_cells(stiff, 1) * upper_mask
    near_zdn = shift_cells(stiff, -1) * lower_mask
    face_xup = 0.5 * (stiff + near_xup)
    face_xdn = 0.5 * (stiff + near_xdn)
    face_yup = 0.5 * (stiff + near_yup)
    face_ydn = 0.5 * (stiff + near_ydn)
    face_zup = 0.5 * (stiff + near_zup)
    face_zdn = 0.5 * (stiff + near_zdn)
    diagonal_sum = (mass_term + face_xup + face_xdn + face_yup + face_ydn + face_zup + face_zdn)[
        :, None
    ]
    gradients = [
        0.5 * (near_xup - near_xdn),
        0.5 * (near_yup - near_ydn),
        0.5 * (near_zup - near_zdn),
    ]
    tensor = [
        [strains[:, 0], strains[:, 5], strains[:, 4]],
        [strains[:, 5], strains[:, 1], strains[:, 3]],
        [strains[:, 4], strains[:, 3], strains[:, 2]],
    ]
    source = jnp.stack(
        [
            gradients[0] * tensor[comp][0][:, None, None]
            + gradients[1] * tensor[comp][1][:, None, None]
            + gradients[2] * tensor[comp][2][:, None, None]
            for comp in range(3)
        ],
        1,
    )

    def expand(values):
        return values[:, None, None, None]

    def boundary_planes(value):
        size = lax.axis_size("yb")
        up = [(i, i + 1) for i in range(size - 1)]
        down = [(i + 1, i) for i in range(size - 1)]
        before = lax.ppermute(value[:, :, -1:], "yb", up)
        after = lax.ppermute(value[:, :, :1], "yb", down)
        return jnp.concatenate([before, after], 2)

    def operate(direction, edges):
        wide = jnp.concatenate([edges[:, :, :1], direction, edges[:, :, 1:]], 2)
        return (
            diagonal_sum * direction
            - face_xup[:, None] * wide[:, :, 2:]
            - face_xdn[:, None] * wide[:, :, :-2]
            - face_yup[:, None] * shift_cells(direction, RES)
            - face_ydn[:, None] * shift_cells(direction, -RES)
            - face_zup[:, None] * (shift_cells(direction, 1) * upper_mask)
            - face_zdn[:, None] * (shift_cells(direction, -1) * lower_mask)
        )

    answer = jnp.zeros_like(source)
    residual = source
    direction = source
    residual_edges = boundary_planes(source)
    direction_edges = residual_edges
    for step in range(ITERS):
        image = operate(direction, direction_edges)
        last = step + 1 == ITERS
        if not last:
            image_edges = boundary_planes(image)
        local = jnp.stack(
            [
                local_dot(direction, image),
                local_dot(residual, residual),
                local_dot(residual, image),
                local_dot(image, image),
            ],
            -1,
        )
        sums = axis_sum(local, "yb")
        norm_now = sums[:, 1]
        alpha = norm_now / sums[:, 0]
        answer = answer + expand(alpha) * direction
        if last:
            break
        norm_next = norm_now - 2.0 * alpha * sums[:, 2] + alpha * alpha * sums[:, 3]
        beta = expand(norm_next / norm_now)
        residual = residual - expand(alpha) * image
        residual_edges = residual_edges - expand(alpha) * image_edges
        direction = residual + beta * direction
        direction_edges = residual_edges + beta * direction_edges
    volume = float(RES**3)
    stiff_part = jnp.sum(stiff, axis=(1, 2)) / volume
    moment = [
        [jnp.sum(answer[:, comp] * gradients[other], axis=(1, 2)) for other in range(3)]
        for comp in range(3)
    ]
    pairs = [(0, 0), (1, 1), (2, 2), (1, 2), (0, 2), (0, 1)]
    partial_here = jnp.stack(
        [
            stiff_part * strains[:, slot]
            - 0.5
            * (moment[pairs[slot][0]][pairs[slot][1]] + moment[pairs[slot][1]][pairs[slot][0]])
            / volume
            for slot in range(6)
        ],
        1,
    )
    per_spot = float(rve_count * lax.axis_size("hot") // spot_count)
    rve_one = axis_sum(partial_here, "yb")
    placed = (jnp.arange(rve_count)[:, None] == mine).astype(jnp.float32) * rve_one
    rve_totals = axis_sum(placed, "xc")
    spot_local = jnp.dot(
        spot_onehot.T,
        rve_totals,
        precision=lax.Precision.HIGHEST,
        preferred_element_type=jnp.float32,
    )
    owned = axis_reduce_scatter(spot_local, "hot")
    return (owned / per_spot, lax.all_to_all(answer, "xc", 2, 0, tiled=True))


def solution(mesh):
    hot, dom = mesh.shape["hot"], mesh.shape["dom"]
    rves_here = RVES // hot
    grouped = Mesh(mesh.devices.reshape(hot, dom // rves_here, rves_here), ("hot", "yb", "xc"))
    return jax.shard_map(
        shards,
        mesh=grouped,
        in_specs=(
            P("hot", None),
            P("hot", ("yb", "xc"), None),
            P("hot", ("yb", "xc"), None),
            P(),
            P(),
            P("hot"),
        ),
        out_specs=(P("hot", None), P("hot", None, ("yb", "xc"), None)),
        check_vma=False,
    )
```

profile of v0, /device:TPU:0, one launch (start us, length us, event | category | flops | bytes accessed | tf_op | source)
XLA Modules:
  0.0 279.0 jit_solution(6680186240454881646)
XLA Ops:
  0.6 4.1 %collective-permute-start.1 = (f32[4,6]{1,0:T(4,128)}, f32[4,6]{1,0:T(4,128)S(1)}, u32[]{:S(2)}, u32[]{:S(2)}) collective-permute-start(f32[4,6]{1,0:T(4,128)} %param.6), channel_id=1, source_target_pairs={{0,64},{32,96},{64,0},{96,32},{1,65},{33,97},{65,1},{97,33},{2,66}... | collective-permute-start | bytes 296 | tf_op jit(solution)/shard_map/ppermute | solution.py:68
  7.7 15.0 %shard_map.77 = f32[8,2,4096]{2,1,0:T(2,128)} custom-call(bf16[3,16,64]{2,1,0:T(8,128)(2,1)} %fusion.95.pieces_ref, s32[8,2,4096]{2,1,0:T(2,128)} %codes_ref.1, s32[8,2,4096]{2,1,0:T(2,128)} %grains_ref.1), custom_call_target="tpu_custom_call" | custom-call | tf_op jit(solution)/shard_map/pallas_call | solution.py:122
  22.7 4.3 %all-to-all-start = ((f32[8,2,4096]{2,1,0:T(2,128)}), f32[8,2,4096]{2,1,0:T(2,128)S(1)}, u32[]{:S(2)}, u32[]{:S(2)}) async-start(f32[8,2,4096]{2,1,0:T(2,128)} %shard_map.77), calls=%async_computation | async-start | bytes 524288 | tf_op jit(solution)/shard_map/all_to_all | solution.py:186
  33.0 1.5 all-to-all-done
  34.8 1.3 collective-permute-start.3
  36.1 4.5 %collective-permute-start.4 = (f32[1,1,4096]{2,1,0:T(1,128)S(1)}, f32[1,1,4096]{2,1,0:T(1,128)S(1)}, u32[]{:S(2)}, u32[]{:S(2)}) collective-permute-start(f32[1,1,4096]{2,1,0:T(1,128)S(1)} %get-tuple-element.149), channel_id=1, source_target_pairs={{0,8},{8,16},{16,24},{1,9},{9,17},{17,25},{2,10},{10,18},{18,26},{... | collective-permute-start | bytes 49160 | tf_op jit(solution)/shard_map/ppermute | solution.py:24
  48.5 4.5 %collective-permute-start.6 = (f32[1,3,1,4096]{3,2,1,0:T(1,128)S(1)}, f32[1,3,1,4096]{3,2,1,0:T(1,128)S(1)}, u32[]{:S(2)}, u32[]{:S(2)}) collective-permute-start(f32[1,3,1,4096]{3,2,1,0:T(1,128)S(1)} %get-tuple-element.132), channel_id=1, source_target_pairs={{0,8},{8,16},{16,24},{1,9},{9,17},{17,25},{2,10},{10,18},{18,26},{... | collective-permute-start | bytes 147464 | tf_op jit(solution)/shard_map/ppermute | solution.py:236
  53.4 1.4 collective-permute-done.6
  54.8 1.5 multiply_reduce_fusion.29
  56.3 1.9 pad_maximum_fusion.25
  58.2 4.0 %collective-permute-start.8 = (f32[1,4]{1,0:T(1,128)S(1)}, f32[1,4]{1,0:T(1,128)S(1)}, u32[]{:S(2)}, u32[]{:S(2)}) collective-permute-start(f32[1,4]{1,0:T(1,128)S(1)} %pad_maximum_fusion.25), channel_id=1, source_target_pairs={{0,16},{8,24},{16,0},{24,8},{1,17},{9,25},{17,1},{25,9},{2,18},{10... | collective-permute-start | bytes 56 | tf_op jit(solution)/shard_map/ppermute | solution.py:58
  63.3 3.9 %collective-permute-start.10 = (f32[1,3,1,4096]{3,2,1,0:T(1,128)S(1)}, f32[1,3,1,4096]{3,2,1,0:T(1,128)S(1)}, u32[]{:S(2)}, u32[]{:S(2)}) collective-permute-start(f32[1,3,1,4096]{3,2,1,0:T(1,128)S(1)} %get-tuple-element.125), channel_id=1, source_target_pairs={{0,8},{8,16},{16,24},{1,9},{9,17},{17,25},{2,10},{10,18},{18,26},{... | collective-permute-start | bytes 147464 | tf_op jit(solution)/shard_map/ppermute | solution.py:236
  67.3 1.3 collective-permute-start.11
  68.6 1.9 add_add_fusion.7
  76.1 1.6 multiply_reduce_fusion.27
  77.7 2.7 pad_maximum_fusion.26
  80.4 4.3 %collective-permute-start.13 = (f32[1,4]{1,0:T(1,128)S(1)}, f32[1,4]{1,0:T(1,128)S(1)}, u32[]{:S(2)}, u32[]{:S(2)}) collective-permute-start(f32[1,4]{1,0:T(1,128)S(1)} %pad_maximum_fusion.26), channel_id=1, source_target_pairs={{0,16},{8,24},{16,0},{24,8},{1,17},{9,25},{17,1},{25,9},{2,18},{10... | collective-permute-start | bytes 56 | tf_op jit(solution)/shard_map/ppermute | solution.py:58
  85.8 3.9 %collective-permute-start.15 = (f32[1,3,1,4096]{3,2,1,0:T(1,128)S(1)}, f32[1,3,1,4096]{3,2,1,0:T(1,128)S(1)}, u32[]{:S(2)}, u32[]{:S(2)}) collective-permute-start(f32[1,3,1,4096]{3,2,1,0:T(1,128)S(1)} %get-tuple-element.119), channel_id=1, source_target_pairs={{0,8},{8,16},{16,24},{1,9},{9,17},{17,25},{2,10},{10,18},{18,26},{... | collective-permute-start | bytes 147464 | tf_op jit(solution)/shard_map/ppermute | solution.py:236
  89.7 1.3 collective-permute-start.16
  91.1 2.7 add_add_fusion.6
  99.4 1.6 multiply_reduce_fusion.23
  101.0 2.6 pad_maximum_fusion.27
  103.6 4.3 %collective-permute-start.18 = (f32[1,4]{1,0:T(1,128)S(1)}, f32[1,4]{1,0:T(1,128)S(1)}, u32[]{:S(2)}, u32[]{:S(2)}) collective-permute-start(f32[1,4]{1,0:T(1,128)S(1)} %pad_maximum_fusion.27), channel_id=1, source_target_pairs={{0,16},{8,24},{16,0},{24,8},{1,17},{9,25},{17,1},{25,9},{2,18},{10... | collective-permute-start | bytes 56 | tf_op jit(solution)/shard_map/ppermute | solution.py:58
  109.0 3.9 %collective-permute-start.20 = (f32[1,3,1,4096]{3,2,1,0:T(1,128)S(1)}, f32[1,3,1,4096]{3,2,1,0:T(1,128)S(1)}, u32[]{:S(2)}, u32[]{:S(2)}) collective-permute-start(f32[1,3,1,4096]{3,2,1,0:T(1,128)S(1)} %get-tuple-element.113), channel_id=1, source_target_pairs={{0,8},{8,16},{16,24},{1,9},{9,17},{17,25},{2,10},{10,18},{18,26},{... | collective-permute-start | bytes 147464 | tf_op jit(solution)/shard_map/ppermute | solution.py:236
  112.9 1.5 collective-permute-start.21
  114.4 2.6 add_add_fusion.5
  122.7 1.6 multiply_reduce_fusion.19
  124.3 2.6 pad_maximum_fusion.28
  126.9 4.3 %collective-permute-start.23 = (f32[1,4]{1,0:T(1,128)S(1)}, f32[1,4]{1,0:T(1,128)S(1)}, u32[]{:S(2)}, u32[]{:S(2)}) collective-permute-start(f32[1,4]{1,0:T(1,128)S(1)} %pad_maximum_fusion.28), channel_id=1, source_target_pairs={{0,16},{8,24},{16,0},{24,8},{1,17},{9,25},{17,1},{25,9},{2,18},{10... | collective-permute-start | bytes 56 | tf_op jit(solution)/shard_map/ppermute | solution.py:58
  132.3 3.9 %collective-permute-start.25 = (f32[1,3,1,4096]{3,2,1,0:T(1,128)S(1)}, f32[1,3,1,4096]{3,2,1,0:T(1,128)S(1)}, u32[]{:S(2)}, u32[]{:S(2)}) collective-permute-start(f32[1,3,1,4096]{3,2,1,0:T(1,128)S(1)} %get-tuple-element.107), channel_id=1, source_target_pairs={{0,8},{8,16},{16,24},{1,9},{9,17},{17,25},{2,10},{10,18},{18,26},{... | collective-permute-start | bytes 147464 | tf_op jit(solution)/shard_map/ppermute | solution.py:236
  137.6 2.6 add_add_fusion.4
  145.7 1.6 multiply_reduce_fusion.15
  147.3 2.6 pad_maximum_fusion.29
  149.9 4.3 %collective-permute-start.28 = (f32[1,4]{1,0:T(1,128)S(1)}, f32[1,4]{1,0:T(1,128)S(1)}, u32[]{:S(2)}, u32[]{:S(2)}) collective-permute-start(f32[1,4]{1,0:T(1,128)S(1)} %pad_maximum_fusion.29), channel_id=1, source_target_pairs={{0,16},{8,24},{16,0},{24,8},{1,17},{9,25},{17,1},{25,9},{2,18},{10... | collective-permute-start | bytes 56 | tf_op jit(solution)/shard_map/ppermute | solution.py:58
  155.3 3.9 %collective-permute-start.30 = (f32[1,3,1,4096]{3,2,1,0:T(1,128)S(1)}, f32[1,3,1,4096]{3,2,1,0:T(1,128)S(1)}, u32[]{:S(2)}, u32[]{:S(2)}) collective-permute-start(f32[1,3,1,4096]{3,2,1,0:T(1,128)S(1)} %get-tuple-element.101), channel_id=1, source_target_pairs={{0,8},{8,16},{16,24},{1,9},{9,17},{17,25},{2,10},{10,18},{18,26},{... | collective-permute-start | bytes 147464 | tf_op jit(solution)/shard_map/ppermute | solution.py:236
  160.6 2.6 add_add_fusion.3
  168.6 1.5 multiply_reduce_fusion.11
  170.1 2.6 pad_maximum_fusion.30
  172.7 4.3 %collective-permute-start.33 = (f32[1,4]{1,0:T(1,128)S(1)}, f32[1,4]{1,0:T(1,128)S(1)}, u32[]{:S(2)}, u32[]{:S(2)}) collective-permute-start(f32[1,4]{1,0:T(1,128)S(1)} %pad_maximum_fusion.30), channel_id=1, source_target_pairs={{0,16},{8,24},{16,0},{24,8},{1,17},{9,25},{17,1},{25,9},{2,18},{10... | collective-permute-start | bytes 56 | tf_op jit(solution)/shard_map/ppermute | solution.py:58
  178.1 3.9 %collective-permute-start.35 = (f32[1,3,1,4096]{3,2,1,0:T(1,128)S(1)}, f32[1,3,1,4096]{3,2,1,0:T(1,128)S(1)}, u32[]{:S(2)}, u32[]{:S(2)}) collective-permute-start(f32[1,3,1,4096]{3,2,1,0:T(1,128)S(1)} %get-tuple-element.95), channel_id=1, source_target_pairs={{0,8},{8,16},{16,24},{1,9},{9,17},{17,25},{2,10},{10,18},{18,26},{... | collective-permute-start | bytes 147464 | tf_op jit(solution)/shard_map/ppermute | solution.py:236
  183.3 2.6 add_add_fusion.2
  191.3 1.6 multiply_reduce_fusion.7
  192.9 2.6 pad_maximum_fusion.31
  195.4 4.3 %collective-permute-start.38 = (f32[1,4]{1,0:T(1,128)S(1)}, f32[1,4]{1,0:T(1,128)S(1)}, u32[]{:S(2)}, u32[]{:S(2)}) collective-permute-start(f32[1,4]{1,0:T(1,128)S(1)} %pad_maximum_fusion.31), channel_id=1, source_target_pairs={{0,16},{8,24},{16,0},{24,8},{1,17},{9,25},{17,1},{25,9},{2,18},{10... | collective-permute-start | bytes 56 | tf_op jit(solution)/shard_map/ppermute | solution.py:58
  200.8 3.9 %collective-permute-start.40 = (f32[1,3,1,4096]{3,2,1,0:T(1,128)S(1)}, f32[1,3,1,4096]{3,2,1,0:T(1,128)S(1)}, u32[]{:S(2)}, u32[]{:S(2)}) collective-permute-start(f32[1,3,1,4096]{3,2,1,0:T(1,128)S(1)} %get-tuple-element.93), channel_id=1, source_target_pairs={{0,8},{8,16},{16,24},{1,9},{9,17},{17,25},{2,10},{10,18},{18,26},{... | collective-permute-start | bytes 147464 | tf_op jit(solution)/shard_map/ppermute | solution.py:236
  206.1 2.6 add_add_fusion.1
  214.2 1.6 multiply_reduce_fusion.3
  215.8 2.6 pad_maximum_fusion.32
  218.4 4.3 %collective-permute-start.43 = (f32[1,4]{1,0:T(1,128)S(1)}, f32[1,4]{1,0:T(1,128)S(1)}, u32[]{:S(2)}, u32[]{:S(2)}) collective-permute-start(f32[1,4]{1,0:T(1,128)S(1)} %pad_maximum_fusion.32), channel_id=1, source_target_pairs={{0,16},{8,24},{16,0},{24,8},{1,17},{9,25},{17,1},{25,9},{2,18},{10... | collective-permute-start | bytes 56 | tf_op jit(solution)/shard_map/ppermute | solution.py:58
  224.3 3.2 %collective-permute-done.44 = f32[1,4]{1,0:T(1,128)S(1)} collective-permute-done((f32[1,4]{1,0:T(1,128)S(1)}, f32[1,4]{1,0:T(1,128)S(1)}, u32[]{:S(2)}, u32[]{:S(2)}) %collective-permute-start.44) | collective-permute-done | bytes 48 | tf_op jit(solution)/shard_map/ppermute | solution.py:58
  227.5 2.6 add_add_fusion
  241.3 2.0 collective-permute-start.47
  243.4 2.1 collective-permute-start.45
  246.1 2.3 collective-permute-done.46
  248.6 1.7 copy.46
  250.3 3.5 %all-to-all-start.1 = ((f32[1,3,16,4096]{3,0,1,2:T(1,128)}), f32[1,3,16,4096]{3,0,1,2:T(1,128)S(1)}, u32[]{:S(2)}, u32[]{:S(2)}) async-start(f32[1,3,16,4096]{3,0,1,2:T(1,128)} %copy.46), calls=%async_computation.1 | async-start | bytes 1572864 | tf_op jit(solution)/shard_map/all_to_all | solution.py:311
  253.9 3.2 %collective-permute-start.51 = (f32[8,6]{1,0:T(8,128)S(1)}, f32[8,6]{1,0:T(8,128)S(1)}, u32[]{:S(2)}, u32[]{:S(2)}) collective-permute-start(f32[8,6]{1,0:T(8,128)S(1)} %fusion.111), channel_id=1, source_target_pairs={{0,6},{1,7},{2,4},{3,5},{4,2},{5,3},{6,0},{7,1},{8,14},{9,15},{10,... | collective-permute-start | bytes 584 | tf_op jit(solution)/shard_map/ppermute | solution.py:58
  258.0 5.8 %collective-permute-done.51 = f32[8,6]{1,0:T(8,128)S(1)} collective-permute-done((f32[8,6]{1,0:T(8,128)S(1)}, f32[8,6]{1,0:T(8,128)S(1)}, u32[]{:S(2)}, u32[]{:S(2)}) %collective-permute-start.51) | collective-permute-done | bytes 224 | tf_op jit(solution)/shard_map/ppermute | solution.py:58
  263.8 3.2 %collective-permute-done.50 = f32[8,6]{1,0:T(8,128)S(1)} collective-permute-done((f32[8,6]{1,0:T(8,128)S(1)}, f32[8,6]{1,0:T(8,128)S(1)}, u32[]{:S(2)}, u32[]{:S(2)}) %collective-permute-start.50) | collective-permute-done | bytes 224 | tf_op jit(solution)/shard_map/ppermute | solution.py:58
  267.3 1.7 collective-permute-start.52
  269.0 2.5 collective-permute-start.54
  271.6 2.3 collective-permute-done.54
  273.8 2.8 %collective-permute-done.53 = f32[4,6]{0,1:T(8,128)S(1)} collective-permute-done((f32[4,6]{0,1:T(8,128)S(1)}, f32[4,6]{0,1:T(8,128)S(1)}, u32[]{:S(2)}, u32[]{:S(2)}) %collective-permute-start.53) | collective-permute-done | bytes 128 | tf_op jit(solution)/shard_map/ppermute | solution.py:83
  277.5 1.5 copy.52
  (164 shorter events, 40.5 us)
Async XLA Ops:
  0.6 26.4 %collective-permute-start.1 = (f32[4,6]{1,0:T(4,128)}, f32[4,6]{1,0:T(4,128)S(1)}, u32[]{:S(2)}, u32[]{:S(2)}) collective-permute-start(f32[4,6]{1,0:T(4,128)} %param.6), channel_id=1, source_target_pairs={{0,64},{32,96},{64,0},{96,32},{1,65},{33,97},{65,1},{97,33},{2,66}... | collective-permute-start | bytes 296 | tf_op jit(solution)/shard_map/ppermute | solution.py:68
  4.7 22.3 %collective-permute-start = (f32[4,6]{1,0:T(4,128)}, f32[4,6]{1,0:T(4,128)S(1)}, u32[]{:S(2)}, u32[]{:S(2)}) collective-permute-start(f32[4,6]{1,0:T(4,128)} %param.6), channel_id=1, source_target_pairs={{0,96},{32,64},{64,32},{96,0},{1,97},{33,65},{65,33},{97,1},{2,98}... | collective-permute-start | bytes 296 | tf_op jit(solution)/shard_map/ppermute | solution.py:68
  5.4 21.6 %collective-permute-start.2 = (f32[4,6]{1,0:T(4,128)}, f32[4,6]{1,0:T(4,128)S(1)}, u32[]{:S(2)}, u32[]{:S(2)}) collective-permute-start(f32[4,6]{1,0:T(4,128)} %param.6), channel_id=1, source_target_pairs={{0,32},{32,0},{64,96},{96,64},{1,33},{33,1},{65,97},{97,65},{2,34}... | collective-permute-start | bytes 296 | tf_op jit(solution)/shard_map/ppermute | solution.py:68
  5.7 0.7 copy-start.1
  22.7 11.8 %all-to-all-start = ((f32[8,2,4096]{2,1,0:T(2,128)}), f32[8,2,4096]{2,1,0:T(2,128)S(1)}, u32[]{:S(2)}, u32[]{:S(2)}) async-start(f32[8,2,4096]{2,1,0:T(2,128)} %shard_map.77), calls=%async_computation | async-start | bytes 524288 | tf_op jit(solution)/shard_map/all_to_all | solution.py:186
  27.0 0.7 copy-start
  27.7 0.7 copy-start.2
  34.8 11.3 %collective-permute-start.3 = (f32[1,1,4096]{2,1,0:T(1,128)S(1)}, f32[1,1,4096]{2,1,0:T(1,128)S(1)}, u32[]{:S(2)}, u32[]{:S(2)}) collective-permute-start(f32[1,1,4096]{2,1,0:T(1,128)S(1)} %get-tuple-element.148), channel_id=1, source_target_pairs={{8,0},{16,8},{24,16},{9,1},{17,9},{25,17},{10,2},{18,10},{26,18},{... | collective-permute-start | bytes 49160 | tf_op jit(solution)/shard_map/ppermute | solution.py:25
  36.1 10.0 %collective-permute-start.4 = (f32[1,1,4096]{2,1,0:T(1,128)S(1)}, f32[1,1,4096]{2,1,0:T(1,128)S(1)}, u32[]{:S(2)}, u32[]{:S(2)}) collective-permute-start(f32[1,1,4096]{2,1,0:T(1,128)S(1)} %get-tuple-element.149), channel_id=1, source_target_pairs={{0,8},{8,16},{16,24},{1,9},{9,17},{17,25},{2,10},{10,18},{18,26},{... | collective-permute-start | bytes 49160 | tf_op jit(solution)/shard_map/ppermute | solution.py:24
  47.2 6.1 %collective-permute-start.5 = (f32[1,3,1,4096]{3,2,1,0:T(1,128)S(1)}, f32[1,3,1,4096]{3,2,1,0:T(1,128)S(1)}, u32[]{:S(2)}, u32[]{:S(2)}) collective-permute-start(f32[1,3,1,4096]{3,2,1,0:T(1,128)S(1)} %get-tuple-element.131), channel_id=1, source_target_pairs={{8,0},{16,8},{24,16},{9,1},{17,9},{25,17},{10,2},{18,10},{26,18},{... | collective-permute-start | bytes 147464 | tf_op jit(solution)/shard_map/ppermute | solution.py:237
  48.5 6.3 %collective-permute-start.6 = (f32[1,3,1,4096]{3,2,1,0:T(1,128)S(1)}, f32[1,3,1,4096]{3,2,1,0:T(1,128)S(1)}, u32[]{:S(2)}, u32[]{:S(2)}) collective-permute-start(f32[1,3,1,4096]{3,2,1,0:T(1,128)S(1)} %get-tuple-element.132), channel_id=1, source_target_pairs={{0,8},{8,16},{16,24},{1,9},{9,17},{17,25},{2,10},{10,18},{18,26},{... | collective-permute-start | bytes 147464 | tf_op jit(solution)/shard_map/ppermute | solution.py:236
  58.2 10.3 %collective-permute-start.8 = (f32[1,4]{1,0:T(1,128)S(1)}, f32[1,4]{1,0:T(1,128)S(1)}, u32[]{:S(2)}, u32[]{:S(2)}) collective-permute-start(f32[1,4]{1,0:T(1,128)S(1)} %pad_maximum_fusion.25), channel_id=1, source_target_pairs={{0,16},{8,24},{16,0},{24,8},{1,17},{9,25},{17,1},{25,9},{2,18},{10... | collective-permute-start | bytes 56 | tf_op jit(solution)/shard_map/ppermute | solution.py:58
  62.2 6.4 %collective-permute-start.9 = (f32[1,4]{1,0:T(1,128)S(1)}, f32[1,4]{1,0:T(1,128)S(1)}, u32[]{:S(2)}, u32[]{:S(2)}) collective-permute-start(f32[1,4]{1,0:T(1,128)S(1)} %pad_maximum_fusion.25), channel_id=1, source_target_pairs={{0,24},{8,16},{16,8},{24,0},{1,25},{9,17},{17,9},{25,1},{2,26},{10... | collective-permute-start | bytes 56 | tf_op jit(solution)/shard_map/ppermute | solution.py:58
  63.2 5.3 %collective-permute-start.7 = (f32[1,4]{1,0:T(1,128)S(1)}, f32[1,4]{1,0:T(1,128)S(1)}, u32[]{:S(2)}, u32[]{:S(2)}) collective-permute-start(f32[1,4]{1,0:T(1,128)S(1)} %pad_maximum_fusion.25), channel_id=1, source_target_pairs={{0,8},{8,0},{16,24},{24,16},{1,9},{9,1},{17,25},{25,17},{2,10},{10... | collective-permute-start | bytes 56 | tf_op jit(solution)/shard_map/ppermute | solution.py:58
  63.3 12.5 %collective-permute-start.10 = (f32[1,3,1,4096]{3,2,1,0:T(1,128)S(1)}, f32[1,3,1,4096]{3,2,1,0:T(1,128)S(1)}, u32[]{:S(2)}, u32[]{:S(2)}) collective-permute-start(f32[1,3,1,4096]{3,2,1,0:T(1,128)S(1)} %get-tuple-element.125), channel_id=1, source_target_pairs={{0,8},{8,16},{16,24},{1,9},{9,17},{17,25},{2,10},{10,18},{18,26},{... | collective-permute-start | bytes 147464 | tf_op jit(solution)/shard_map/ppermute | solution.py:236
  67.3 8.6 %collective-permute-start.11 = (f32[1,3,1,4096]{3,2,1,0:T(1,128)S(1)}, f32[1,3,1,4096]{3,2,1,0:T(1,128)S(1)}, u32[]{:S(2)}, u32[]{:S(2)}) collective-permute-start(f32[1,3,1,4096]{3,2,1,0:T(1,128)S(1)} %get-tuple-element.126), channel_id=1, source_target_pairs={{8,0},{16,8},{24,16},{9,1},{17,9},{25,17},{10,2},{18,10},{26,18},{... | collective-permute-start | bytes 147464 | tf_op jit(solution)/shard_map/ppermute | solution.py:237
  80.4 10.7 %collective-permute-start.13 = (f32[1,4]{1,0:T(1,128)S(1)}, f32[1,4]{1,0:T(1,128)S(1)}, u32[]{:S(2)}, u32[]{:S(2)}) collective-permute-start(f32[1,4]{1,0:T(1,128)S(1)} %pad_maximum_fusion.26), channel_id=1, source_target_pairs={{0,16},{8,24},{16,0},{24,8},{1,17},{9,25},{17,1},{25,9},{2,18},{10... | collective-permute-start | bytes 56 | tf_op jit(solution)/shard_map/ppermute | solution.py:58
  84.7 6.4 %collective-permute-start.14 = (f32[1,4]{1,0:T(1,128)S(1)}, f32[1,4]{1,0:T(1,128)S(1)}, u32[]{:S(2)}, u32[]{:S(2)}) collective-permute-start(f32[1,4]{1,0:T(1,128)S(1)} %pad_maximum_fusion.26), channel_id=1, source_target_pairs={{0,24},{8,16},{16,8},{24,0},{1,25},{9,17},{17,9},{25,1},{2,26},{10... | collective-permute-start | bytes 56 | tf_op jit(solution)/shard_map/ppermute | solution.py:58
  85.7 5.3 %collective-permute-start.12 = (f32[1,4]{1,0:T(1,128)S(1)}, f32[1,4]{1,0:T(1,128)S(1)}, u32[]{:S(2)}, u32[]{:S(2)}) collective-permute-start(f32[1,4]{1,0:T(1,128)S(1)} %pad_maximum_fusion.26), channel_id=1, source_target_pairs={{0,8},{8,0},{16,24},{24,16},{1,9},{9,1},{17,25},{25,17},{2,10},{10... | collective-permute-start | bytes 56 | tf_op jit(solution)/shard_map/ppermute | solution.py:58
  85.8 13.1 %collective-permute-start.15 = (f32[1,3,1,4096]{3,2,1,0:T(1,128)S(1)}, f32[1,3,1,4096]{3,2,1,0:T(1,128)S(1)}, u32[]{:S(2)}, u32[]{:S(2)}) collective-permute-start(f32[1,3,1,4096]{3,2,1,0:T(1,128)S(1)} %get-tuple-element.119), channel_id=1, source_target_pairs={{0,8},{8,16},{16,24},{1,9},{9,17},{17,25},{2,10},{10,18},{18,26},{... | collective-permute-start | bytes 147464 | tf_op jit(solution)/shard_map/ppermute | solution.py:236
  89.7 9.2 %collective-permute-start.16 = (f32[1,3,1,4096]{3,2,1,0:T(1,128)S(1)}, f32[1,3,1,4096]{3,2,1,0:T(1,128)S(1)}, u32[]{:S(2)}, u32[]{:S(2)}) collective-permute-start(f32[1,3,1,4096]{3,2,1,0:T(1,128)S(1)} %get-tuple-element.120), channel_id=1, source_target_pairs={{8,0},{16,8},{24,16},{9,1},{17,9},{25,17},{10,2},{18,10},{26,18},{... | collective-permute-start | bytes 147464 | tf_op jit(solution)/shard_map/ppermute | solution.py:237
  103.6 10.8 %collective-permute-start.18 = (f32[1,4]{1,0:T(1,128)S(1)}, f32[1,4]{1,0:T(1,128)S(1)}, u32[]{:S(2)}, u32[]{:S(2)}) collective-permute-start(f32[1,4]{1,0:T(1,128)S(1)} %pad_maximum_fusion.27), channel_id=1, source_target_pairs={{0,16},{8,24},{16,0},{24,8},{1,17},{9,25},{17,1},{25,9},{2,18},{10... | collective-permute-start | bytes 56 | tf_op jit(solution)/shard_map/ppermute | solution.py:58
  107.8 6.6 %collective-permute-start.19 = (f32[1,4]{1,0:T(1,128)S(1)}, f32[1,4]{1,0:T(1,128)S(1)}, u32[]{:S(2)}, u32[]{:S(2)}) collective-permute-start(f32[1,4]{1,0:T(1,128)S(1)} %pad_maximum_fusion.27), channel_id=1, source_target_pairs={{0,24},{8,16},{16,8},{24,0},{1,25},{9,17},{17,9},{25,1},{2,26},{10... | collective-permute-start | bytes 56 | tf_op jit(solution)/shard_map/ppermute | solution.py:58
  108.9 5.5 %collective-permute-start.17 = (f32[1,4]{1,0:T(1,128)S(1)}, f32[1,4]{1,0:T(1,128)S(1)}, u32[]{:S(2)}, u32[]{:S(2)}) collective-permute-start(f32[1,4]{1,0:T(1,128)S(1)} %pad_maximum_fusion.27), channel_id=1, source_target_pairs={{0,8},{8,0},{16,24},{24,16},{1,9},{9,1},{17,25},{25,17},{2,10},{10... | collective-permute-start | bytes 56 | tf_op jit(solution)/shard_map/ppermute | solution.py:58
  109.0 13.2 %collective-permute-start.20 = (f32[1,3,1,4096]{3,2,1,0:T(1,128)S(1)}, f32[1,3,1,4096]{3,2,1,0:T(1,128)S(1)}, u32[]{:S(2)}, u32[]{:S(2)}) collective-permute-start(f32[1,3,1,4096]{3,2,1,0:T(1,128)S(1)} %get-tuple-element.113), channel_id=1, source_target_pairs={{0,8},{8,16},{16,24},{1,9},{9,17},{17,25},{2,10},{10,18},{18,26},{... | collective-permute-start | bytes 147464 | tf_op jit(solution)/shard_map/ppermute | solution.py:236
  112.9 9.3 %collective-permute-start.21 = (f32[1,3,1,4096]{3,2,1,0:T(1,128)S(1)}, f32[1,3,1,4096]{3,2,1,0:T(1,128)S(1)}, u32[]{:S(2)}, u32[]{:S(2)}) collective-permute-start(f32[1,3,1,4096]{3,2,1,0:T(1,128)S(1)} %get-tuple-element.114), channel_id=1, source_target_pairs={{8,0},{16,8},{24,16},{9,1},{17,9},{25,17},{10,2},{18,10},{26,18},{... | collective-permute-start | bytes 147464 | tf_op jit(solution)/shard_map/ppermute | solution.py:237
  126.9 10.7 %collective-permute-start.23 = (f32[1,4]{1,0:T(1,128)S(1)}, f32[1,4]{1,0:T(1,128)S(1)}, u32[]{:S(2)}, u32[]{:S(2)}) collective-permute-start(f32[1,4]{1,0:T(1,128)S(1)} %pad_maximum_fusion.28), channel_id=1, source_target_pairs={{0,16},{8,24},{16,0},{24,8},{1,17},{9,25},{17,1},{25,9},{2,18},{10... | collective-permute-start | bytes 56 | tf_op jit(solution)/shard_map/ppermute | solution.py:58
  131.2 6.4 %collective-permute-start.24 = (f32[1,4]{1,0:T(1,128)S(1)}, f32[1,4]{1,0:T(1,128)S(1)}, u32[]{:S(2)}, u32[]{:S(2)}) collective-permute-start(f32[1,4]{1,0:T(1,128)S(1)} %pad_maximum_fusion.28), channel_id=1, source_target_pairs={{0,24},{8,16},{16,8},{24,0},{1,25},{9,17},{17,9},{25,1},{2,26},{10... | collective-permute-start | bytes 56 | tf_op jit(solution)/shard_map/ppermute | solution.py:58
  132.2 5.3 %collective-permute-start.22 = (f32[1,4]{1,0:T(1,128)S(1)}, f32[1,4]{1,0:T(1,128)S(1)}, u32[]{:S(2)}, u32[]{:S(2)}) collective-permute-start(f32[1,4]{1,0:T(1,128)S(1)} %pad_maximum_fusion.28), channel_id=1, source_target_pairs={{0,8},{8,0},{16,24},{24,16},{1,9},{9,1},{17,25},{25,17},{2,10},{10... | collective-permute-start | bytes 56 | tf_op jit(solution)/shard_map/ppermute | solution.py:58
  132.3 13.2 %collective-permute-start.25 = (f32[1,3,1,4096]{3,2,1,0:T(1,128)S(1)}, f32[1,3,1,4096]{3,2,1,0:T(1,128)S(1)}, u32[]{:S(2)}, u32[]{:S(2)}) collective-permute-start(f32[1,3,1,4096]{3,2,1,0:T(1,128)S(1)} %get-tuple-element.107), channel_id=1, source_target_pairs={{0,8},{8,16},{16,24},{1,9},{9,17},{17,25},{2,10},{10,18},{18,26},{... | collective-permute-start | bytes 147464 | tf_op jit(solution)/shard_map/ppermute | solution.py:236
  136.2 9.2 %collective-permute-start.26 = (f32[1,3,1,4096]{3,2,1,0:T(1,128)S(1)}, f32[1,3,1,4096]{3,2,1,0:T(1,128)S(1)}, u32[]{:S(2)}, u32[]{:S(2)}) collective-permute-start(f32[1,3,1,4096]{3,2,1,0:T(1,128)S(1)} %get-tuple-element.108), channel_id=1, source_target_pairs={{8,0},{16,8},{24,16},{9,1},{17,9},{25,17},{10,2},{18,10},{26,18},{... | collective-permute-start | bytes 147464 | tf_op jit(solution)/shard_map/ppermute | solution.py:237
  149.9 10.7 %collective-permute-start.28 = (f32[1,4]{1,0:T(1,128)S(1)}, f32[1,4]{1,0:T(1,128)S(1)}, u32[]{:S(2)}, u32[]{:S(2)}) collective-permute-start(f32[1,4]{1,0:T(1,128)S(1)} %pad_maximum_fusion.29), channel_id=1, source_target_pairs={{0,16},{8,24},{16,0},{24,8},{1,17},{9,25},{17,1},{25,9},{2,18},{10... | collective-permute-start | bytes 56 | tf_op jit(solution)/shard_map/ppermute | solution.py:58
  154.2 6.4 %collective-permute-start.29 = (f32[1,4]{1,0:T(1,128)S(1)}, f32[1,4]{1,0:T(1,128)S(1)}, u32[]{:S(2)}, u32[]{:S(2)}) collective-permute-start(f32[1,4]{1,0:T(1,128)S(1)} %pad_maximum_fusion.29), channel_id=1, source_target_pairs={{0,24},{8,16},{16,8},{24,0},{1,25},{9,17},{17,9},{25,1},{2,26},{10... | collective-permute-start | bytes 56 | tf_op jit(solution)/shard_map/ppermute | solution.py:58
  155.2 5.3 %collective-permute-start.27 = (f32[1,4]{1,0:T(1,128)S(1)}, f32[1,4]{1,0:T(1,128)S(1)}, u32[]{:S(2)}, u32[]{:S(2)}) collective-permute-start(f32[1,4]{1,0:T(1,128)S(1)} %pad_maximum_fusion.29), channel_id=1, source_target_pairs={{0,8},{8,0},{16,24},{24,16},{1,9},{9,1},{17,25},{25,17},{2,10},{10... | collective-permute-start | bytes 56 | tf_op jit(solution)/shard_map/ppermute | solution.py:58
  155.3 12.9 %collective-permute-start.30 = (f32[1,3,1,4096]{3,2,1,0:T(1,128)S(1)}, f32[1,3,1,4096]{3,2,1,0:T(1,128)S(1)}, u32[]{:S(2)}, u32[]{:S(2)}) collective-permute-start(f32[1,3,1,4096]{3,2,1,0:T(1,128)S(1)} %get-tuple-element.101), channel_id=1, source_target_pairs={{0,8},{8,16},{16,24},{1,9},{9,17},{17,25},{2,10},{10,18},{18,26},{... | collective-permute-start | bytes 147464 | tf_op jit(solution)/shard_map/ppermute | solution.py:236
  159.3 9.0 %collective-permute-start.31 = (f32[1,3,1,4096]{3,2,1,0:T(1,128)S(1)}, f32[1,3,1,4096]{3,2,1,0:T(1,128)S(1)}, u32[]{:S(2)}, u32[]{:S(2)}) collective-permute-start(f32[1,3,1,4096]{3,2,1,0:T(1,128)S(1)} %get-tuple-element.102), channel_id=1, source_target_pairs={{8,0},{16,8},{24,16},{9,1},{17,9},{25,17},{10,2},{18,10},{26,18},{... | collective-permute-start | bytes 147464 | tf_op jit(solution)/shard_map/ppermute | solution.py:237
  172.7 10.7 %collective-permute-start.33 = (f32[1,4]{1,0:T(1,128)S(1)}, f32[1,4]{1,0:T(1,128)S(1)}, u32[]{:S(2)}, u32[]{:S(2)}) collective-permute-start(f32[1,4]{1,0:T(1,128)S(1)} %pad_maximum_fusion.30), channel_id=1, source_target_pairs={{0,16},{8,24},{16,0},{24,8},{1,17},{9,25},{17,1},{25,9},{2,18},{10... | collective-permute-start | bytes 56 | tf_op jit(solution)/shard_map/ppermute | solution.py:58
  177.0 6.4 %collective-permute-start.34 = (f32[1,4]{1,0:T(1,128)S(1)}, f32[1,4]{1,0:T(1,128)S(1)}, u32[]{:S(2)}, u32[]{:S(2)}) collective-permute-start(f32[1,4]{1,0:T(1,128)S(1)} %pad_maximum_fusion.30), channel_id=1, source_target_pairs={{0,24},{8,16},{16,8},{24,0},{1,25},{9,17},{17,9},{25,1},{2,26},{10... | collective-permute-start | bytes 56 | tf_op jit(solution)/shard_map/ppermute | solution.py:58
  178.0 5.3 %collective-permute-start.32 = (f32[1,4]{1,0:T(1,128)S(1)}, f32[1,4]{1,0:T(1,128)S(1)}, u32[]{:S(2)}, u32[]{:S(2)}) collective-permute-start(f32[1,4]{1,0:T(1,128)S(1)} %pad_maximum_fusion.30), channel_id=1, source_target_pairs={{0,8},{8,0},{16,24},{24,16},{1,9},{9,1},{17,25},{25,17},{2,10},{10... | collective-permute-start | bytes 56 | tf_op jit(solution)/shard_map/ppermute | solution.py:58
  178.1 13.0 %collective-permute-start.35 = (f32[1,3,1,4096]{3,2,1,0:T(1,128)S(1)}, f32[1,3,1,4096]{3,2,1,0:T(1,128)S(1)}, u32[]{:S(2)}, u32[]{:S(2)}) collective-permute-start(f32[1,3,1,4096]{3,2,1,0:T(1,128)S(1)} %get-tuple-element.95), channel_id=1, source_target_pairs={{0,8},{8,16},{16,24},{1,9},{9,17},{17,25},{2,10},{10,18},{18,26},{... | collective-permute-start | bytes 147464 | tf_op jit(solution)/shard_map/ppermute | solution.py:236
  182.0 9.1 %collective-permute-start.36 = (f32[1,3,1,4096]{3,2,1,0:T(1,128)S(1)}, f32[1,3,1,4096]{3,2,1,0:T(1,128)S(1)}, u32[]{:S(2)}, u32[]{:S(2)}) collective-permute-start(f32[1,3,1,4096]{3,2,1,0:T(1,128)S(1)} %get-tuple-element.96), channel_id=1, source_target_pairs={{8,0},{16,8},{24,16},{9,1},{17,9},{25,17},{10,2},{18,10},{26,18},{... | collective-permute-start | bytes 147464 | tf_op jit(solution)/shard_map/ppermute | solution.py:237
  195.4 10.7 %collective-permute-start.38 = (f32[1,4]{1,0:T(1,128)S(1)}, f32[1,4]{1,0:T(1,128)S(1)}, u32[]{:S(2)}, u32[]{:S(2)}) collective-permute-start(f32[1,4]{1,0:T(1,128)S(1)} %pad_maximum_fusion.31), channel_id=1, source_target_pairs={{0,16},{8,24},{16,0},{24,8},{1,17},{9,25},{17,1},{25,9},{2,18},{10... | collective-permute-start | bytes 56 | tf_op jit(solution)/shard_map/ppermute | solution.py:58
  199.7 6.4 %collective-permute-start.39 = (f32[1,4]{1,0:T(1,128)S(1)}, f32[1,4]{1,0:T(1,128)S(1)}, u32[]{:S(2)}, u32[]{:S(2)}) collective-permute-start(f32[1,4]{1,0:T(1,128)S(1)} %pad_maximum_fusion.31), channel_id=1, source_target_pairs={{0,24},{8,16},{16,8},{24,0},{1,25},{9,17},{17,9},{25,1},{2,26},{10... | collective-permute-start | bytes 56 | tf_op jit(solution)/shard_map/ppermute | solution.py:58
  200.8 5.3 %collective-permute-start.37 = (f32[1,4]{1,0:T(1,128)S(1)}, f32[1,4]{1,0:T(1,128)S(1)}, u32[]{:S(2)}, u32[]{:S(2)}) collective-permute-start(f32[1,4]{1,0:T(1,128)S(1)} %pad_maximum_fusion.31), channel_id=1, source_target_pairs={{0,8},{8,0},{16,24},{24,16},{1,9},{9,1},{17,25},{25,17},{2,10},{10... | collective-permute-start | bytes 56 | tf_op jit(solution)/shard_map/ppermute | solution.py:58
  200.8 13.1 %collective-permute-start.40 = (f32[1,3,1,4096]{3,2,1,0:T(1,128)S(1)}, f32[1,3,1,4096]{3,2,1,0:T(1,128)S(1)}, u32[]{:S(2)}, u32[]{:S(2)}) collective-permute-start(f32[1,3,1,4096]{3,2,1,0:T(1,128)S(1)} %get-tuple-element.93), channel_id=1, source_target_pairs={{0,8},{8,16},{16,24},{1,9},{9,17},{17,25},{2,10},{10,18},{18,26},{... | collective-permute-start | bytes 147464 | tf_op jit(solution)/shard_map/ppermute | solution.py:236
  204.8 9.1 %collective-permute-start.41 = (f32[1,3,1,4096]{3,2,1,0:T(1,128)S(1)}, f32[1,3,1,4096]{3,2,1,0:T(1,128)S(1)}, u32[]{:S(2)}, u32[]{:S(2)}) collective-permute-start(f32[1,3,1,4096]{3,2,1,0:T(1,128)S(1)} %get-tuple-element.94), channel_id=1, source_target_pairs={{8,0},{16,8},{24,16},{9,1},{17,9},{25,17},{10,2},{18,10},{26,18},{... | collective-permute-start | bytes 147464 | tf_op jit(solution)/shard_map/ppermute | solution.py:237
  218.4 5.9 %collective-permute-start.43 = (f32[1,4]{1,0:T(1,128)S(1)}, f32[1,4]{1,0:T(1,128)S(1)}, u32[]{:S(2)}, u32[]{:S(2)}) collective-permute-start(f32[1,4]{1,0:T(1,128)S(1)} %pad_maximum_fusion.32), channel_id=1, source_target_pairs={{0,16},{8,24},{16,0},{24,8},{1,17},{9,25},{17,1},{25,9},{2,18},{10... | collective-permute-start | bytes 56 | tf_op jit(solution)/shard_map/ppermute | solution.py:58
  222.7 4.8 %collective-permute-start.44 = (f32[1,4]{1,0:T(1,128)S(1)}, f32[1,4]{1,0:T(1,128)S(1)}, u32[]{:S(2)}, u32[]{:S(2)}) collective-permute-start(f32[1,4]{1,0:T(1,128)S(1)} %pad_maximum_fusion.32), channel_id=1, source_target_pairs={{0,24},{8,16},{16,8},{24,0},{1,25},{9,17},{17,9},{25,1},{2,26},{10... | collective-permute-start | bytes 56 | tf_op jit(solution)/shard_map/ppermute | solution.py:58
  223.8 3.7 %collective-permute-start.42 = (f32[1,4]{1,0:T(1,128)S(1)}, f32[1,4]{1,0:T(1,128)S(1)}, u32[]{:S(2)}, u32[]{:S(2)}) collective-permute-start(f32[1,4]{1,0:T(1,128)S(1)} %pad_maximum_fusion.32), channel_id=1, source_target_pairs={{0,8},{8,0},{16,24},{24,16},{1,9},{9,1},{17,25},{25,17},{2,10},{10... | collective-permute-start | bytes 56 | tf_op jit(solution)/shard_map/ppermute | solution.py:58
  241.3 4.8 %collective-permute-start.47 = (f32[1,6]{1,0:T(1,128)S(1)}, f32[1,6]{1,0:T(1,128)S(1)}, u32[]{:S(2)}, u32[]{:S(2)}) collective-permute-start(f32[1,6]{1,0:T(1,128)S(1)} %stack.208), channel_id=1, source_target_pairs={{0,24},{8,16},{16,8},{24,0},{1,25},{9,17},{17,9},{25,1},{2,26},{10... | collective-permute-start | bytes 80 | tf_op jit(solution)/shard_map/ppermute | solution.py:58
  243.4 5.1 %collective-permute-start.46 = (f32[1,6]{1,0:T(1,128)S(1)}, f32[1,6]{1,0:T(1,128)S(1)}, u32[]{:S(2)}, u32[]{:S(2)}) collective-permute-start(f32[1,6]{1,0:T(1,128)S(1)} %stack.208), channel_id=1, source_target_pairs={{0,16},{8,24},{16,0},{24,8},{1,17},{9,25},{17,1},{25,9},{2,18},{10... | collective-permute-start | bytes 80 | tf_op jit(solution)/shard_map/ppermute | solution.py:58
  243.4 5.1 %collective-permute-start.45 = (f32[1,6]{1,0:T(1,128)S(1)}, f32[1,6]{1,0:T(1,128)S(1)}, u32[]{:S(2)}, u32[]{:S(2)}) collective-permute-start(f32[1,6]{1,0:T(1,128)S(1)} %stack.208), channel_id=1, source_target_pairs={{0,8},{8,0},{16,24},{24,16},{1,9},{9,1},{17,25},{25,17},{2,10},{10... | collective-permute-start | bytes 80 | tf_op jit(solution)/shard_map/ppermute | solution.py:58
  248.5 5.3 %collective-permute-start.48 = (f32[8,6]{1,0:T(8,128)S(1)}, f32[8,6]{1,0:T(8,128)S(1)}, u32[]{:S(2)}, u32[]{:S(2)}) collective-permute-start(f32[8,6]{1,0:T(8,128)S(1)} %broadcast_multiply_fusion), channel_id=1, source_target_pairs={{0,1},{1,0},{2,3},{3,2},{4,5},{5,4},{6,7},{7,6},{8,9},{9,8},{10,11... | collective-permute-start | bytes 584 | tf_op jit(solution)/shard_map/ppermute | solution.py:58
  250.3 27.2 %all-to-all-start.1 = ((f32[1,3,16,4096]{3,0,1,2:T(1,128)}), f32[1,3,16,4096]{3,0,1,2:T(1,128)S(1)}, u32[]{:S(2)}, u32[]{:S(2)}) async-start(f32[1,3,16,4096]{3,0,1,2:T(1,128)} %copy.46), calls=%async_computation.1 | async-start | bytes 1572864 | tf_op jit(solution)/shard_map/all_to_all | solution.py:311
  253.9 9.9 %collective-permute-start.51 = (f32[8,6]{1,0:T(8,128)S(1)}, f32[8,6]{1,0:T(8,128)S(1)}, u32[]{:S(2)}, u32[]{:S(2)}) collective-permute-start(f32[8,6]{1,0:T(8,128)S(1)} %fusion.111), channel_id=1, source_target_pairs={{0,6},{1,7},{2,4},{3,5},{4,2},{5,3},{6,0},{7,1},{8,14},{9,15},{10,... | collective-permute-start | bytes 584 | tf_op jit(solution)/shard_map/ppermute | solution.py:58
  257.1 9.9 %collective-permute-start.50 = (f32[8,6]{1,0:T(8,128)S(1)}, f32[8,6]{1,0:T(8,128)S(1)}, u32[]{:S(2)}, u32[]{:S(2)}) collective-permute-start(f32[8,6]{1,0:T(8,128)S(1)} %fusion.111), channel_id=1, source_target_pairs={{0,4},{1,5},{2,6},{3,7},{4,0},{5,1},{6,2},{7,3},{8,12},{9,13},{10,... | collective-permute-start | bytes 584 | tf_op jit(solution)/shard_map/ppermute | solution.py:58
  257.9 9.1 %collective-permute-start.49 = (f32[8,6]{1,0:T(8,128)S(1)}, f32[8,6]{1,0:T(8,128)S(1)}, u32[]{:S(2)}, u32[]{:S(2)}) collective-permute-start(f32[8,6]{1,0:T(8,128)S(1)} %fusion.111), channel_id=1, source_target_pairs={{0,2},{1,3},{2,0},{3,1},{4,6},{5,7},{6,4},{7,5},{8,10},{9,11},{10,... | collective-permute-start | bytes 584 | tf_op jit(solution)/shard_map/ppermute | solution.py:58
  267.3 4.3 %collective-permute-start.52 = (f32[4,6]{0,1:T(8,128)S(1)}, f32[4,6]{0,1:T(8,128)S(1)}, u32[]{:S(2)}, u32[]{:S(2)}) collective-permute-start(f32[4,6]{0,1:T(8,128)S(1)} %get-tuple-element.171), channel_id=1, source_target_pairs={{0,32},{32,0},{64,96},{96,64},{1,33},{33,1},{65,97},{97,65},{2,34}... | collective-permute-start | bytes 296 | tf_op jit(solution)/shard_map/ppermute | solution.py:83
  269.0 4.8 %collective-permute-start.54 = (f32[4,6]{0,1:T(8,128)S(1)}, f32[4,6]{0,1:T(8,128)S(1)}, u32[]{:S(2)}, u32[]{:S(2)}) collective-permute-start(f32[4,6]{0,1:T(8,128)S(1)} %get-tuple-element.172), channel_id=1, source_target_pairs={{0,96},{32,64},{64,32},{96,0},{1,97},{33,65},{65,33},{97,1},{2,98}... | collective-permute-start | bytes 296 | tf_op jit(solution)/shard_map/ppermute | solution.py:83
  271.6 5.1 %collective-permute-start.53 = (f32[4,6]{0,1:T(8,128)S(1)}, f32[4,6]{0,1:T(8,128)S(1)}, u32[]{:S(2)}, u32[]{:S(2)}) collective-permute-start(f32[4,6]{0,1:T(8,128)S(1)} %get-tuple-element.173), channel_id=1, source_target_pairs={{0,64},{32,96},{64,0},{96,32},{1,65},{33,97},{65,1},{97,33},{2,66}... | collective-permute-start | bytes 296 | tf_op jit(solution)/shard_map/ppermute | solution.py:83
where the time goes:
time: 281 us; the launch traced here: 279 us
  starting transfers between devices  116 us (41%)
  other arithmetic  60.2 us (21%)
  between operations  45.5 us (16%)
  waiting for transfers between devices  23.9 us (9%)
  local copies, waits for them, and re-layouts  17.8 us (6%)
  Pallas kernels  15 us (5%)
    ppermute x31, starting transfers between devices, axis_sum(): vals[o] = lax.ppermute(value, axis, [(i, i ^ mask) for i in range(size)])  50.6 us
    ppermute x8, starting transfers between devices, boundary_planes(): before = lax.ppermute(value[:, :, -1:], 'yb', up)  32.1 us
    add x9, other arithmetic, tree_sum(): v + cur[o | 1 << level]  20.2 us
    another operation x8, other arithmetic, shards(): jnp.stack([local_dot(direction, image), local_dot(residual, residual), lo...  20.1 us
    ppermute x31, waiting for transfers between devices, axis_sum(): vals[o] = lax.ppermute(value, axis, [(i, i ^ mask) for i in range(size)])  15.8 us
    pallas_call x1, Pallas kernels, stiffness(): pl.pallas_call(stiffness_kernel, grid=(rves,), in_specs=[pl.BlockSpec(pie...  15 us
    reduce_sum x8, other arithmetic, local_dot(): return jnp.sum(first * second, axis=(1, 2, 3))  12.5 us
    ppermute x8, starting transfers between devices, boundary_planes(): after = lax.ppermute(value[:, :, :1], 'yb', down)  10.5 us
  transfers between devices with their start and end apart: 57, of which 10 were waited for; matrix products, arithmetic and copies ran while one was open for 12% of the time, Pallas kernels for 5%

commit v1 on v0

--- a/solution.py
+++ b/solution.py
@@ -186,17 +186,18 @@
     stiff = lax.all_to_all(stiff_slabs, "xc", 0, 1, tiled=True)
     mine = lax.axis_index("xc")
     strains = lax.dynamic_slice_in_dim(strains, mine, 1, 0)
-    padded = padded_2(stiff, (("yb", 1),), 1)
-
-    def squares(residual):
-        return axis_sum(local_dot(residual, residual), "yb")
-
-    near_xup = padded[:, 2:]
-    near_xdn = padded[:, :-2]
-    near_yup = shift_cells(stiff, RES)
-    near_ydn = shift_cells(stiff, -RES)
-    near_zup = shift_cells(stiff, 1) * upper_mask
-    near_zdn = shift_cells(stiff, -1) * lower_mask
+    padded = padded_2(stiff, (("yb", 1),), 2)
+    wide = padded[:, 1:-1]
+    wide_xup, wide_xdn = padded[:, 2:], padded[:, :-2]
+    wide_yup, wide_ydn = shift_cells(wide, RES), shift_cells(wide, -RES)
+    wide_zup, wide_zdn = shift_cells(wide, 1) * upper_mask, shift_cells(wide, -1) * lower_mask
+
+    def inner(planes):
+        return planes[:, 1:-1]
+
+    near_xup, near_xdn = inner(wide_xup), inner(wide_xdn)
+    near_yup, near_ydn = inner(wide_yup), inner(wide_ydn)
+    near_zup, near_zdn = inner(wide_zup), inner(wide_zdn)
     face_xup = 0.5 * (stiff + near_xup)
     face_xdn = 0.5 * (stiff + near_xdn)
     face_yup = 0.5 * (stiff + near_yup)
@@ -206,24 +207,34 @@
     diagonal_sum = (mass_term + face_xup + face_xdn + face_yup + face_ydn + face_zup + face_zdn)[
         :, None
     ]
-    gradients = [
-        0.5 * (near_xup - near_xdn),
-        0.5 * (near_yup - near_ydn),
-        0.5 * (near_zup - near_zdn),
-    ]
+    wide_gradients = [
+        0.5 * (wide_xup - wide_xdn),
+        0.5 * (wide_yup - wide_ydn),
+        0.5 * (wide_zup - wide_zdn),
+    ]
+    gradients = [inner(g) for g in wide_gradients]
     tensor = [
         [strains[:, 0], strains[:, 5], strains[:, 4]],
         [strains[:, 5], strains[:, 1], strains[:, 3]],
         [strains[:, 4], strains[:, 3], strains[:, 2]],
     ]
-    source = jnp.stack(
+    wide_source = jnp.stack(
         [
-            gradients[0] * tensor[comp][0][:, None, None]
-            + gradients[1] * tensor[comp][1][:, None, None]
-            + gradients[2] * tensor[comp][2][:, None, None]
+            wide_gradients[0] * tensor[comp][0][:, None, None]
+            + wide_gradients[1] * tensor[comp][1][:, None, None]
+            + wide_gradients[2] * tensor[comp][2][:, None, None]
             for comp in range(3)
         ],
         1,
+    )
+    source = wide_source[:, :, 1:-1]
+    plane_block = lax.axis_index("yb")
+    source_edges = jnp.concatenate(
+        [
+            jnp.where(plane_block != 0, wide_source[:, :, :1], 0.0),
+            jnp.where(plane_block != lax.axis_size("yb") - 1, wide_source[:, :, -1:], 0.0),
+        ],
+        2,
     )
 
     def expand(values):
@@ -252,22 +263,28 @@
     answer = jnp.zeros_like(source)
     residual = source
     direction = source
-    residual_edges = boundary_planes(source)
+    residual_edges = source_edges
     direction_edges = residual_edges
     for step in range(ITERS):
         image = operate(direction, direction_edges)
         last = step + 1 == ITERS
         if not last:
             image_edges = boundary_planes(image)
-        local = jnp.stack(
-            [
-                local_dot(direction, image),
-                local_dot(residual, residual),
-                local_dot(residual, image),
-                local_dot(image, image),
-            ],
-            -1,
-        )
+        terms = [
+            local_dot(direction, image),
+            local_dot(residual, residual),
+            local_dot(residual, image),
+            local_dot(image, image),
+        ]
+        if last:
+            for held in (answer, direction):
+                terms += [
+                    jnp.sum(held[:, comp] * gradients[other], axis=(1, 2))
+                    for comp in range(3)
+                    for other in range(3)
+                ]
+            terms.append(jnp.sum(stiff, axis=(1, 2)))
+        local = jnp.stack(terms, -1)
         sums = axis_sum(local, "yb")
         norm_now = sums[:, 1]
         alpha = norm_now / sums[:, 0]
@@ -281,13 +298,13 @@
         direction = residual + beta * direction
         direction_edges = residual_edges + beta * direction_edges
     volume = float(RES**3)
-    stiff_part = jnp.sum(stiff, axis=(1, 2)) / volume
+    stiff_part = sums[:, 22] / volume
     moment = [
-        [jnp.sum(answer[:, comp] * gradients[other], axis=(1, 2)) for other in range(3)]
+        [sums[:, 4 + 3 * comp + other] + alpha * sums[:, 13 + 3 * comp + other] for other in range(3)]
         for comp in range(3)
     ]
     pairs = [(0, 0), (1, 1), (2, 2), (1, 2), (0, 2), (0, 1)]
-    partial_here = jnp.stack(
+    rve_one = jnp.stack(
         [
             stiff_part * strains[:, slot]
             - 0.5
@@ -298,7 +315,6 @@
         1,
     )
     per_spot = float(rve_count * lax.axis_size("hot") // spot_count)
-    rve_one = axis_sum(partial_here, "yb")
     placed = (jnp.arange(rve_count)[:, None] == mine).astype(jnp.float32) * rve_one
     rve_totals = axis_sum(placed, "xc")
     spot_local = jnp.dot(

time: 281 us -> 282 us (level)
  local copies, waits for them, and re-layouts: 17.8 us -> 31.3 us
  starting transfers between devices: 116 us -> 104 us
  other arithmetic: 60.2 us -> 56.5 us
  between operations: 45.5 us -> 49 us
    another operation x0 -> x1, local copies, waits for them, and re-layouts: none -> 14.5 us  [shards(): local = jnp.stack(terms, -1)]
    ppermute x31 -> x28, starting transfers between devices: 50.6 us -> 45.2 us  [axis_sum(): vals[o] = lax.ppermute(value, axis, [(i, i ^ mask) for i in range(size)])]
    ppermute x8 -> x7, starting transfers between devices: 32.1 us -> 27.5 us  [boundary_planes(): before = lax.ppermute(value[:, :, -1:], 'yb', up)]
    ppermute x1, waiting for transfers between devices: 0.01 us -> 3.6 us  [padded_2(): after = lax.ppermute(leading, axis, down)]
    ppermute x31 -> x28, waiting for transfers between devices: 15.8 us -> 12.6 us  [axis_sum(): vals[o] = lax.ppermute(value, axis, [(i, i ^ mask) for i in range(size)])]
    another operation x12 -> x11, other arithmetic: 21.3 us -> 18.9 us  [the longest x7 17.5 us: shards(): local = jnp.stack(terms, -1)]
    ppermute x8 -> x7, starting transfers between devices: 10.5 us -> 9.04 us  [boundary_planes(): after = lax.ppermute(value[:, :, :1], 'yb', down)]
  transfers between devices with their start and end apart: 57 -> 52, of which waited for: 10 -> 9; matrix products, arithmetic and copies ran while one was open for 12% -> 13% of each run, Pallas kernels for 5% -> 5%
where the time goes in v1:
time: 282 us; the launch traced here: 280 us
  starting transfers between devices  104 us (37%)
  other arithmetic  56.5 us (20%)
  between operations  49 us (17%)
  local copies, waits for them, and re-layouts  31.3 us (11%)
  waiting for transfers between devices  24.1 us (9%)
  Pallas kernels  15 us (5%)
    ppermute x28, starting transfers between devices, axis_sum(): vals[o] = lax.ppermute(value, axis, [(i, i ^ mask) for i in range(size)])  45.2 us
    ppermute x7, starting transfers between devices, boundary_planes(): before = lax.ppermute(value[:, :, -1:], 'yb', up)  27.5 us
    add x9, other arithmetic, tree_sum(): v + cur[o | 1 << level]  17.6 us
    another operation x7, other arithmetic, shards(): local = jnp.stack(terms, -1)  17.5 us
    pallas_call x1, Pallas kernels, stiffness(): pl.pallas_call(stiffness_kernel, grid=(rves,), in_specs=[pl.BlockSpec(pie...  15 us
    another operation x1, local copies, waits for them, and re-layouts, shards(): local = jnp.stack(terms, -1)  14.5 us
    reduce_sum x8, other arithmetic, local_dot(): return jnp.sum(first * second, axis=(1, 2, 3))  12.7 us
    ppermute x28, waiting for transfers between devices, axis_sum(): vals[o] = lax.ppermute(value, axis, [(i, i ^ mask) for i in range(size)])  12.6 us
  transfers between devices with their start and end apart: 52, of which 9 were waited for; matrix products, arithmetic and copies ran while one was open for 13% of the time, Pallas kernels for 5%

profile of v1, /device:TPU:0, one launch (start us, length us, event | category | flops | bytes accessed | tf_op | source)
XLA Modules:
  0.0 280.0 jit_solution(2765129584340245238)
XLA Ops:
  0.7 4.1 %collective-permute-start.3 = (f32[4,6]{1,0:T(4,128)}, f32[4,6]{1,0:T(4,128)S(1)}, u32[]{:S(2)}, u32[]{:S(2)}) collective-permute-start(f32[4,6]{1,0:T(4,128)} %param.6), channel_id=1, source_target_pairs={{0,64},{32,96},{64,0},{96,32},{1,65},{33,97},{65,1},{97,33},{2,66}... | collective-permute-start | bytes 296 | tf_op jit(solution)/shard_map/ppermute | solution.py:68
  7.1 15.0 %shard_map.77 = f32[8,2,4096]{2,1,0:T(2,128)} custom-call(bf16[3,16,64]{2,1,0:T(8,128)(2,1)} %fusion.95.pieces_ref, s32[8,2,4096]{2,1,0:T(2,128)} %codes_ref.1, s32[8,2,4096]{2,1,0:T(2,128)} %grains_ref.1), custom_call_target="tpu_custom_call" | custom-call | tf_op jit(solution)/shard_map/pallas_call | solution.py:122
  22.0 4.3 %all-to-all-start = ((f32[8,2,4096]{2,1,0:T(2,128)}), f32[8,2,4096]{2,1,0:T(2,128)S(1)}, u32[]{:S(2)}, u32[]{:S(2)}) async-start(f32[8,2,4096]{2,1,0:T(2,128)} %shard_map.77), calls=%async_computation | async-start | bytes 524288 | tf_op jit(solution)/shard_map/all_to_all | solution.py:186
  31.1 2.8 all-to-all-done
  34.1 3.5 %collective-permute-start.1 = (f32[1,2,4096]{2,1,0:T(2,128)S(1)}, f32[1,2,4096]{2,1,0:T(2,128)S(1)}, u32[]{:S(2)}, u32[]{:S(2)}) collective-permute-start(f32[1,2,4096]{2,1,0:T(2,128)S(1)} %get-tuple-element.164), channel_id=1, source_target_pairs={{0,8},{8,16},{16,24},{1,9},{9,17},{17,25},{2,10},{10,18},{18,26},{... | collective-permute-start | bytes 98312 | tf_op jit(solution)/shard_map/ppermute | solution.py:24
  39.8 3.6 %collective-permute-done = f32[1,2,4096]{2,1,0:T(2,128)S(1)} collective-permute-done((f32[1,2,4096]{2,1,0:T(2,128)S(1)}, f32[1,2,4096]{2,1,0:T(2,128)S(1)}, u32[]{:S(2)}, u32[]{:S(2)}) %collective-permute-start) | collective-permute-done | bytes 32800 | tf_op jit(solution)/shard_map/ppermute | solution.py:25
  45.6 1.6 multiply_reduce_fusion.29
  47.2 2.0 pad_maximum_fusion.21
  49.2 2.9 %collective-permute-start.6 = (f32[1,4]{1,0:T(1,128)S(1)}, f32[1,4]{1,0:T(1,128)S(1)}, u32[]{:S(2)}, u32[]{:S(2)}) collective-permute-start(f32[1,4]{1,0:T(1,128)S(1)} %pad_maximum_fusion.21), channel_id=1, source_target_pairs={{0,16},{8,24},{16,0},{24,8},{1,17},{9,25},{17,1},{25,9},{2,18},{10... | collective-permute-start | bytes 56 | tf_op jit(solution)/shard_map/ppermute | solution.py:58
  52.1 1.3 collective-permute-start.7
  53.5 3.9 %collective-permute-start.8 = (f32[1,3,1,4096]{3,2,1,0:T(1,128)S(1)}, f32[1,3,1,4096]{3,2,1,0:T(1,128)S(1)}, u32[]{:S(2)}, u32[]{:S(2)}) collective-permute-start(f32[1,3,1,4096]{3,2,1,0:T(1,128)S(1)} %get-tuple-element.147), channel_id=1, source_target_pairs={{0,8},{8,16},{16,24},{1,9},{9,17},{17,25},{2,10},{10,18},{18,26},{... | collective-permute-start | bytes 147464 | tf_op jit(solution)/shard_map/ppermute | solution.py:247
  58.8 2.0 add_add_fusion.7
  66.5 1.6 multiply_reduce_fusion.27
  68.1 2.6 pad_maximum_fusion.22
  70.7 4.0 %collective-permute-start.11 = (f32[1,4]{1,0:T(1,128)S(1)}, f32[1,4]{1,0:T(1,128)S(1)}, u32[]{:S(2)}, u32[]{:S(2)}) collective-permute-start(f32[1,4]{1,0:T(1,128)S(1)} %pad_maximum_fusion.22), channel_id=1, source_target_pairs={{0,16},{8,24},{16,0},{24,8},{1,17},{9,25},{17,1},{25,9},{2,18},{10... | collective-permute-start | bytes 56 | tf_op jit(solution)/shard_map/ppermute | solution.py:58
  74.7 1.3 collective-permute-start.12
  76.1 3.9 %collective-permute-start.13 = (f32[1,3,1,4096]{3,2,1,0:T(1,128)S(1)}, f32[1,3,1,4096]{3,2,1,0:T(1,128)S(1)}, u32[]{:S(2)}, u32[]{:S(2)}) collective-permute-start(f32[1,3,1,4096]{3,2,1,0:T(1,128)S(1)} %get-tuple-element.141), channel_id=1, source_target_pairs={{0,8},{8,16},{16,24},{1,9},{9,17},{17,25},{2,10},{10,18},{18,26},{... | collective-permute-start | bytes 147464 | tf_op jit(solution)/shard_map/ppermute | solution.py:247
  80.0 1.3 collective-permute-start.14
  81.4 2.6 add_add_fusion.6
  89.5 1.6 multiply_reduce_fusion.23
  91.1 2.5 pad_maximum_fusion.23
  93.6 4.0 %collective-permute-start.16 = (f32[1,4]{1,0:T(1,128)S(1)}, f32[1,4]{1,0:T(1,128)S(1)}, u32[]{:S(2)}, u32[]{:S(2)}) collective-permute-start(f32[1,4]{1,0:T(1,128)S(1)} %pad_maximum_fusion.23), channel_id=1, source_target_pairs={{0,16},{8,24},{16,0},{24,8},{1,17},{9,25},{17,1},{25,9},{2,18},{10... | collective-permute-start | bytes 56 | tf_op jit(solution)/shard_map/ppermute | solution.py:58
  97.6 1.3 collective-permute-start.17
  99.0 3.9 %collective-permute-start.18 = (f32[1,3,1,4096]{3,2,1,0:T(1,128)S(1)}, f32[1,3,1,4096]{3,2,1,0:T(1,128)S(1)}, u32[]{:S(2)}, u32[]{:S(2)}) collective-permute-start(f32[1,3,1,4096]{3,2,1,0:T(1,128)S(1)} %get-tuple-element.135), channel_id=1, source_target_pairs={{0,8},{8,16},{16,24},{1,9},{9,17},{17,25},{2,10},{10,18},{18,26},{... | collective-permute-start | bytes 147464 | tf_op jit(solution)/shard_map/ppermute | solution.py:247
  104.3 2.5 add_add_fusion.5
  112.5 1.6 multiply_reduce_fusion.19
  114.1 2.7 pad_maximum_fusion.24
  116.7 4.0 %collective-permute-start.21 = (f32[1,4]{1,0:T(1,128)S(1)}, f32[1,4]{1,0:T(1,128)S(1)}, u32[]{:S(2)}, u32[]{:S(2)}) collective-permute-start(f32[1,4]{1,0:T(1,128)S(1)} %pad_maximum_fusion.24), channel_id=1, source_target_pairs={{0,16},{8,24},{16,0},{24,8},{1,17},{9,25},{17,1},{25,9},{2,18},{10... | collective-permute-start | bytes 56 | tf_op jit(solution)/shard_map/ppermute | solution.py:58
  120.7 1.3 collective-permute-start.22
  122.2 3.9 %collective-permute-start.23 = (f32[1,3,1,4096]{3,2,1,0:T(1,128)S(1)}, f32[1,3,1,4096]{3,2,1,0:T(1,128)S(1)}, u32[]{:S(2)}, u32[]{:S(2)}) collective-permute-start(f32[1,3,1,4096]{3,2,1,0:T(1,128)S(1)} %get-tuple-element.129), channel_id=1, source_target_pairs={{0,8},{8,16},{16,24},{1,9},{9,17},{17,25},{2,10},{10,18},{18,26},{... | collective-permute-start | bytes 147464 | tf_op jit(solution)/shard_map/ppermute | solution.py:247
  127.4 2.7 add_add_fusion.4
  135.5 1.6 multiply_reduce_fusion.15
  137.1 2.6 pad_maximum_fusion.25
  139.7 4.0 %collective-permute-start.26 = (f32[1,4]{1,0:T(1,128)S(1)}, f32[1,4]{1,0:T(1,128)S(1)}, u32[]{:S(2)}, u32[]{:S(2)}) collective-permute-start(f32[1,4]{1,0:T(1,128)S(1)} %pad_maximum_fusion.25), channel_id=1, source_target_pairs={{0,16},{8,24},{16,0},{24,8},{1,17},{9,25},{17,1},{25,9},{2,18},{10... | collective-permute-start | bytes 56 | tf_op jit(solution)/shard_map/ppermute | solution.py:58
  143.7 1.3 collective-permute-start.27
  145.1 3.9 %collective-permute-start.28 = (f32[1,3,1,4096]{3,2,1,0:T(1,128)S(1)}, f32[1,3,1,4096]{3,2,1,0:T(1,128)S(1)}, u32[]{:S(2)}, u32[]{:S(2)}) collective-permute-start(f32[1,3,1,4096]{3,2,1,0:T(1,128)S(1)} %get-tuple-element.123), channel_id=1, source_target_pairs={{0,8},{8,16},{16,24},{1,9},{9,17},{17,25},{2,10},{10,18},{18,26},{... | collective-permute-start | bytes 147464 | tf_op jit(solution)/shard_map/ppermute | solution.py:247
  150.4 2.6 add_add_fusion.3
  158.6 1.6 multiply_reduce_fusion.11
  160.2 2.6 pad_maximum_fusion.26
  162.8 4.0 %collective-permute-start.31 = (f32[1,4]{1,0:T(1,128)S(1)}, f32[1,4]{1,0:T(1,128)S(1)}, u32[]{:S(2)}, u32[]{:S(2)}) collective-permute-start(f32[1,4]{1,0:T(1,128)S(1)} %pad_maximum_fusion.26), channel_id=1, source_target_pairs={{0,16},{8,24},{16,0},{24,8},{1,17},{9,25},{17,1},{25,9},{2,18},{10... | collective-permute-start | bytes 56 | tf_op jit(solution)/shard_map/ppermute | solution.py:58
  166.8 1.3 collective-permute-start.32
  168.2 3.9 %collective-permute-start.33 = (f32[1,3,1,4096]{3,2,1,0:T(1,128)S(1)}, f32[1,3,1,4096]{3,2,1,0:T(1,128)S(1)}, u32[]{:S(2)}, u32[]{:S(2)}) collective-permute-start(f32[1,3,1,4096]{3,2,1,0:T(1,128)S(1)} %get-tuple-element.117), channel_id=1, source_target_pairs={{0,8},{8,16},{16,24},{1,9},{9,17},{17,25},{2,10},{10,18},{18,26},{... | collective-permute-start | bytes 147464 | tf_op jit(solution)/shard_map/ppermute | solution.py:247
  173.4 2.6 add_add_fusion.2
  181.3 1.6 multiply_reduce_fusion.7
  182.9 2.5 pad_maximum_fusion.27
  185.4 4.0 %collective-permute-start.36 = (f32[1,4]{1,0:T(1,128)S(1)}, f32[1,4]{1,0:T(1,128)S(1)}, u32[]{:S(2)}, u32[]{:S(2)}) collective-permute-start(f32[1,4]{1,0:T(1,128)S(1)} %pad_maximum_fusion.27), channel_id=1, source_target_pairs={{0,16},{8,24},{16,0},{24,8},{1,17},{9,25},{17,1},{25,9},{2,18},{10... | collective-permute-start | bytes 56 | tf_op jit(solution)/shard_map/ppermute | solution.py:58
  189.4 1.3 collective-permute-start.37
  190.8 3.9 %collective-permute-start.38 = (f32[1,3,1,4096]{3,2,1,0:T(1,128)S(1)}, f32[1,3,1,4096]{3,2,1,0:T(1,128)S(1)}, u32[]{:S(2)}, u32[]{:S(2)}) collective-permute-start(f32[1,3,1,4096]{3,2,1,0:T(1,128)S(1)} %get-tuple-element.115), channel_id=1, source_target_pairs={{0,8},{8,16},{16,24},{1,9},{9,17},{17,25},{2,10},{10,18},{18,26},{... | collective-permute-start | bytes 147464 | tf_op jit(solution)/shard_map/ppermute | solution.py:247
  196.1 2.5 add_add_fusion.1
  206.6 1.6 multiply_reduce_fusion
  208.2 14.5 %stack.277 = f32[1,23]{1,0:T(1,128)S(1)} concatenate(f32[1,1]{1,0:T(1,128)} %bitcast.88, f32[1,1]{1,0:T(1,128)} %bitcast.89, f32[1,1]{1,0:T(1,128)} %bitcast.90, f32[1,1]{1,0:T(1,128)} %bitcast.91, f32[1,1]{1,0:T(1,128)} %bitcast.93, f32[1,1]{1,0:T(1,128)} %bitcast.94, f32[1,1]{1,0:T(1,128)} %bitcast.95, f32[1,1]{1,0:T(1,128)} %bitcast.97, f32[1,1]{1,0:T(1,128)} %bitcast.98, ...), dimensions={1} | concatenate | bytes 184 | tf_op jit(solution)/shard_map/stack | solution.py:287
  222.7 2.6 collective-permute-start.42
  225.3 2.2 collective-permute-start.41
  227.5 2.8 %collective-permute-done.41 = f32[1,23]{1,0:T(1,128)S(1)} collective-permute-done((f32[1,23]{1,0:T(1,128)S(1)}, f32[1,23]{1,0:T(1,128)S(1)}, u32[]{:S(2)}, u32[]{:S(2)}) %collective-permute-start.41) | collective-permute-done | bytes 124 | tf_op jit(solution)/shard_map/ppermute | solution.py:58
  249.6 1.7 copy.49
  251.3 3.5 %all-to-all-start.1 = ((f32[1,3,16,4096]{3,0,1,2:T(1,128)}), f32[1,3,16,4096]{3,0,1,2:T(1,128)S(1)}, u32[]{:S(2)}, u32[]{:S(2)}) async-start(f32[1,3,16,4096]{3,0,1,2:T(1,128)} %copy.49), calls=%async_computation.1 | async-start | bytes 1572864 | tf_op jit(solution)/shard_map/all_to_all | solution.py:327
  254.9 3.2 %collective-permute-start.46 = (f32[8,6]{1,0:T(8,128)S(1)}, f32[8,6]{1,0:T(8,128)S(1)}, u32[]{:S(2)}, u32[]{:S(2)}) collective-permute-start(f32[8,6]{1,0:T(8,128)S(1)} %fusion.111), channel_id=1, source_target_pairs={{0,6},{1,7},{2,4},{3,5},{4,2},{5,3},{6,0},{7,1},{8,14},{9,15},{10,... | collective-permute-start | bytes 584 | tf_op jit(solution)/shard_map/ppermute | solution.py:58
  259.1 5.8 %collective-permute-done.46 = f32[8,6]{1,0:T(8,128)S(1)} collective-permute-done((f32[8,6]{1,0:T(8,128)S(1)}, f32[8,6]{1,0:T(8,128)S(1)}, u32[]{:S(2)}, u32[]{:S(2)}) %collective-permute-start.46) | collective-permute-done | bytes 224 | tf_op jit(solution)/shard_map/ppermute | solution.py:58
  264.8 3.2 %collective-permute-done.45 = f32[8,6]{1,0:T(8,128)S(1)} collective-permute-done((f32[8,6]{1,0:T(8,128)S(1)}, f32[8,6]{1,0:T(8,128)S(1)}, u32[]{:S(2)}, u32[]{:S(2)}) %collective-permute-start.45) | collective-permute-done | bytes 224 | tf_op jit(solution)/shard_map/ppermute | solution.py:58
  268.3 1.7 collective-permute-start.47
  270.1 2.5 collective-permute-start.49
  272.6 2.3 collective-permute-done.49
  274.9 2.8 %collective-permute-done.48 = f32[4,6]{0,1:T(8,128)S(1)} collective-permute-done((f32[4,6]{0,1:T(8,128)S(1)}, f32[4,6]{0,1:T(8,128)S(1)}, u32[]{:S(2)}, u32[]{:S(2)}) %collective-permute-start.48) | collective-permute-done | bytes 128 | tf_op jit(solution)/shard_map/ppermute | solution.py:83
  278.5 1.5 copy.55
  (157 shorter events, 34.7 us)
Async XLA Ops:
  0.6 25.8 %copy-start = (f32[4,6]{1,0:T(4,128)S(1)}, f32[4,6]{1,0:T(4,128)}, u32[]{:S(2)}) copy-start(f32[4,6]{1,0:T(4,128)} %param.6) | copy-start | bytes 292
  0.6 25.8 %copy-start.1 = (s32[8]{0:T(128)S(1)}, s32[8]{0:T(128)}, u32[]{:S(2)}) copy-start(s32[8]{0:T(128)} %param.11) | copy-start | bytes 100
  0.7 25.7 %collective-permute-start.3 = (f32[4,6]{1,0:T(4,128)}, f32[4,6]{1,0:T(4,128)S(1)}, u32[]{:S(2)}, u32[]{:S(2)}) collective-permute-start(f32[4,6]{1,0:T(4,128)} %param.6), channel_id=1, source_target_pairs={{0,64},{32,96},{64,0},{96,32},{1,65},{33,97},{65,1},{97,33},{2,66}... | collective-permute-start | bytes 296 | tf_op jit(solution)/shard_map/ppermute | solution.py:68
  4.7 21.7 %collective-permute-start.2 = (f32[4,6]{1,0:T(4,128)}, f32[4,6]{1,0:T(4,128)S(1)}, u32[]{:S(2)}, u32[]{:S(2)}) collective-permute-start(f32[4,6]{1,0:T(4,128)} %param.6), channel_id=1, source_target_pairs={{0,96},{32,64},{64,32},{96,0},{1,97},{33,65},{65,33},{97,1},{2,98}... | collective-permute-start | bytes 296 | tf_op jit(solution)/shard_map/ppermute | solution.py:68
  5.4 21.0 %collective-permute-start.4 = (f32[4,6]{1,0:T(4,128)}, f32[4,6]{1,0:T(4,128)S(1)}, u32[]{:S(2)}, u32[]{:S(2)}) collective-permute-start(f32[4,6]{1,0:T(4,128)} %param.6), channel_id=1, source_target_pairs={{0,32},{32,0},{64,96},{96,64},{1,33},{33,1},{65,97},{97,65},{2,34}... | collective-permute-start | bytes 296 | tf_op jit(solution)/shard_map/ppermute | solution.py:68
  22.0 11.8 %all-to-all-start = ((f32[8,2,4096]{2,1,0:T(2,128)}), f32[8,2,4096]{2,1,0:T(2,128)S(1)}, u32[]{:S(2)}, u32[]{:S(2)}) async-start(f32[8,2,4096]{2,1,0:T(2,128)} %shard_map.77), calls=%async_computation | async-start | bytes 524288 | tf_op jit(solution)/shard_map/all_to_all | solution.py:186
  34.1 5.7 %collective-permute-start.1 = (f32[1,2,4096]{2,1,0:T(2,128)S(1)}, f32[1,2,4096]{2,1,0:T(2,128)S(1)}, u32[]{:S(2)}, u32[]{:S(2)}) collective-permute-start(f32[1,2,4096]{2,1,0:T(2,128)S(1)} %get-tuple-element.164), channel_id=1, source_target_pairs={{0,8},{8,16},{16,24},{1,9},{9,17},{17,25},{2,10},{10,18},{18,26},{... | collective-permute-start | bytes 98312 | tf_op jit(solution)/shard_map/ppermute | solution.py:24
  37.6 5.8 %collective-permute-start = (f32[1,2,4096]{2,1,0:T(2,128)S(1)}, f32[1,2,4096]{2,1,0:T(2,128)S(1)}, u32[]{:S(2)}, u32[]{:S(2)}) collective-permute-start(f32[1,2,4096]{2,1,0:T(2,128)S(1)} %get-tuple-element.165), channel_id=1, source_target_pairs={{8,0},{16,8},{24,16},{9,1},{17,9},{25,17},{10,2},{18,10},{26,18},{... | collective-permute-start | bytes 98312 | tf_op jit(solution)/shard_map/ppermute | solution.py:25
  49.2 9.6 %collective-permute-start.6 = (f32[1,4]{1,0:T(1,128)S(1)}, f32[1,4]{1,0:T(1,128)S(1)}, u32[]{:S(2)}, u32[]{:S(2)}) collective-permute-start(f32[1,4]{1,0:T(1,128)S(1)} %pad_maximum_fusion.21), channel_id=1, source_target_pairs={{0,16},{8,24},{16,0},{24,8},{1,17},{9,25},{17,1},{25,9},{2,18},{10... | collective-permute-start | bytes 56 | tf_op jit(solution)/shard_map/ppermute | solution.py:58
  52.1 6.7 %collective-permute-start.7 = (f32[1,4]{1,0:T(1,128)S(1)}, f32[1,4]{1,0:T(1,128)S(1)}, u32[]{:S(2)}, u32[]{:S(2)}) collective-permute-start(f32[1,4]{1,0:T(1,128)S(1)} %pad_maximum_fusion.21), channel_id=1, source_target_pairs={{0,24},{8,16},{16,8},{24,0},{1,25},{9,17},{17,9},{25,1},{2,26},{10... | collective-permute-start | bytes 56 | tf_op jit(solution)/shard_map/ppermute | solution.py:58
  53.4 5.3 %collective-permute-start.5 = (f32[1,4]{1,0:T(1,128)S(1)}, f32[1,4]{1,0:T(1,128)S(1)}, u32[]{:S(2)}, u32[]{:S(2)}) collective-permute-start(f32[1,4]{1,0:T(1,128)S(1)} %pad_maximum_fusion.21), channel_id=1, source_target_pairs={{0,8},{8,0},{16,24},{24,16},{1,9},{9,1},{17,25},{25,17},{2,10},{10... | collective-permute-start | bytes 56 | tf_op jit(solution)/shard_map/ppermute | solution.py:58
  53.5 12.7 %collective-permute-start.8 = (f32[1,3,1,4096]{3,2,1,0:T(1,128)S(1)}, f32[1,3,1,4096]{3,2,1,0:T(1,128)S(1)}, u32[]{:S(2)}, u32[]{:S(2)}) collective-permute-start(f32[1,3,1,4096]{3,2,1,0:T(1,128)S(1)} %get-tuple-element.147), channel_id=1, source_target_pairs={{0,8},{8,16},{16,24},{1,9},{9,17},{17,25},{2,10},{10,18},{18,26},{... | collective-permute-start | bytes 147464 | tf_op jit(solution)/shard_map/ppermute | solution.py:247
  57.4 8.8 %collective-permute-start.9 = (f32[1,3,1,4096]{3,2,1,0:T(1,128)S(1)}, f32[1,3,1,4096]{3,2,1,0:T(1,128)S(1)}, u32[]{:S(2)}, u32[]{:S(2)}) collective-permute-start(f32[1,3,1,4096]{3,2,1,0:T(1,128)S(1)} %get-tuple-element.148), channel_id=1, source_target_pairs={{8,0},{16,8},{24,16},{9,1},{17,9},{25,17},{10,2},{18,10},{26,18},{... | collective-permute-start | bytes 147464 | tf_op jit(solution)/shard_map/ppermute | solution.py:248
  70.7 10.7 %collective-permute-start.11 = (f32[1,4]{1,0:T(1,128)S(1)}, f32[1,4]{1,0:T(1,128)S(1)}, u32[]{:S(2)}, u32[]{:S(2)}) collective-permute-start(f32[1,4]{1,0:T(1,128)S(1)} %pad_maximum_fusion.22), channel_id=1, source_target_pairs={{0,16},{8,24},{16,0},{24,8},{1,17},{9,25},{17,1},{25,9},{2,18},{10... | collective-permute-start | bytes 56 | tf_op jit(solution)/shard_map/ppermute | solution.py:58
  74.7 6.7 %collective-permute-start.12 = (f32[1,4]{1,0:T(1,128)S(1)}, f32[1,4]{1,0:T(1,128)S(1)}, u32[]{:S(2)}, u32[]{:S(2)}) collective-permute-start(f32[1,4]{1,0:T(1,128)S(1)} %pad_maximum_fusion.22), channel_id=1, source_target_pairs={{0,24},{8,16},{16,8},{24,0},{1,25},{9,17},{17,9},{25,1},{2,26},{10... | collective-permute-start | bytes 56 | tf_op jit(solution)/shard_map/ppermute | solution.py:58
  76.0 5.3 %collective-permute-start.10 = (f32[1,4]{1,0:T(1,128)S(1)}, f32[1,4]{1,0:T(1,128)S(1)}, u32[]{:S(2)}, u32[]{:S(2)}) collective-permute-start(f32[1,4]{1,0:T(1,128)S(1)} %pad_maximum_fusion.22), channel_id=1, source_target_pairs={{0,8},{8,0},{16,24},{24,16},{1,9},{9,1},{17,25},{25,17},{2,10},{10... | collective-permute-start | bytes 56 | tf_op jit(solution)/shard_map/ppermute | solution.py:58
  76.1 13.0 %collective-permute-start.13 = (f32[1,3,1,4096]{3,2,1,0:T(1,128)S(1)}, f32[1,3,1,4096]{3,2,1,0:T(1,128)S(1)}, u32[]{:S(2)}, u32[]{:S(2)}) collective-permute-start(f32[1,3,1,4096]{3,2,1,0:T(1,128)S(1)} %get-tuple-element.141), channel_id=1, source_target_pairs={{0,8},{8,16},{16,24},{1,9},{9,17},{17,25},{2,10},{10,18},{18,26},{... | collective-permute-start | bytes 147464 | tf_op jit(solution)/shard_map/ppermute | solution.py:247
  80.0 9.0 %collective-permute-start.14 = (f32[1,3,1,4096]{3,2,1,0:T(1,128)S(1)}, f32[1,3,1,4096]{3,2,1,0:T(1,128)S(1)}, u32[]{:S(2)}, u32[]{:S(2)}) collective-permute-start(f32[1,3,1,4096]{3,2,1,0:T(1,128)S(1)} %get-tuple-element.142), channel_id=1, source_target_pairs={{8,0},{16,8},{24,16},{9,1},{17,9},{25,17},{10,2},{18,10},{26,18},{... | collective-permute-start | bytes 147464 | tf_op jit(solution)/shard_map/ppermute | solution.py:248
  93.6 10.7 %collective-permute-start.16 = (f32[1,4]{1,0:T(1,128)S(1)}, f32[1,4]{1,0:T(1,128)S(1)}, u32[]{:S(2)}, u32[]{:S(2)}) collective-permute-start(f32[1,4]{1,0:T(1,128)S(1)} %pad_maximum_fusion.23), channel_id=1, source_target_pairs={{0,16},{8,24},{16,0},{24,8},{1,17},{9,25},{17,1},{25,9},{2,18},{10... | collective-permute-start | bytes 56 | tf_op jit(solution)/shard_map/ppermute | solution.py:58
  97.6 6.7 %collective-permute-start.17 = (f32[1,4]{1,0:T(1,128)S(1)}, f32[1,4]{1,0:T(1,128)S(1)}, u32[]{:S(2)}, u32[]{:S(2)}) collective-permute-start(f32[1,4]{1,0:T(1,128)S(1)} %pad_maximum_fusion.23), channel_id=1, source_target_pairs={{0,24},{8,16},{16,8},{24,0},{1,25},{9,17},{17,9},{25,1},{2,26},{10... | collective-permute-start | bytes 56 | tf_op jit(solution)/shard_map/ppermute | solution.py:58
  98.9 5.3 %collective-permute-start.15 = (f32[1,4]{1,0:T(1,128)S(1)}, f32[1,4]{1,0:T(1,128)S(1)}, u32[]{:S(2)}, u32[]{:S(2)}) collective-permute-start(f32[1,4]{1,0:T(1,128)S(1)} %pad_maximum_fusion.23), channel_id=1, source_target_pairs={{0,8},{8,0},{16,24},{24,16},{1,9},{9,1},{17,25},{25,17},{2,10},{10... | collective-permute-start | bytes 56 | tf_op jit(solution)/shard_map/ppermute | solution.py:58
  99.0 13.0 %collective-permute-start.18 = (f32[1,3,1,4096]{3,2,1,0:T(1,128)S(1)}, f32[1,3,1,4096]{3,2,1,0:T(1,128)S(1)}, u32[]{:S(2)}, u32[]{:S(2)}) collective-permute-start(f32[1,3,1,4096]{3,2,1,0:T(1,128)S(1)} %get-tuple-element.135), channel_id=1, source_target_pairs={{0,8},{8,16},{16,24},{1,9},{9,17},{17,25},{2,10},{10,18},{18,26},{... | collective-permute-start | bytes 147464 | tf_op jit(solution)/shard_map/ppermute | solution.py:247
  102.9 9.1 %collective-permute-start.19 = (f32[1,3,1,4096]{3,2,1,0:T(1,128)S(1)}, f32[1,3,1,4096]{3,2,1,0:T(1,128)S(1)}, u32[]{:S(2)}, u32[]{:S(2)}) collective-permute-start(f32[1,3,1,4096]{3,2,1,0:T(1,128)S(1)} %get-tuple-element.136), channel_id=1, source_target_pairs={{8,0},{16,8},{24,16},{9,1},{17,9},{25,17},{10,2},{18,10},{26,18},{... | collective-permute-start | bytes 147464 | tf_op jit(solution)/shard_map/ppermute | solution.py:248
  116.7 10.7 %collective-permute-start.21 = (f32[1,4]{1,0:T(1,128)S(1)}, f32[1,4]{1,0:T(1,128)S(1)}, u32[]{:S(2)}, u32[]{:S(2)}) collective-permute-start(f32[1,4]{1,0:T(1,128)S(1)} %pad_maximum_fusion.24), channel_id=1, source_target_pairs={{0,16},{8,24},{16,0},{24,8},{1,17},{9,25},{17,1},{25,9},{2,18},{10... | collective-permute-start | bytes 56 | tf_op jit(solution)/shard_map/ppermute | solution.py:58
  120.7 6.7 %collective-permute-start.22 = (f32[1,4]{1,0:T(1,128)S(1)}, f32[1,4]{1,0:T(1,128)S(1)}, u32[]{:S(2)}, u32[]{:S(2)}) collective-permute-start(f32[1,4]{1,0:T(1,128)S(1)} %pad_maximum_fusion.24), channel_id=1, source_target_pairs={{0,24},{8,16},{16,8},{24,0},{1,25},{9,17},{17,9},{25,1},{2,26},{10... | collective-permute-start | bytes 56 | tf_op jit(solution)/shard_map/ppermute | solution.py:58
  122.1 5.3 %collective-permute-start.20 = (f32[1,4]{1,0:T(1,128)S(1)}, f32[1,4]{1,0:T(1,128)S(1)}, u32[]{:S(2)}, u32[]{:S(2)}) collective-permute-start(f32[1,4]{1,0:T(1,128)S(1)} %pad_maximum_fusion.24), channel_id=1, source_target_pairs={{0,8},{8,0},{16,24},{24,16},{1,9},{9,1},{17,25},{25,17},{2,10},{10... | collective-permute-start | bytes 56 | tf_op jit(solution)/shard_map/ppermute | solution.py:58
  122.2 13.1 %collective-permute-start.23 = (f32[1,3,1,4096]{3,2,1,0:T(1,128)S(1)}, f32[1,3,1,4096]{3,2,1,0:T(1,128)S(1)}, u32[]{:S(2)}, u32[]{:S(2)}) collective-permute-start(f32[1,3,1,4096]{3,2,1,0:T(1,128)S(1)} %get-tuple-element.129), channel_id=1, source_target_pairs={{0,8},{8,16},{16,24},{1,9},{9,17},{17,25},{2,10},{10,18},{18,26},{... | collective-permute-start | bytes 147464 | tf_op jit(solution)/shard_map/ppermute | solution.py:247
  126.1 9.2 %collective-permute-start.24 = (f32[1,3,1,4096]{3,2,1,0:T(1,128)S(1)}, f32[1,3,1,4096]{3,2,1,0:T(1,128)S(1)}, u32[]{:S(2)}, u32[]{:S(2)}) collective-permute-start(f32[1,3,1,4096]{3,2,1,0:T(1,128)S(1)} %get-tuple-element.130), channel_id=1, source_target_pairs={{8,0},{16,8},{24,16},{9,1},{17,9},{25,17},{10,2},{18,10},{26,18},{... | collective-permute-start | bytes 147464 | tf_op jit(solution)/shard_map/ppermute | solution.py:248
  139.7 10.7 %collective-permute-start.26 = (f32[1,4]{1,0:T(1,128)S(1)}, f32[1,4]{1,0:T(1,128)S(1)}, u32[]{:S(2)}, u32[]{:S(2)}) collective-permute-start(f32[1,4]{1,0:T(1,128)S(1)} %pad_maximum_fusion.25), channel_id=1, source_target_pairs={{0,16},{8,24},{16,0},{24,8},{1,17},{9,25},{17,1},{25,9},{2,18},{10... | collective-permute-start | bytes 56 | tf_op jit(solution)/shard_map/ppermute | solution.py:58
  143.7 6.7 %collective-permute-start.27 = (f32[1,4]{1,0:T(1,128)S(1)}, f32[1,4]{1,0:T(1,128)S(1)}, u32[]{:S(2)}, u32[]{:S(2)}) collective-permute-start(f32[1,4]{1,0:T(1,128)S(1)} %pad_maximum_fusion.25), channel_id=1, source_target_pairs={{0,24},{8,16},{16,8},{24,0},{1,25},{9,17},{17,9},{25,1},{2,26},{10... | collective-permute-start | bytes 56 | tf_op jit(solution)/shard_map/ppermute | solution.py:58
  145.1 5.3 %collective-permute-start.25 = (f32[1,4]{1,0:T(1,128)S(1)}, f32[1,4]{1,0:T(1,128)S(1)}, u32[]{:S(2)}, u32[]{:S(2)}) collective-permute-start(f32[1,4]{1,0:T(1,128)S(1)} %pad_maximum_fusion.25), channel_id=1, source_target_pairs={{0,8},{8,0},{16,24},{24,16},{1,9},{9,1},{17,25},{25,17},{2,10},{10... | collective-permute-start | bytes 56 | tf_op jit(solution)/shard_map/ppermute | solution.py:58
  145.1 13.1 %collective-permute-start.28 = (f32[1,3,1,4096]{3,2,1,0:T(1,128)S(1)}, f32[1,3,1,4096]{3,2,1,0:T(1,128)S(1)}, u32[]{:S(2)}, u32[]{:S(2)}) collective-permute-start(f32[1,3,1,4096]{3,2,1,0:T(1,128)S(1)} %get-tuple-element.123), channel_id=1, source_target_pairs={{0,8},{8,16},{16,24},{1,9},{9,17},{17,25},{2,10},{10,18},{18,26},{... | collective-permute-start | bytes 147464 | tf_op jit(solution)/shard_map/ppermute | solution.py:247
  149.1 9.2 %collective-permute-start.29 = (f32[1,3,1,4096]{3,2,1,0:T(1,128)S(1)}, f32[1,3,1,4096]{3,2,1,0:T(1,128)S(1)}, u32[]{:S(2)}, u32[]{:S(2)}) collective-permute-start(f32[1,3,1,4096]{3,2,1,0:T(1,128)S(1)} %get-tuple-element.124), channel_id=1, source_target_pairs={{8,0},{16,8},{24,16},{9,1},{17,9},{25,17},{10,2},{18,10},{26,18},{... | collective-permute-start | bytes 147464 | tf_op jit(solution)/shard_map/ppermute | solution.py:248
  162.8 10.7 %collective-permute-start.31 = (f32[1,4]{1,0:T(1,128)S(1)}, f32[1,4]{1,0:T(1,128)S(1)}, u32[]{:S(2)}, u32[]{:S(2)}) collective-permute-start(f32[1,4]{1,0:T(1,128)S(1)} %pad_maximum_fusion.26), channel_id=1, source_target_pairs={{0,16},{8,24},{16,0},{24,8},{1,17},{9,25},{17,1},{25,9},{2,18},{10... | collective-permute-start | bytes 56 | tf_op jit(solution)/shard_map/ppermute | solution.py:58
  166.8 6.7 %collective-permute-start.32 = (f32[1,4]{1,0:T(1,128)S(1)}, f32[1,4]{1,0:T(1,128)S(1)}, u32[]{:S(2)}, u32[]{:S(2)}) collective-permute-start(f32[1,4]{1,0:T(1,128)S(1)} %pad_maximum_fusion.26), channel_id=1, source_target_pairs={{0,24},{8,16},{16,8},{24,0},{1,25},{9,17},{17,9},{25,1},{2,26},{10... | collective-permute-start | bytes 56 | tf_op jit(solution)/shard_map/ppermute | solution.py:58
  168.1 5.3 %collective-permute-start.30 = (f32[1,4]{1,0:T(1,128)S(1)}, f32[1,4]{1,0:T(1,128)S(1)}, u32[]{:S(2)}, u32[]{:S(2)}) collective-permute-start(f32[1,4]{1,0:T(1,128)S(1)} %pad_maximum_fusion.26), channel_id=1, source_target_pairs={{0,8},{8,0},{16,24},{24,16},{1,9},{9,1},{17,25},{25,17},{2,10},{10... | collective-permute-start | bytes 56 | tf_op jit(solution)/shard_map/ppermute | solution.py:58
  168.2 12.9 %collective-permute-start.33 = (f32[1,3,1,4096]{3,2,1,0:T(1,128)S(1)}, f32[1,3,1,4096]{3,2,1,0:T(1,128)S(1)}, u32[]{:S(2)}, u32[]{:S(2)}) collective-permute-start(f32[1,3,1,4096]{3,2,1,0:T(1,128)S(1)} %get-tuple-element.117), channel_id=1, source_target_pairs={{0,8},{8,16},{16,24},{1,9},{9,17},{17,25},{2,10},{10,18},{18,26},{... | collective-permute-start | bytes 147464 | tf_op jit(solution)/shard_map/ppermute | solution.py:247
  172.1 9.0 %collective-permute-start.34 = (f32[1,3,1,4096]{3,2,1,0:T(1,128)S(1)}, f32[1,3,1,4096]{3,2,1,0:T(1,128)S(1)}, u32[]{:S(2)}, u32[]{:S(2)}) collective-permute-start(f32[1,3,1,4096]{3,2,1,0:T(1,128)S(1)} %get-tuple-element.118), channel_id=1, source_target_pairs={{8,0},{16,8},{24,16},{9,1},{17,9},{25,17},{10,2},{18,10},{26,18},{... | collective-permute-start | bytes 147464 | tf_op jit(solution)/shard_map/ppermute | solution.py:248
  185.4 10.7 %collective-permute-start.36 = (f32[1,4]{1,0:T(1,128)S(1)}, f32[1,4]{1,0:T(1,128)S(1)}, u32[]{:S(2)}, u32[]{:S(2)}) collective-permute-start(f32[1,4]{1,0:T(1,128)S(1)} %pad_maximum_fusion.27), channel_id=1, source_target_pairs={{0,16},{8,24},{16,0},{24,8},{1,17},{9,25},{17,1},{25,9},{2,18},{10... | collective-permute-start | bytes 56 | tf_op jit(solution)/shard_map/ppermute | solution.py:58
  189.4 6.7 %collective-permute-start.37 = (f32[1,4]{1,0:T(1,128)S(1)}, f32[1,4]{1,0:T(1,128)S(1)}, u32[]{:S(2)}, u32[]{:S(2)}) collective-permute-start(f32[1,4]{1,0:T(1,128)S(1)} %pad_maximum_fusion.27), channel_id=1, source_target_pairs={{0,24},{8,16},{16,8},{24,0},{1,25},{9,17},{17,9},{25,1},{2,26},{10... | collective-permute-start | bytes 56 | tf_op jit(solution)/shard_map/ppermute | solution.py:58
  190.8 5.3 %collective-permute-start.35 = (f32[1,4]{1,0:T(1,128)S(1)}, f32[1,4]{1,0:T(1,128)S(1)}, u32[]{:S(2)}, u32[]{:S(2)}) collective-permute-start(f32[1,4]{1,0:T(1,128)S(1)} %pad_maximum_fusion.27), channel_id=1, source_target_pairs={{0,8},{8,0},{16,24},{24,16},{1,9},{9,1},{17,25},{25,17},{2,10},{10... | collective-permute-start | bytes 56 | tf_op jit(solution)/shard_map/ppermute | solution.py:58
  190.8 15.5 %collective-permute-start.38 = (f32[1,3,1,4096]{3,2,1,0:T(1,128)S(1)}, f32[1,3,1,4096]{3,2,1,0:T(1,128)S(1)}, u32[]{:S(2)}, u32[]{:S(2)}) collective-permute-start(f32[1,3,1,4096]{3,2,1,0:T(1,128)S(1)} %get-tuple-element.115), channel_id=1, source_target_pairs={{0,8},{8,16},{16,24},{1,9},{9,17},{17,25},{2,10},{10,18},{18,26},{... | collective-permute-start | bytes 147464 | tf_op jit(solution)/shard_map/ppermute | solution.py:247
  194.8 11.5 %collective-permute-start.39 = (f32[1,3,1,4096]{3,2,1,0:T(1,128)S(1)}, f32[1,3,1,4096]{3,2,1,0:T(1,128)S(1)}, u32[]{:S(2)}, u32[]{:S(2)}) collective-permute-start(f32[1,3,1,4096]{3,2,1,0:T(1,128)S(1)} %get-tuple-element.116), channel_id=1, source_target_pairs={{8,0},{16,8},{24,16},{9,1},{17,9},{25,17},{10,2},{18,10},{26,18},{... | collective-permute-start | bytes 147464 | tf_op jit(solution)/shard_map/ppermute | solution.py:248
  222.7 4.9 %collective-permute-start.42 = (f32[1,23]{1,0:T(1,128)S(1)}, f32[1,23]{1,0:T(1,128)S(1)}, u32[]{:S(2)}, u32[]{:S(2)}) collective-permute-start(f32[1,23]{1,0:T(1,128)S(1)} %stack.277), channel_id=1, source_target_pairs={{0,24},{8,16},{16,8},{24,0},{1,25},{9,17},{17,9},{25,1},{2,26},{10... | collective-permute-start | bytes 284 | tf_op jit(solution)/shard_map/ppermute | solution.py:58
  225.3 5.1 %collective-permute-start.41 = (f32[1,23]{1,0:T(1,128)S(1)}, f32[1,23]{1,0:T(1,128)S(1)}, u32[]{:S(2)}, u32[]{:S(2)}) collective-permute-start(f32[1,23]{1,0:T(1,128)S(1)} %stack.277), channel_id=1, source_target_pairs={{0,16},{8,24},{16,0},{24,8},{1,17},{9,25},{17,1},{25,9},{2,18},{10... | collective-permute-start | bytes 284 | tf_op jit(solution)/shard_map/ppermute | solution.py:58
  227.5 3.6 %collective-permute-start.40 = (f32[1,23]{1,0:T(1,128)S(1)}, f32[1,23]{1,0:T(1,128)S(1)}, u32[]{:S(2)}, u32[]{:S(2)}) collective-permute-start(f32[1,23]{1,0:T(1,128)S(1)} %stack.277), channel_id=1, source_target_pairs={{0,8},{8,0},{16,24},{24,16},{1,9},{9,1},{17,25},{25,17},{2,10},{10... | collective-permute-start | bytes 284 | tf_op jit(solution)/shard_map/ppermute | solution.py:58
  249.5 5.4 %collective-permute-start.43 = (f32[8,6]{1,0:T(8,128)S(1)}, f32[8,6]{1,0:T(8,128)S(1)}, u32[]{:S(2)}, u32[]{:S(2)}) collective-permute-start(f32[8,6]{1,0:T(8,128)S(1)} %broadcast_multiply_fusion), channel_id=1, source_target_pairs={{0,1},{1,0},{2,3},{3,2},{4,5},{5,4},{6,7},{7,6},{8,9},{9,8},{10,11... | collective-permute-start | bytes 584 | tf_op jit(solution)/shard_map/ppermute | solution.py:58
  251.3 27.2 %all-to-all-start.1 = ((f32[1,3,16,4096]{3,0,1,2:T(1,128)}), f32[1,3,16,4096]{3,0,1,2:T(1,128)S(1)}, u32[]{:S(2)}, u32[]{:S(2)}) async-start(f32[1,3,16,4096]{3,0,1,2:T(1,128)} %copy.49), calls=%async_computation.1 | async-start | bytes 1572864 | tf_op jit(solution)/shard_map/all_to_all | solution.py:327
  254.9 9.9 %collective-permute-start.46 = (f32[8,6]{1,0:T(8,128)S(1)}, f32[8,6]{1,0:T(8,128)S(1)}, u32[]{:S(2)}, u32[]{:S(2)}) collective-permute-start(f32[8,6]{1,0:T(8,128)S(1)} %fusion.111), channel_id=1, source_target_pairs={{0,6},{1,7},{2,4},{3,5},{4,2},{5,3},{6,0},{7,1},{8,14},{9,15},{10,... | collective-permute-start | bytes 584 | tf_op jit(solution)/shard_map/ppermute | solution.py:58
  258.1 9.9 %collective-permute-start.45 = (f32[8,6]{1,0:T(8,128)S(1)}, f32[8,6]{1,0:T(8,128)S(1)}, u32[]{:S(2)}, u32[]{:S(2)}) collective-permute-start(f32[8,6]{1,0:T(8,128)S(1)} %fusion.111), channel_id=1, source_target_pairs={{0,4},{1,5},{2,6},{3,7},{4,0},{5,1},{6,2},{7,3},{8,12},{9,13},{10,... | collective-permute-start | bytes 584 | tf_op jit(solution)/shard_map/ppermute | solution.py:58
  258.9 9.1 %collective-permute-start.44 = (f32[8,6]{1,0:T(8,128)S(1)}, f32[8,6]{1,0:T(8,128)S(1)}, u32[]{:S(2)}, u32[]{:S(2)}) collective-permute-start(f32[8,6]{1,0:T(8,128)S(1)} %fusion.111), channel_id=1, source_target_pairs={{0,2},{1,3},{2,0},{3,1},{4,6},{5,7},{6,4},{7,5},{8,10},{9,11},{10,... | collective-permute-start | bytes 584 | tf_op jit(solution)/shard_map/ppermute | solution.py:58
  268.3 4.3 %collective-permute-start.47 = (f32[4,6]{0,1:T(8,128)S(1)}, f32[4,6]{0,1:T(8,128)S(1)}, u32[]{:S(2)}, u32[]{:S(2)}) collective-permute-start(f32[4,6]{0,1:T(8,128)S(1)} %get-tuple-element.187), channel_id=1, source_target_pairs={{0,32},{32,0},{64,96},{96,64},{1,33},{33,1},{65,97},{97,65},{2,34}... | collective-permute-start | bytes 296 | tf_op jit(solution)/shard_map/ppermute | solution.py:83
  270.1 4.8 %collective-permute-start.49 = (f32[4,6]{0,1:T(8,128)S(1)}, f32[4,6]{0,1:T(8,128)S(1)}, u32[]{:S(2)}, u32[]{:S(2)}) collective-permute-start(f32[4,6]{0,1:T(8,128)S(1)} %get-tuple-element.188), channel_id=1, source_target_pairs={{0,96},{32,64},{64,32},{96,0},{1,97},{33,65},{65,33},{97,1},{2,98}... | collective-permute-start | bytes 296 | tf_op jit(solution)/shard_map/ppermute | solution.py:83
  272.6 5.1 %collective-permute-start.48 = (f32[4,6]{0,1:T(8,128)S(1)}, f32[4,6]{0,1:T(8,128)S(1)}, u32[]{:S(2)}, u32[]{:S(2)}) collective-permute-start(f32[4,6]{0,1:T(8,128)S(1)} %get-tuple-element.189), channel_id=1, source_target_pairs={{0,64},{32,96},{64,0},{96,32},{1,65},{33,97},{65,1},{97,33},{2,66}... | collective-permute-start | bytes 296 | tf_op jit(solution)/shard_map/ppermute | solution.py:83

commit v2 on v1

--- a/solution.py
+++ b/solution.py
@@ -298,22 +298,11 @@
         direction = residual + beta * direction
         direction_edges = residual_edges + beta * direction_edges
     volume = float(RES**3)
-    stiff_part = sums[:, 22] / volume
-    moment = [
-        [sums[:, 4 + 3 * comp + other] + alpha * sums[:, 13 + 3 * comp + other] for other in range(3)]
-        for comp in range(3)
-    ]
-    pairs = [(0, 0), (1, 1), (2, 2), (1, 2), (0, 2), (0, 1)]
-    rve_one = jnp.stack(
-        [
-            stiff_part * strains[:, slot]
-            - 0.5
-            * (moment[pairs[slot][0]][pairs[slot][1]] + moment[pairs[slot][1]][pairs[slot][0]])
-            / volume
-            for slot in range(6)
-        ],
-        1,
-    )
+    moments = sums[:, 4:13] + alpha[:, None] * sums[:, 13:22]
+    pair_sum = jnp.take(moments, jnp.array([0, 4, 8, 5, 2, 1]), axis=1) + jnp.take(
+        moments, jnp.array([0, 4, 8, 7, 6, 3]), axis=1
+    )
+    rve_one = sums[:, 22:23] / volume * strains - 0.5 * pair_sum / volume
     per_spot = float(rve_count * lax.axis_size("hot") // spot_count)
     placed = (jnp.arange(rve_count)[:, None] == mine).astype(jnp.float32) * rve_one
     rve_totals = axis_sum(placed, "xc")

time: 282 us -> 266 us (0.943)
  between operations: 49 us -> 33.8 us
  transfers between devices with their start and end apart: 52 -> 52, of which waited for: 9 -> 9; matrix products, arithmetic and copies ran while one was open for 13% -> 13% of each run, Pallas kernels for 5% -> 6%
where the time goes in v2:
time: 266 us; the launch traced here: 264 us
  starting transfers between devices  104 us (39%)
  other arithmetic  55.7 us (21%)
  between operations  33.8 us (13%)
  local copies, waits for them, and re-layouts  31.8 us (12%)
  waiting for transfers between devices  23.9 us (9%)
  Pallas kernels  15 us (6%)
    ppermute x28, starting transfers between devices, axis_sum(): vals[o] = lax.ppermute(value, axis, [(i, i ^ mask) for i in range(size)])  45.2 us
    ppermute x7, starting transfers between devices, boundary_planes(): before = lax.ppermute(value[:, :, -1:], 'yb', up)  27.5 us
    add x9, other arithmetic, tree_sum(): v + cur[o | 1 << level]  17.2 us
    another operation x7, other arithmetic, shards(): local = jnp.stack(terms, -1)  17.1 us
    pallas_call x1, Pallas kernels, stiffness(): pl.pallas_call(stiffness_kernel, grid=(rves,), in_specs=[pl.BlockSpec(pie...  15 us
    another operation x1, local copies, waits for them, and re-layouts, shards(): local = jnp.stack(terms, -1)  14.5 us
    ppermute x28, waiting for transfers between devices, axis_sum(): vals[o] = lax.ppermute(value, axis, [(i, i ^ mask) for i in range(size)])  12.6 us
    reduce_sum x8, other arithmetic, local_dot(): return jnp.sum(first * second, axis=(1, 2, 3))  12.4 us
  transfers between devices with their start and end apart: 52, of which 9 were waited for; matrix products, arithmetic and copies ran while one was open for 13% of the time, Pallas kernels for 6%

profile of v2, /device:TPU:0, one launch (start us, length us, event | category | flops | bytes accessed | tf_op | source)
XLA Modules:
  0.0 264.3 jit_solution(11108648897346912188)
XLA Ops:
  0.7 4.1 %collective-permute-start.3 = (f32[4,6]{1,0:T(4,128)}, f32[4,6]{1,0:T(4,128)S(1)}, u32[]{:S(2)}, u32[]{:S(2)}) collective-permute-start(f32[4,6]{1,0:T(4,128)} %param.10), channel_id=1, source_target_pairs={{0,64},{32,96},{64,0},{96,32},{1,65},{33,97},{65,1},{97,33},{2,66}... | collective-permute-start | bytes 296 | tf_op jit(solution)/shard_map/ppermute | solution.py:68
  7.1 15.0 %shard_map.95 = f32[8,2,4096]{2,1,0:T(2,128)} custom-call(bf16[3,16,64]{2,1,0:T(8,128)(2,1)} %fusion.95.pieces_ref, s32[8,2,4096]{2,1,0:T(2,128)} %codes_ref.1, s32[8,2,4096]{2,1,0:T(2,128)} %grains_ref.1), custom_call_target="tpu_custom_call" | custom-call | tf_op jit(solution)/shard_map/pallas_call | solution.py:122
  22.1 4.3 %all-to-all-start = ((f32[8,2,4096]{2,1,0:T(2,128)}), f32[8,2,4096]{2,1,0:T(2,128)S(1)}, u32[]{:S(2)}, u32[]{:S(2)}) async-start(f32[8,2,4096]{2,1,0:T(2,128)} %shard_map.95), calls=%async_computation | async-start | bytes 524288 | tf_op jit(solution)/shard_map/all_to_all | solution.py:186
  31.2 2.7 %all-to-all-done = f32[8,2,4096]{2,1,0:T(2,128)S(1)} async-done(((f32[8,2,4096]{2,1,0:T(2,128)}), f32[8,2,4096]{2,1,0:T(2,128)S(1)}, u32[]{:S(2)}, u32[]{:S(2)}) %all-to-all-start) | async-done | bytes 262176 | tf_op jit(solution)/shard_map/all_to_all | solution.py:186
  34.1 3.5 %collective-permute-start.1 = (f32[1,2,4096]{2,1,0:T(2,128)S(1)}, f32[1,2,4096]{2,1,0:T(2,128)S(1)}, u32[]{:S(2)}, u32[]{:S(2)}) collective-permute-start(f32[1,2,4096]{2,1,0:T(2,128)S(1)} %get-tuple-element.165), channel_id=1, source_target_pairs={{0,8},{8,16},{16,24},{1,9},{9,17},{17,25},{2,10},{10,18},{18,26},{... | collective-permute-start | bytes 98312 | tf_op jit(solution)/shard_map/ppermute | solution.py:24
  37.6 1.3 collective-permute-start
  39.9 3.5 %collective-permute-done = f32[1,2,4096]{2,1,0:T(2,128)S(1)} collective-permute-done((f32[1,2,4096]{2,1,0:T(2,128)S(1)}, f32[1,2,4096]{2,1,0:T(2,128)S(1)}, u32[]{:S(2)}, u32[]{:S(2)}) %collective-permute-start) | collective-permute-done | bytes 32800 | tf_op jit(solution)/shard_map/ppermute | solution.py:25
  45.6 1.5 multiply_reduce_fusion.29
  47.1 1.9 pad_maximum_fusion.21
  49.1 2.9 %collective-permute-start.6 = (f32[1,4]{1,0:T(1,128)S(1)}, f32[1,4]{1,0:T(1,128)S(1)}, u32[]{:S(2)}, u32[]{:S(2)}) collective-permute-start(f32[1,4]{1,0:T(1,128)S(1)} %pad_maximum_fusion.21), channel_id=1, source_target_pairs={{0,16},{8,24},{16,0},{24,8},{1,17},{9,25},{17,1},{25,9},{2,18},{10... | collective-permute-start | bytes 56 | tf_op jit(solution)/shard_map/ppermute | solution.py:58
  52.0 1.3 collective-permute-start.7
  53.4 3.9 %collective-permute-start.8 = (f32[1,3,1,4096]{3,2,1,0:T(1,128)S(1)}, f32[1,3,1,4096]{3,2,1,0:T(1,128)S(1)}, u32[]{:S(2)}, u32[]{:S(2)}) collective-permute-start(f32[1,3,1,4096]{3,2,1,0:T(1,128)S(1)} %get-tuple-element.148), channel_id=1, source_target_pairs={{0,8},{8,16},{16,24},{1,9},{9,17},{17,25},{2,10},{10,18},{18,26},{... | collective-permute-start | bytes 147464 | tf_op jit(solution)/shard_map/ppermute | solution.py:247
  58.7 1.9 add_add_fusion.7
  66.2 1.6 multiply_reduce_fusion.27
  67.8 2.6 pad_maximum_fusion.22
  70.4 4.0 %collective-permute-start.11 = (f32[1,4]{1,0:T(1,128)S(1)}, f32[1,4]{1,0:T(1,128)S(1)}, u32[]{:S(2)}, u32[]{:S(2)}) collective-permute-start(f32[1,4]{1,0:T(1,128)S(1)} %pad_maximum_fusion.22), channel_id=1, source_target_pairs={{0,16},{8,24},{16,0},{24,8},{1,17},{9,25},{17,1},{25,9},{2,18},{10... | collective-permute-start | bytes 56 | tf_op jit(solution)/shard_map/ppermute | solution.py:58
  74.4 1.3 collective-permute-start.12
  75.8 3.9 %collective-permute-start.13 = (f32[1,3,1,4096]{3,2,1,0:T(1,128)S(1)}, f32[1,3,1,4096]{3,2,1,0:T(1,128)S(1)}, u32[]{:S(2)}, u32[]{:S(2)}) collective-permute-start(f32[1,3,1,4096]{3,2,1,0:T(1,128)S(1)} %get-tuple-element.142), channel_id=1, source_target_pairs={{0,8},{8,16},{16,24},{1,9},{9,17},{17,25},{2,10},{10,18},{18,26},{... | collective-permute-start | bytes 147464 | tf_op jit(solution)/shard_map/ppermute | solution.py:247
  81.1 2.6 add_add_fusion.6
  89.2 1.6 multiply_reduce_fusion.23
  90.8 2.5 pad_maximum_fusion.23
  93.3 4.0 %collective-permute-start.16 = (f32[1,4]{1,0:T(1,128)S(1)}, f32[1,4]{1,0:T(1,128)S(1)}, u32[]{:S(2)}, u32[]{:S(2)}) collective-permute-start(f32[1,4]{1,0:T(1,128)S(1)} %pad_maximum_fusion.23), channel_id=1, source_target_pairs={{0,16},{8,24},{16,0},{24,8},{1,17},{9,25},{17,1},{25,9},{2,18},{10... | collective-permute-start | bytes 56 | tf_op jit(solution)/shard_map/ppermute | solution.py:58
  97.3 1.3 collective-permute-start.17
  98.7 3.9 %collective-permute-start.18 = (f32[1,3,1,4096]{3,2,1,0:T(1,128)S(1)}, f32[1,3,1,4096]{3,2,1,0:T(1,128)S(1)}, u32[]{:S(2)}, u32[]{:S(2)}) collective-permute-start(f32[1,3,1,4096]{3,2,1,0:T(1,128)S(1)} %get-tuple-element.136), channel_id=1, source_target_pairs={{0,8},{8,16},{16,24},{1,9},{9,17},{17,25},{2,10},{10,18},{18,26},{... | collective-permute-start | bytes 147464 | tf_op jit(solution)/shard_map/ppermute | solution.py:247
  104.0 2.5 add_add_fusion.5
  112.2 1.5 multiply_reduce_fusion.19
  113.7 2.6 pad_maximum_fusion.24
  116.3 4.0 %collective-permute-start.21 = (f32[1,4]{1,0:T(1,128)S(1)}, f32[1,4]{1,0:T(1,128)S(1)}, u32[]{:S(2)}, u32[]{:S(2)}) collective-permute-start(f32[1,4]{1,0:T(1,128)S(1)} %pad_maximum_fusion.24), channel_id=1, source_target_pairs={{0,16},{8,24},{16,0},{24,8},{1,17},{9,25},{17,1},{25,9},{2,18},{10... | collective-permute-start | bytes 56 | tf_op jit(solution)/shard_map/ppermute | solution.py:58
  120.3 1.3 collective-permute-start.22
  121.7 3.9 %collective-permute-start.23 = (f32[1,3,1,4096]{3,2,1,0:T(1,128)S(1)}, f32[1,3,1,4096]{3,2,1,0:T(1,128)S(1)}, u32[]{:S(2)}, u32[]{:S(2)}) collective-permute-start(f32[1,3,1,4096]{3,2,1,0:T(1,128)S(1)} %get-tuple-element.130), channel_id=1, source_target_pairs={{0,8},{8,16},{16,24},{1,9},{9,17},{17,25},{2,10},{10,18},{18,26},{... | collective-permute-start | bytes 147464 | tf_op jit(solution)/shard_map/ppermute | solution.py:247
  127.0 2.6 add_add_fusion.4
  134.8 1.5 multiply_reduce_fusion.15
  136.3 2.5 pad_maximum_fusion.25
  138.9 4.0 %collective-permute-start.26 = (f32[1,4]{1,0:T(1,128)S(1)}, f32[1,4]{1,0:T(1,128)S(1)}, u32[]{:S(2)}, u32[]{:S(2)}) collective-permute-start(f32[1,4]{1,0:T(1,128)S(1)} %pad_maximum_fusion.25), channel_id=1, source_target_pairs={{0,16},{8,24},{16,0},{24,8},{1,17},{9,25},{17,1},{25,9},{2,18},{10... | collective-permute-start | bytes 56 | tf_op jit(solution)/shard_map/ppermute | solution.py:58
  142.9 1.3 collective-permute-start.27
  144.3 3.9 %collective-permute-start.28 = (f32[1,3,1,4096]{3,2,1,0:T(1,128)S(1)}, f32[1,3,1,4096]{3,2,1,0:T(1,128)S(1)}, u32[]{:S(2)}, u32[]{:S(2)}) collective-permute-start(f32[1,3,1,4096]{3,2,1,0:T(1,128)S(1)} %get-tuple-element.124), channel_id=1, source_target_pairs={{0,8},{8,16},{16,24},{1,9},{9,17},{17,25},{2,10},{10,18},{18,26},{... | collective-permute-start | bytes 147464 | tf_op jit(solution)/shard_map/ppermute | solution.py:247
  149.6 2.5 add_add_fusion.3
  157.4 1.5 multiply_reduce_fusion.11
  159.0 2.5 pad_maximum_fusion.26
  161.5 4.0 %collective-permute-start.31 = (f32[1,4]{1,0:T(1,128)S(1)}, f32[1,4]{1,0:T(1,128)S(1)}, u32[]{:S(2)}, u32[]{:S(2)}) collective-permute-start(f32[1,4]{1,0:T(1,128)S(1)} %pad_maximum_fusion.26), channel_id=1, source_target_pairs={{0,16},{8,24},{16,0},{24,8},{1,17},{9,25},{17,1},{25,9},{2,18},{10... | collective-permute-start | bytes 56 | tf_op jit(solution)/shard_map/ppermute | solution.py:58
  165.5 1.3 collective-permute-start.32
  166.9 3.9 %collective-permute-start.33 = (f32[1,3,1,4096]{3,2,1,0:T(1,128)S(1)}, f32[1,3,1,4096]{3,2,1,0:T(1,128)S(1)}, u32[]{:S(2)}, u32[]{:S(2)}) collective-permute-start(f32[1,3,1,4096]{3,2,1,0:T(1,128)S(1)} %get-tuple-element.118), channel_id=1, source_target_pairs={{0,8},{8,16},{16,24},{1,9},{9,17},{17,25},{2,10},{10,18},{18,26},{... | collective-permute-start | bytes 147464 | tf_op jit(solution)/shard_map/ppermute | solution.py:247
  172.2 2.5 add_add_fusion.2
  179.9 1.5 multiply_reduce_fusion.7
  181.4 2.5 pad_maximum_fusion.27
  183.9 4.0 %collective-permute-start.36 = (f32[1,4]{1,0:T(1,128)S(1)}, f32[1,4]{1,0:T(1,128)S(1)}, u32[]{:S(2)}, u32[]{:S(2)}) collective-permute-start(f32[1,4]{1,0:T(1,128)S(1)} %pad_maximum_fusion.27), channel_id=1, source_target_pairs={{0,16},{8,24},{16,0},{24,8},{1,17},{9,25},{17,1},{25,9},{2,18},{10... | collective-permute-start | bytes 56 | tf_op jit(solution)/shard_map/ppermute | solution.py:58
  187.9 1.3 collective-permute-start.37
  189.3 3.9 %collective-permute-start.38 = (f32[1,3,1,4096]{3,2,1,0:T(1,128)S(1)}, f32[1,3,1,4096]{3,2,1,0:T(1,128)S(1)}, u32[]{:S(2)}, u32[]{:S(2)}) collective-permute-start(f32[1,3,1,4096]{3,2,1,0:T(1,128)S(1)} %get-tuple-element.116), channel_id=1, source_target_pairs={{0,8},{8,16},{16,24},{1,9},{9,17},{17,25},{2,10},{10,18},{18,26},{... | collective-permute-start | bytes 147464 | tf_op jit(solution)/shard_map/ppermute | solution.py:247
  194.5 2.5 add_add_fusion.1
  205.2 1.6 multiply_reduce_fusion
  206.8 14.5 %stack.256 = f32[1,23]{1,0:T(1,128)S(1)} concatenate(f32[1,1]{1,0:T(1,128)} %bitcast.88, f32[1,1]{1,0:T(1,128)} %bitcast.89, f32[1,1]{1,0:T(1,128)} %bitcast.90, f32[1,1]{1,0:T(1,128)} %bitcast.91, f32[1,1]{1,0:T(1,128)} %bitcast.93, f32[1,1]{1,0:T(1,128)} %bitcast.94, f32[1,1]{1,0:T(1,128)} %bitcast.95, f32[1,1]{1,0:T(1,128)} %bitcast.97, f32[1,1]{1,0:T(1,128)} %bitcast.98, ...), dimensions={1} | concatenate | bytes 184 | tf_op jit(solution)/shard_map/stack | solution.py:287
  221.3 2.6 collective-permute-start.42
  223.9 2.2 collective-permute-start.41
  226.1 2.8 %collective-permute-done.41 = f32[1,23]{1,0:T(1,128)S(1)} collective-permute-done((f32[1,23]{1,0:T(1,128)S(1)}, f32[1,23]{1,0:T(1,128)S(1)}, u32[]{:S(2)}, u32[]{:S(2)}) %collective-permute-start.41) | collective-permute-done | bytes 124 | tf_op jit(solution)/shard_map/ppermute | solution.py:58
  233.9 1.7 copy.51
  235.6 3.5 %all-to-all-start.1 = ((f32[1,3,16,4096]{3,0,1,2:T(1,128)}), f32[1,3,16,4096]{3,0,1,2:T(1,128)S(1)}, u32[]{:S(2)}, u32[]{:S(2)}) async-start(f32[1,3,16,4096]{3,0,1,2:T(1,128)} %copy.51), calls=%async_computation.1 | async-start | bytes 1572864 | tf_op jit(solution)/shard_map/all_to_all | solution.py:316
  239.3 3.2 %collective-permute-start.46 = (f32[8,6]{1,0:T(8,128)S(1)}, f32[8,6]{1,0:T(8,128)S(1)}, u32[]{:S(2)}, u32[]{:S(2)}) collective-permute-start(f32[8,6]{1,0:T(8,128)S(1)} %fusion.111), channel_id=1, source_target_pairs={{0,6},{1,7},{2,4},{3,5},{4,2},{5,3},{6,0},{7,1},{8,14},{9,15},{10,... | collective-permute-start | bytes 584 | tf_op jit(solution)/shard_map/ppermute | solution.py:58
  243.4 5.8 %collective-permute-done.46 = f32[8,6]{1,0:T(8,128)S(1)} collective-permute-done((f32[8,6]{1,0:T(8,128)S(1)}, f32[8,6]{1,0:T(8,128)S(1)}, u32[]{:S(2)}, u32[]{:S(2)}) %collective-permute-start.46) | collective-permute-done | bytes 224 | tf_op jit(solution)/shard_map/ppermute | solution.py:58
  249.2 3.2 %collective-permute-done.45 = f32[8,6]{1,0:T(8,128)S(1)} collective-permute-done((f32[8,6]{1,0:T(8,128)S(1)}, f32[8,6]{1,0:T(8,128)S(1)}, u32[]{:S(2)}, u32[]{:S(2)}) %collective-permute-start.45) | collective-permute-done | bytes 224 | tf_op jit(solution)/shard_map/ppermute | solution.py:58
  252.6 1.7 collective-permute-start.47
  254.4 2.5 collective-permute-start.49
  256.9 2.3 collective-permute-done.49
  259.2 2.8 %collective-permute-done.48 = f32[4,6]{0,1:T(8,128)S(1)} collective-permute-done((f32[4,6]{0,1:T(8,128)S(1)}, f32[4,6]{0,1:T(8,128)S(1)}, u32[]{:S(2)}, u32[]{:S(2)}) %collective-permute-start.48) | collective-permute-done | bytes 128 | tf_op jit(solution)/shard_map/ppermute | solution.py:83
  262.8 1.5 copy.57
  (164 shorter events, 35.4 us)
Async XLA Ops:
  0.6 25.8 %copy-start.1 = (s32[6]{0:T(128)S(1)}, s32[6]{0:T(128)}, u32[]{:S(2)}) copy-start(s32[6]{0:T(128)} %constant.189) | copy-start | bytes 76
  0.6 25.8 %copy-start.2 = (s32[6]{0:T(128)S(1)}, s32[6]{0:T(128)}, u32[]{:S(2)}) copy-start(s32[6]{0:T(128)} %constant.188) | copy-start | bytes 76
  0.7 25.8 %copy-start = (f32[4,6]{1,0:T(4,128)S(1)}, f32[4,6]{1,0:T(4,128)}, u32[]{:S(2)}) copy-start(f32[4,6]{1,0:T(4,128)} %param.10) | copy-start | bytes 292
  0.7 25.8 %copy-start.3 = (s32[8]{0:T(128)S(1)}, s32[8]{0:T(128)}, u32[]{:S(2)}) copy-start(s32[8]{0:T(128)} %param.15) | copy-start | bytes 100
  0.7 25.8 %collective-permute-start.3 = (f32[4,6]{1,0:T(4,128)}, f32[4,6]{1,0:T(4,128)S(1)}, u32[]{:S(2)}, u32[]{:S(2)}) collective-permute-start(f32[4,6]{1,0:T(4,128)} %param.10), channel_id=1, source_target_pairs={{0,64},{32,96},{64,0},{96,32},{1,65},{33,97},{65,1},{97,33},{2,66}... | collective-permute-start | bytes 296 | tf_op jit(solution)/shard_map/ppermute | solution.py:68
  4.7 21.7 %collective-permute-start.2 = (f32[4,6]{1,0:T(4,128)}, f32[4,6]{1,0:T(4,128)S(1)}, u32[]{:S(2)}, u32[]{:S(2)}) collective-permute-start(f32[4,6]{1,0:T(4,128)} %param.10), channel_id=1, source_target_pairs={{0,96},{32,64},{64,32},{96,0},{1,97},{33,65},{65,33},{97,1},{2,98}... | collective-permute-start | bytes 296 | tf_op jit(solution)/shard_map/ppermute | solution.py:68
  5.5 21.0 %collective-permute-start.4 = (f32[4,6]{1,0:T(4,128)}, f32[4,6]{1,0:T(4,128)S(1)}, u32[]{:S(2)}, u32[]{:S(2)}) collective-permute-start(f32[4,6]{1,0:T(4,128)} %param.10), channel_id=1, source_target_pairs={{0,32},{32,0},{64,96},{96,64},{1,33},{33,1},{65,97},{97,65},{2,34}... | collective-permute-start | bytes 296 | tf_op jit(solution)/shard_map/ppermute | solution.py:68
  22.1 11.8 %all-to-all-start = ((f32[8,2,4096]{2,1,0:T(2,128)}), f32[8,2,4096]{2,1,0:T(2,128)S(1)}, u32[]{:S(2)}, u32[]{:S(2)}) async-start(f32[8,2,4096]{2,1,0:T(2,128)} %shard_map.95), calls=%async_computation | async-start | bytes 524288 | tf_op jit(solution)/shard_map/all_to_all | solution.py:186
  34.1 5.8 %collective-permute-start.1 = (f32[1,2,4096]{2,1,0:T(2,128)S(1)}, f32[1,2,4096]{2,1,0:T(2,128)S(1)}, u32[]{:S(2)}, u32[]{:S(2)}) collective-permute-start(f32[1,2,4096]{2,1,0:T(2,128)S(1)} %get-tuple-element.165), channel_id=1, source_target_pairs={{0,8},{8,16},{16,24},{1,9},{9,17},{17,25},{2,10},{10,18},{18,26},{... | collective-permute-start | bytes 98312 | tf_op jit(solution)/shard_map/ppermute | solution.py:24
  37.6 5.8 %collective-permute-start = (f32[1,2,4096]{2,1,0:T(2,128)S(1)}, f32[1,2,4096]{2,1,0:T(2,128)S(1)}, u32[]{:S(2)}, u32[]{:S(2)}) collective-permute-start(f32[1,2,4096]{2,1,0:T(2,128)S(1)} %get-tuple-element.166), channel_id=1, source_target_pairs={{8,0},{16,8},{24,16},{9,1},{17,9},{25,17},{10,2},{18,10},{26,18},{... | collective-permute-start | bytes 98312 | tf_op jit(solution)/shard_map/ppermute | solution.py:25
  49.1 9.6 %collective-permute-start.6 = (f32[1,4]{1,0:T(1,128)S(1)}, f32[1,4]{1,0:T(1,128)S(1)}, u32[]{:S(2)}, u32[]{:S(2)}) collective-permute-start(f32[1,4]{1,0:T(1,128)S(1)} %pad_maximum_fusion.21), channel_id=1, source_target_pairs={{0,16},{8,24},{16,0},{24,8},{1,17},{9,25},{17,1},{25,9},{2,18},{10... | collective-permute-start | bytes 56 | tf_op jit(solution)/shard_map/ppermute | solution.py:58
  52.0 6.7 %collective-permute-start.7 = (f32[1,4]{1,0:T(1,128)S(1)}, f32[1,4]{1,0:T(1,128)S(1)}, u32[]{:S(2)}, u32[]{:S(2)}) collective-permute-start(f32[1,4]{1,0:T(1,128)S(1)} %pad_maximum_fusion.21), channel_id=1, source_target_pairs={{0,24},{8,16},{16,8},{24,0},{1,25},{9,17},{17,9},{25,1},{2,26},{10... | collective-permute-start | bytes 56 | tf_op jit(solution)/shard_map/ppermute | solution.py:58
  53.3 5.3 %collective-permute-start.5 = (f32[1,4]{1,0:T(1,128)S(1)}, f32[1,4]{1,0:T(1,128)S(1)}, u32[]{:S(2)}, u32[]{:S(2)}) collective-permute-start(f32[1,4]{1,0:T(1,128)S(1)} %pad_maximum_fusion.21), channel_id=1, source_target_pairs={{0,8},{8,0},{16,24},{24,16},{1,9},{9,1},{17,25},{25,17},{2,10},{10... | collective-permute-start | bytes 56 | tf_op jit(solution)/shard_map/ppermute | solution.py:58
  53.4 12.5 %collective-permute-start.8 = (f32[1,3,1,4096]{3,2,1,0:T(1,128)S(1)}, f32[1,3,1,4096]{3,2,1,0:T(1,128)S(1)}, u32[]{:S(2)}, u32[]{:S(2)}) collective-permute-start(f32[1,3,1,4096]{3,2,1,0:T(1,128)S(1)} %get-tuple-element.148), channel_id=1, source_target_pairs={{0,8},{8,16},{16,24},{1,9},{9,17},{17,25},{2,10},{10,18},{18,26},{... | collective-permute-start | bytes 147464 | tf_op jit(solution)/shard_map/ppermute | solution.py:247
  57.3 8.6 %collective-permute-start.9 = (f32[1,3,1,4096]{3,2,1,0:T(1,128)S(1)}, f32[1,3,1,4096]{3,2,1,0:T(1,128)S(1)}, u32[]{:S(2)}, u32[]{:S(2)}) collective-permute-start(f32[1,3,1,4096]{3,2,1,0:T(1,128)S(1)} %get-tuple-element.149), channel_id=1, source_target_pairs={{8,0},{16,8},{24,16},{9,1},{17,9},{25,17},{10,2},{18,10},{26,18},{... | collective-permute-start | bytes 147464 | tf_op jit(solution)/shard_map/ppermute | solution.py:248
  70.4 10.7 %collective-permute-start.11 = (f32[1,4]{1,0:T(1,128)S(1)}, f32[1,4]{1,0:T(1,128)S(1)}, u32[]{:S(2)}, u32[]{:S(2)}) collective-permute-start(f32[1,4]{1,0:T(1,128)S(1)} %pad_maximum_fusion.22), channel_id=1, source_target_pairs={{0,16},{8,24},{16,0},{24,8},{1,17},{9,25},{17,1},{25,9},{2,18},{10... | collective-permute-start | bytes 56 | tf_op jit(solution)/shard_map/ppermute | solution.py:58
  74.4 6.7 %collective-permute-start.12 = (f32[1,4]{1,0:T(1,128)S(1)}, f32[1,4]{1,0:T(1,128)S(1)}, u32[]{:S(2)}, u32[]{:S(2)}) collective-permute-start(f32[1,4]{1,0:T(1,128)S(1)} %pad_maximum_fusion.22), channel_id=1, source_target_pairs={{0,24},{8,16},{16,8},{24,0},{1,25},{9,17},{17,9},{25,1},{2,26},{10... | collective-permute-start | bytes 56 | tf_op jit(solution)/shard_map/ppermute | solution.py:58
  75.7 5.3 %collective-permute-start.10 = (f32[1,4]{1,0:T(1,128)S(1)}, f32[1,4]{1,0:T(1,128)S(1)}, u32[]{:S(2)}, u32[]{:S(2)}) collective-permute-start(f32[1,4]{1,0:T(1,128)S(1)} %pad_maximum_fusion.22), channel_id=1, source_target_pairs={{0,8},{8,0},{16,24},{24,16},{1,9},{9,1},{17,25},{25,17},{2,10},{10... | collective-permute-start | bytes 56 | tf_op jit(solution)/shard_map/ppermute | solution.py:58
  75.8 13.0 %collective-permute-start.13 = (f32[1,3,1,4096]{3,2,1,0:T(1,128)S(1)}, f32[1,3,1,4096]{3,2,1,0:T(1,128)S(1)}, u32[]{:S(2)}, u32[]{:S(2)}) collective-permute-start(f32[1,3,1,4096]{3,2,1,0:T(1,128)S(1)} %get-tuple-element.142), channel_id=1, source_target_pairs={{0,8},{8,16},{16,24},{1,9},{9,17},{17,25},{2,10},{10,18},{18,26},{... | collective-permute-start | bytes 147464 | tf_op jit(solution)/shard_map/ppermute | solution.py:247
  79.7 9.1 %collective-permute-start.14 = (f32[1,3,1,4096]{3,2,1,0:T(1,128)S(1)}, f32[1,3,1,4096]{3,2,1,0:T(1,128)S(1)}, u32[]{:S(2)}, u32[]{:S(2)}) collective-permute-start(f32[1,3,1,4096]{3,2,1,0:T(1,128)S(1)} %get-tuple-element.143), channel_id=1, source_target_pairs={{8,0},{16,8},{24,16},{9,1},{17,9},{25,17},{10,2},{18,10},{26,18},{... | collective-permute-start | bytes 147464 | tf_op jit(solution)/shard_map/ppermute | solution.py:248
  93.3 10.7 %collective-permute-start.16 = (f32[1,4]{1,0:T(1,128)S(1)}, f32[1,4]{1,0:T(1,128)S(1)}, u32[]{:S(2)}, u32[]{:S(2)}) collective-permute-start(f32[1,4]{1,0:T(1,128)S(1)} %pad_maximum_fusion.23), channel_id=1, source_target_pairs={{0,16},{8,24},{16,0},{24,8},{1,17},{9,25},{17,1},{25,9},{2,18},{10... | collective-permute-start | bytes 56 | tf_op jit(solution)/shard_map/ppermute | solution.py:58
  97.3 6.7 %collective-permute-start.17 = (f32[1,4]{1,0:T(1,128)S(1)}, f32[1,4]{1,0:T(1,128)S(1)}, u32[]{:S(2)}, u32[]{:S(2)}) collective-permute-start(f32[1,4]{1,0:T(1,128)S(1)} %pad_maximum_fusion.23), channel_id=1, source_target_pairs={{0,24},{8,16},{16,8},{24,0},{1,25},{9,17},{17,9},{25,1},{2,26},{10... | collective-permute-start | bytes 56 | tf_op jit(solution)/shard_map/ppermute | solution.py:58
  98.6 5.3 %collective-permute-start.15 = (f32[1,4]{1,0:T(1,128)S(1)}, f32[1,4]{1,0:T(1,128)S(1)}, u32[]{:S(2)}, u32[]{:S(2)}) collective-permute-start(f32[1,4]{1,0:T(1,128)S(1)} %pad_maximum_fusion.23), channel_id=1, source_target_pairs={{0,8},{8,0},{16,24},{24,16},{1,9},{9,1},{17,25},{25,17},{2,10},{10... | collective-permute-start | bytes 56 | tf_op jit(solution)/shard_map/ppermute | solution.py:58
  98.7 12.9 %collective-permute-start.18 = (f32[1,3,1,4096]{3,2,1,0:T(1,128)S(1)}, f32[1,3,1,4096]{3,2,1,0:T(1,128)S(1)}, u32[]{:S(2)}, u32[]{:S(2)}) collective-permute-start(f32[1,3,1,4096]{3,2,1,0:T(1,128)S(1)} %get-tuple-element.136), channel_id=1, source_target_pairs={{0,8},{8,16},{16,24},{1,9},{9,17},{17,25},{2,10},{10,18},{18,26},{... | collective-permute-start | bytes 147464 | tf_op jit(solution)/shard_map/ppermute | solution.py:247
  102.7 9.0 %collective-permute-start.19 = (f32[1,3,1,4096]{3,2,1,0:T(1,128)S(1)}, f32[1,3,1,4096]{3,2,1,0:T(1,128)S(1)}, u32[]{:S(2)}, u32[]{:S(2)}) collective-permute-start(f32[1,3,1,4096]{3,2,1,0:T(1,128)S(1)} %get-tuple-element.137), channel_id=1, source_target_pairs={{8,0},{16,8},{24,16},{9,1},{17,9},{25,17},{10,2},{18,10},{26,18},{... | collective-permute-start | bytes 147464 | tf_op jit(solution)/shard_map/ppermute | solution.py:248
  116.3 10.7 %collective-permute-start.21 = (f32[1,4]{1,0:T(1,128)S(1)}, f32[1,4]{1,0:T(1,128)S(1)}, u32[]{:S(2)}, u32[]{:S(2)}) collective-permute-start(f32[1,4]{1,0:T(1,128)S(1)} %pad_maximum_fusion.24), channel_id=1, source_target_pairs={{0,16},{8,24},{16,0},{24,8},{1,17},{9,25},{17,1},{25,9},{2,18},{10... | collective-permute-start | bytes 56 | tf_op jit(solution)/shard_map/ppermute | solution.py:58
  120.3 6.7 %collective-permute-start.22 = (f32[1,4]{1,0:T(1,128)S(1)}, f32[1,4]{1,0:T(1,128)S(1)}, u32[]{:S(2)}, u32[]{:S(2)}) collective-permute-start(f32[1,4]{1,0:T(1,128)S(1)} %pad_maximum_fusion.24), channel_id=1, source_target_pairs={{0,24},{8,16},{16,8},{24,0},{1,25},{9,17},{17,9},{25,1},{2,26},{10... | collective-permute-start | bytes 56 | tf_op jit(solution)/shard_map/ppermute | solution.py:58
  121.6 5.3 %collective-permute-start.20 = (f32[1,4]{1,0:T(1,128)S(1)}, f32[1,4]{1,0:T(1,128)S(1)}, u32[]{:S(2)}, u32[]{:S(2)}) collective-permute-start(f32[1,4]{1,0:T(1,128)S(1)} %pad_maximum_fusion.24), channel_id=1, source_target_pairs={{0,8},{8,0},{16,24},{24,16},{1,9},{9,1},{17,25},{25,17},{2,10},{10... | collective-permute-start | bytes 56 | tf_op jit(solution)/shard_map/ppermute | solution.py:58
  121.7 12.9 %collective-permute-start.23 = (f32[1,3,1,4096]{3,2,1,0:T(1,128)S(1)}, f32[1,3,1,4096]{3,2,1,0:T(1,128)S(1)}, u32[]{:S(2)}, u32[]{:S(2)}) collective-permute-start(f32[1,3,1,4096]{3,2,1,0:T(1,128)S(1)} %get-tuple-element.130), channel_id=1, source_target_pairs={{0,8},{8,16},{16,24},{1,9},{9,17},{17,25},{2,10},{10,18},{18,26},{... | collective-permute-start | bytes 147464 | tf_op jit(solution)/shard_map/ppermute | solution.py:247
  125.6 8.9 %collective-permute-start.24 = (f32[1,3,1,4096]{3,2,1,0:T(1,128)S(1)}, f32[1,3,1,4096]{3,2,1,0:T(1,128)S(1)}, u32[]{:S(2)}, u32[]{:S(2)}) collective-permute-start(f32[1,3,1,4096]{3,2,1,0:T(1,128)S(1)} %get-tuple-element.131), channel_id=1, source_target_pairs={{8,0},{16,8},{24,16},{9,1},{17,9},{25,17},{10,2},{18,10},{26,18},{... | collective-permute-start | bytes 147464 | tf_op jit(solution)/shard_map/ppermute | solution.py:248
  138.9 10.7 %collective-permute-start.26 = (f32[1,4]{1,0:T(1,128)S(1)}, f32[1,4]{1,0:T(1,128)S(1)}, u32[]{:S(2)}, u32[]{:S(2)}) collective-permute-start(f32[1,4]{1,0:T(1,128)S(1)} %pad_maximum_fusion.25), channel_id=1, source_target_pairs={{0,16},{8,24},{16,0},{24,8},{1,17},{9,25},{17,1},{25,9},{2,18},{10... | collective-permute-start | bytes 56 | tf_op jit(solution)/shard_map/ppermute | solution.py:58
  142.9 6.7 %collective-permute-start.27 = (f32[1,4]{1,0:T(1,128)S(1)}, f32[1,4]{1,0:T(1,128)S(1)}, u32[]{:S(2)}, u32[]{:S(2)}) collective-permute-start(f32[1,4]{1,0:T(1,128)S(1)} %pad_maximum_fusion.25), channel_id=1, source_target_pairs={{0,24},{8,16},{16,8},{24,0},{1,25},{9,17},{17,9},{25,1},{2,26},{10... | collective-permute-start | bytes 56 | tf_op jit(solution)/shard_map/ppermute | solution.py:58
  144.2 5.3 %collective-permute-start.25 = (f32[1,4]{1,0:T(1,128)S(1)}, f32[1,4]{1,0:T(1,128)S(1)}, u32[]{:S(2)}, u32[]{:S(2)}) collective-permute-start(f32[1,4]{1,0:T(1,128)S(1)} %pad_maximum_fusion.25), channel_id=1, source_target_pairs={{0,8},{8,0},{16,24},{24,16},{1,9},{9,1},{17,25},{25,17},{2,10},{10... | collective-permute-start | bytes 56 | tf_op jit(solution)/shard_map/ppermute | solution.py:58
  144.3 12.8 %collective-permute-start.28 = (f32[1,3,1,4096]{3,2,1,0:T(1,128)S(1)}, f32[1,3,1,4096]{3,2,1,0:T(1,128)S(1)}, u32[]{:S(2)}, u32[]{:S(2)}) collective-permute-start(f32[1,3,1,4096]{3,2,1,0:T(1,128)S(1)} %get-tuple-element.124), channel_id=1, source_target_pairs={{0,8},{8,16},{16,24},{1,9},{9,17},{17,25},{2,10},{10,18},{18,26},{... | collective-permute-start | bytes 147464 | tf_op jit(solution)/shard_map/ppermute | solution.py:247
  148.2 8.9 %collective-permute-start.29 = (f32[1,3,1,4096]{3,2,1,0:T(1,128)S(1)}, f32[1,3,1,4096]{3,2,1,0:T(1,128)S(1)}, u32[]{:S(2)}, u32[]{:S(2)}) collective-permute-start(f32[1,3,1,4096]{3,2,1,0:T(1,128)S(1)} %get-tuple-element.125), channel_id=1, source_target_pairs={{8,0},{16,8},{24,16},{9,1},{17,9},{25,17},{10,2},{18,10},{26,18},{... | collective-permute-start | bytes 147464 | tf_op jit(solution)/shard_map/ppermute | solution.py:248
  161.5 10.7 %collective-permute-start.31 = (f32[1,4]{1,0:T(1,128)S(1)}, f32[1,4]{1,0:T(1,128)S(1)}, u32[]{:S(2)}, u32[]{:S(2)}) collective-permute-start(f32[1,4]{1,0:T(1,128)S(1)} %pad_maximum_fusion.26), channel_id=1, source_target_pairs={{0,16},{8,24},{16,0},{24,8},{1,17},{9,25},{17,1},{25,9},{2,18},{10... | collective-permute-start | bytes 56 | tf_op jit(solution)/shard_map/ppermute | solution.py:58
  165.5 6.7 %collective-permute-start.32 = (f32[1,4]{1,0:T(1,128)S(1)}, f32[1,4]{1,0:T(1,128)S(1)}, u32[]{:S(2)}, u32[]{:S(2)}) collective-permute-start(f32[1,4]{1,0:T(1,128)S(1)} %pad_maximum_fusion.26), channel_id=1, source_target_pairs={{0,24},{8,16},{16,8},{24,0},{1,25},{9,17},{17,9},{25,1},{2,26},{10... | collective-permute-start | bytes 56 | tf_op jit(solution)/shard_map/ppermute | solution.py:58
  166.8 5.3 %collective-permute-start.30 = (f32[1,4]{1,0:T(1,128)S(1)}, f32[1,4]{1,0:T(1,128)S(1)}, u32[]{:S(2)}, u32[]{:S(2)}) collective-permute-start(f32[1,4]{1,0:T(1,128)S(1)} %pad_maximum_fusion.26), channel_id=1, source_target_pairs={{0,8},{8,0},{16,24},{24,16},{1,9},{9,1},{17,25},{25,17},{2,10},{10... | collective-permute-start | bytes 56 | tf_op jit(solution)/shard_map/ppermute | solution.py:58
  166.9 12.7 %collective-permute-start.33 = (f32[1,3,1,4096]{3,2,1,0:T(1,128)S(1)}, f32[1,3,1,4096]{3,2,1,0:T(1,128)S(1)}, u32[]{:S(2)}, u32[]{:S(2)}) collective-permute-start(f32[1,3,1,4096]{3,2,1,0:T(1,128)S(1)} %get-tuple-element.118), channel_id=1, source_target_pairs={{0,8},{8,16},{16,24},{1,9},{9,17},{17,25},{2,10},{10,18},{18,26},{... | collective-permute-start | bytes 147464 | tf_op jit(solution)/shard_map/ppermute | solution.py:247
  170.8 8.8 %collective-permute-start.34 = (f32[1,3,1,4096]{3,2,1,0:T(1,128)S(1)}, f32[1,3,1,4096]{3,2,1,0:T(1,128)S(1)}, u32[]{:S(2)}, u32[]{:S(2)}) collective-permute-start(f32[1,3,1,4096]{3,2,1,0:T(1,128)S(1)} %get-tuple-element.119), channel_id=1, source_target_pairs={{8,0},{16,8},{24,16},{9,1},{17,9},{25,17},{10,2},{18,10},{26,18},{... | collective-permute-start | bytes 147464 | tf_op jit(solution)/shard_map/ppermute | solution.py:248
  183.9 10.7 %collective-permute-start.36 = (f32[1,4]{1,0:T(1,128)S(1)}, f32[1,4]{1,0:T(1,128)S(1)}, u32[]{:S(2)}, u32[]{:S(2)}) collective-permute-start(f32[1,4]{1,0:T(1,128)S(1)} %pad_maximum_fusion.27), channel_id=1, source_target_pairs={{0,16},{8,24},{16,0},{24,8},{1,17},{9,25},{17,1},{25,9},{2,18},{10... | collective-permute-start | bytes 56 | tf_op jit(solution)/shard_map/ppermute | solution.py:58
  187.9 6.7 %collective-permute-start.37 = (f32[1,4]{1,0:T(1,128)S(1)}, f32[1,4]{1,0:T(1,128)S(1)}, u32[]{:S(2)}, u32[]{:S(2)}) collective-permute-start(f32[1,4]{1,0:T(1,128)S(1)} %pad_maximum_fusion.27), channel_id=1, source_target_pairs={{0,24},{8,16},{16,8},{24,0},{1,25},{9,17},{17,9},{25,1},{2,26},{10... | collective-permute-start | bytes 56 | tf_op jit(solution)/shard_map/ppermute | solution.py:58
  189.2 5.3 %collective-permute-start.35 = (f32[1,4]{1,0:T(1,128)S(1)}, f32[1,4]{1,0:T(1,128)S(1)}, u32[]{:S(2)}, u32[]{:S(2)}) collective-permute-start(f32[1,4]{1,0:T(1,128)S(1)} %pad_maximum_fusion.27), channel_id=1, source_target_pairs={{0,8},{8,0},{16,24},{24,16},{1,9},{9,1},{17,25},{25,17},{2,10},{10... | collective-permute-start | bytes 56 | tf_op jit(solution)/shard_map/ppermute | solution.py:58
  189.3 15.6 %collective-permute-start.38 = (f32[1,3,1,4096]{3,2,1,0:T(1,128)S(1)}, f32[1,3,1,4096]{3,2,1,0:T(1,128)S(1)}, u32[]{:S(2)}, u32[]{:S(2)}) collective-permute-start(f32[1,3,1,4096]{3,2,1,0:T(1,128)S(1)} %get-tuple-element.116), channel_id=1, source_target_pairs={{0,8},{8,16},{16,24},{1,9},{9,17},{17,25},{2,10},{10,18},{18,26},{... | collective-permute-start | bytes 147464 | tf_op jit(solution)/shard_map/ppermute | solution.py:247
  193.2 11.7 %collective-permute-start.39 = (f32[1,3,1,4096]{3,2,1,0:T(1,128)S(1)}, f32[1,3,1,4096]{3,2,1,0:T(1,128)S(1)}, u32[]{:S(2)}, u32[]{:S(2)}) collective-permute-start(f32[1,3,1,4096]{3,2,1,0:T(1,128)S(1)} %get-tuple-element.117), channel_id=1, source_target_pairs={{8,0},{16,8},{24,16},{9,1},{17,9},{25,17},{10,2},{18,10},{26,18},{... | collective-permute-start | bytes 147464 | tf_op jit(solution)/shard_map/ppermute | solution.py:248
  221.3 4.9 %collective-permute-start.42 = (f32[1,23]{1,0:T(1,128)S(1)}, f32[1,23]{1,0:T(1,128)S(1)}, u32[]{:S(2)}, u32[]{:S(2)}) collective-permute-start(f32[1,23]{1,0:T(1,128)S(1)} %stack.256), channel_id=1, source_target_pairs={{0,24},{8,16},{16,8},{24,0},{1,25},{9,17},{17,9},{25,1},{2,26},{10... | collective-permute-start | bytes 284 | tf_op jit(solution)/shard_map/ppermute | solution.py:58
  223.9 5.1 %collective-permute-start.41 = (f32[1,23]{1,0:T(1,128)S(1)}, f32[1,23]{1,0:T(1,128)S(1)}, u32[]{:S(2)}, u32[]{:S(2)}) collective-permute-start(f32[1,23]{1,0:T(1,128)S(1)} %stack.256), channel_id=1, source_target_pairs={{0,16},{8,24},{16,0},{24,8},{1,17},{9,25},{17,1},{25,9},{2,18},{10... | collective-permute-start | bytes 284 | tf_op jit(solution)/shard_map/ppermute | solution.py:58
  226.1 3.6 %collective-permute-start.40 = (f32[1,23]{1,0:T(1,128)S(1)}, f32[1,23]{1,0:T(1,128)S(1)}, u32[]{:S(2)}, u32[]{:S(2)}) collective-permute-start(f32[1,23]{1,0:T(1,128)S(1)} %stack.256), channel_id=1, source_target_pairs={{0,8},{8,0},{16,24},{24,16},{1,9},{9,1},{17,25},{25,17},{2,10},{10... | collective-permute-start | bytes 284 | tf_op jit(solution)/shard_map/ppermute | solution.py:58
  233.8 5.4 %collective-permute-start.43 = (f32[8,6]{1,0:T(8,128)S(1)}, f32[8,6]{1,0:T(8,128)S(1)}, u32[]{:S(2)}, u32[]{:S(2)}) collective-permute-start(f32[8,6]{1,0:T(8,128)S(1)} %broadcast_multiply_fusion), channel_id=1, source_target_pairs={{0,1},{1,0},{2,3},{3,2},{4,5},{5,4},{6,7},{7,6},{8,9},{9,8},{10,11... | collective-permute-start | bytes 584 | tf_op jit(solution)/shard_map/ppermute | solution.py:58
  235.6 27.2 %all-to-all-start.1 = ((f32[1,3,16,4096]{3,0,1,2:T(1,128)}), f32[1,3,16,4096]{3,0,1,2:T(1,128)S(1)}, u32[]{:S(2)}, u32[]{:S(2)}) async-start(f32[1,3,16,4096]{3,0,1,2:T(1,128)} %copy.51), calls=%async_computation.1 | async-start | bytes 1572864 | tf_op jit(solution)/shard_map/all_to_all | solution.py:316
  239.3 9.9 %collective-permute-start.46 = (f32[8,6]{1,0:T(8,128)S(1)}, f32[8,6]{1,0:T(8,128)S(1)}, u32[]{:S(2)}, u32[]{:S(2)}) collective-permute-start(f32[8,6]{1,0:T(8,128)S(1)} %fusion.111), channel_id=1, source_target_pairs={{0,6},{1,7},{2,4},{3,5},{4,2},{5,3},{6,0},{7,1},{8,14},{9,15},{10,... | collective-permute-start | bytes 584 | tf_op jit(solution)/shard_map/ppermute | solution.py:58
  242.4 9.9 %collective-permute-start.45 = (f32[8,6]{1,0:T(8,128)S(1)}, f32[8,6]{1,0:T(8,128)S(1)}, u32[]{:S(2)}, u32[]{:S(2)}) collective-permute-start(f32[8,6]{1,0:T(8,128)S(1)} %fusion.111), channel_id=1, source_target_pairs={{0,4},{1,5},{2,6},{3,7},{4,0},{5,1},{6,2},{7,3},{8,12},{9,13},{10,... | collective-permute-start | bytes 584 | tf_op jit(solution)/shard_map/ppermute | solution.py:58
  243.3 9.1 %collective-permute-start.44 = (f32[8,6]{1,0:T(8,128)S(1)}, f32[8,6]{1,0:T(8,128)S(1)}, u32[]{:S(2)}, u32[]{:S(2)}) collective-permute-start(f32[8,6]{1,0:T(8,128)S(1)} %fusion.111), channel_id=1, source_target_pairs={{0,2},{1,3},{2,0},{3,1},{4,6},{5,7},{6,4},{7,5},{8,10},{9,11},{10,... | collective-permute-start | bytes 584 | tf_op jit(solution)/shard_map/ppermute | solution.py:58
  252.6 4.3 %collective-permute-start.47 = (f32[4,6]{0,1:T(8,128)S(1)}, f32[4,6]{0,1:T(8,128)S(1)}, u32[]{:S(2)}, u32[]{:S(2)}) collective-permute-start(f32[4,6]{0,1:T(8,128)S(1)} %get-tuple-element.188), channel_id=1, source_target_pairs={{0,32},{32,0},{64,96},{96,64},{1,33},{33,1},{65,97},{97,65},{2,34}... | collective-permute-start | bytes 296 | tf_op jit(solution)/shard_map/ppermute | solution.py:83
  254.4 4.8 %collective-permute-start.49 = (f32[4,6]{0,1:T(8,128)S(1)}, f32[4,6]{0,1:T(8,128)S(1)}, u32[]{:S(2)}, u32[]{:S(2)}) collective-permute-start(f32[4,6]{0,1:T(8,128)S(1)} %get-tuple-element.189), channel_id=1, source_target_pairs={{0,96},{32,64},{64,32},{96,0},{1,97},{33,65},{65,33},{97,1},{2,98}... | collective-permute-start | bytes 296 | tf_op jit(solution)/shard_map/ppermute | solution.py:83
  256.9 5.1 %collective-permute-start.48 = (f32[4,6]{0,1:T(8,128)S(1)}, f32[4,6]{0,1:T(8,128)S(1)}, u32[]{:S(2)}, u32[]{:S(2)}) collective-permute-start(f32[4,6]{0,1:T(8,128)S(1)} %get-tuple-element.190), channel_id=1, source_target_pairs={{0,64},{32,96},{64,0},{96,32},{1,65},{33,97},{65,1},{97,33},{2,66}... | collective-permute-start | bytes 296 | tf_op jit(solution)/shard_map/ppermute | solution.py:83

commit v3 on v2

--- a/solution.py
+++ b/solution.py
@@ -285,14 +285,20 @@
                 ]
             terms.append(jnp.sum(stiff, axis=(1, 2)))
         local = jnp.stack(terms, -1)
-        sums = axis_sum(local, "yb")
-        norm_now = sums[:, 1]
-        alpha = norm_now / sums[:, 0]
+        if last:
+            sums = axis_sum(local, "yb")
+            norm_now = sums[:, 1]
+            alpha = norm_now / sums[:, 0]
+        else:
+            lanes = axis_sum(jnp.broadcast_to(local[:, :, None], local.shape + (128,)), "yb")
+            lane_alpha = lanes[:, 1] / lanes[:, 0]
+            lane_next = lanes[:, 1] - 2.0 * lane_alpha * lanes[:, 2] + lane_alpha * lane_alpha * lanes[:, 3]
+            lane_beta = lane_next / lanes[:, 1]
+            alpha = lane_alpha[:, 0]
         answer = answer + expand(alpha) * direction
         if last:
             break
-        norm_next = norm_now - 2.0 * alpha * sums[:, 2] + alpha * alpha * sums[:, 3]
-        beta = expand(norm_next / norm_now)
+        beta = expand(lane_beta[:, 0])
         residual = residual - expand(alpha) * image
         residual_edges = residual_edges - expand(alpha) * image_edges
         direction = residual + beta * direction

time: 266 us -> 228 us (0.86)
  between operations: 33.8 us -> 7.35 us
  waiting for transfers between devices: 23.9 us -> 47.4 us
  other arithmetic: 55.7 us -> 39.7 us
  starting transfers between devices: 104 us -> 89.5 us
  local copies, waits for them, and re-layouts: 31.8 us -> 27.8 us
    ppermute x7, waiting for transfers between devices: 0.02 us -> 24.2 us  [boundary_planes(): after = lax.ppermute(value[:, :, :1], 'yb', down)]
    broadcast_in_dim x0 -> x7, other arithmetic: none -> 17.3 us  [shards(): jnp.broadcast_to(local[:, :, None], local.shape + (128,))]
    another operation x8 -> x1, other arithmetic: 17.8 us -> 0.71 us  [the longest x7 17.1 us: shards(): local = jnp.stack(terms, -1)]
    add x9, other arithmetic: 17.2 us -> 0.59 us  [tree_sum(): v + cur[o | 1 << level]]
    ppermute x28, starting transfers between devices: 45.2 us -> 34 us  [axis_sum(): vals[o] = lax.ppermute(value, axis, [(i, i ^ mask) for i in range(size)])]
    slice x7 -> x0, local copies, waits for them, and re-layouts: 4.49 us -> none  [shards(): norm_next = norm_now - 2.0 * alpha * sums[:, 2] + alpha * alpha * sums[:, 3]]
    ppermute x7, starting transfers between devices: 27.5 us -> 24.5 us  [boundary_planes(): before = lax.ppermute(value[:, :, -1:], 'yb', up)]
  transfers between devices with their start and end apart: 52 -> 52, of which waited for: 9 -> 16; matrix products, arithmetic and copies ran while one was open for 13% -> 7% of each run, Pallas kernels for 6% -> 7%
where the time goes in v3:
time: 228 us; the launch traced here: 227 us
  starting transfers between devices  89.5 us (39%)
  waiting for transfers between devices  47.4 us (21%)
  other arithmetic  39.7 us (17%)
  local copies, waits for them, and re-layouts  27.8 us (12%)
  Pallas kernels  15 us (7%)
  between operations  7.35 us (3%)
    ppermute x28, starting transfers between devices, axis_sum(): vals[o] = lax.ppermute(value, axis, [(i, i ^ mask) for i in range(size)])  34 us
    ppermute x7, starting transfers between devices, boundary_planes(): before = lax.ppermute(value[:, :, -1:], 'yb', up)  24.5 us
    ppermute x7, waiting for transfers between devices, boundary_planes(): after = lax.ppermute(value[:, :, :1], 'yb', down)  24.2 us
    broadcast_in_dim x7, other arithmetic, shards(): jnp.broadcast_to(local[:, :, None], local.shape + (128,))  17.3 us
    pallas_call x1, Pallas kernels, stiffness(): pl.pallas_call(stiffness_kernel, grid=(rves,), in_specs=[pl.BlockSpec(pie...  15 us
    another operation x1, local copies, waits for them, and re-layouts, shards(): local = jnp.stack(terms, -1)  14.5 us
    reduce_sum x8, other arithmetic, local_dot(): return jnp.sum(first * second, axis=(1, 2, 3))  12.3 us
    ppermute x28, waiting for transfers between devices, axis_sum(): vals[o] = lax.ppermute(value, axis, [(i, i ^ mask) for i in range(size)])  11.9 us
  transfers between devices with their start and end apart: 52, of which 16 were waited for; matrix products, arithmetic and copies ran while one was open for 7% of the time, Pallas kernels for 7%

profile of v3, /device:TPU:0, one launch (start us, length us, event | category | flops | bytes accessed | tf_op | source)
XLA Modules:
  0.0 227.1 jit_solution(6325243595513324504)
XLA Ops:
  0.7 4.1 %collective-permute-start.3 = (f32[4,6]{1,0:T(4,128)}, f32[4,6]{1,0:T(4,128)S(1)}, u32[]{:S(2)}, u32[]{:S(2)}) collective-permute-start(f32[4,6]{1,0:T(4,128)} %param.10), channel_id=1, source_target_pairs={{0,64},{32,96},{64,0},{96,32},{1,65},{33,97},{65,1},{97,33},{2,66}... | collective-permute-start | bytes 296 | tf_op jit(solution)/shard_map/ppermute | solution.py:68
  7.1 15.0 %shard_map.95 = f32[8,2,4096]{2,1,0:T(2,128)} custom-call(bf16[3,16,64]{2,1,0:T(8,128)(2,1)} %fusion.95.pieces_ref, s32[8,2,4096]{2,1,0:T(2,128)} %codes_ref.1, s32[8,2,4096]{2,1,0:T(2,128)} %grains_ref.1), custom_call_target="tpu_custom_call" | custom-call | tf_op jit(solution)/shard_map/pallas_call | solution.py:122
  22.1 4.3 %all-to-all-start = ((f32[8,2,4096]{2,1,0:T(2,128)}), f32[8,2,4096]{2,1,0:T(2,128)S(1)}, u32[]{:S(2)}, u32[]{:S(2)}) async-start(f32[8,2,4096]{2,1,0:T(2,128)} %shard_map.95), calls=%async_computation | async-start | bytes 524288 | tf_op jit(solution)/shard_map/all_to_all | solution.py:186
  31.2 2.7 %all-to-all-done = f32[8,2,4096]{2,1,0:T(2,128)S(1)} async-done(((f32[8,2,4096]{2,1,0:T(2,128)}), f32[8,2,4096]{2,1,0:T(2,128)S(1)}, u32[]{:S(2)}, u32[]{:S(2)}) %all-to-all-start) | async-done | bytes 262176 | tf_op jit(solution)/shard_map/all_to_all | solution.py:186
  34.1 3.5 %collective-permute-start.1 = (f32[1,2,4096]{2,1,0:T(2,128)S(1)}, f32[1,2,4096]{2,1,0:T(2,128)S(1)}, u32[]{:S(2)}, u32[]{:S(2)}) collective-permute-start(f32[1,2,4096]{2,1,0:T(2,128)S(1)} %get-tuple-element.179), channel_id=1, source_target_pairs={{0,8},{8,16},{16,24},{1,9},{9,17},{17,25},{2,10},{10,18},{18,26},{... | collective-permute-start | bytes 98312 | tf_op jit(solution)/shard_map/ppermute | solution.py:24
  37.6 1.3 collective-permute-start
  39.9 3.5 %collective-permute-done = f32[1,2,4096]{2,1,0:T(2,128)S(1)} collective-permute-done((f32[1,2,4096]{2,1,0:T(2,128)S(1)}, f32[1,2,4096]{2,1,0:T(2,128)S(1)}, u32[]{:S(2)}, u32[]{:S(2)}) %collective-permute-start) | collective-permute-done | bytes 32800 | tf_op jit(solution)/shard_map/ppermute | solution.py:25
  45.6 1.5 multiply_reduce_fusion.29
  47.1 1.9 maximum_bitcast_fusion
  49.1 2.9 %collective-permute-start.6 = (f32[1,4,128]{2,1,0:T(4,128)S(1)}, f32[1,4,128]{2,1,0:T(4,128)S(1)}, u32[]{:S(2)}, u32[]{:S(2)}) collective-permute-start(f32[1,4,128]{2,1,0:T(4,128)S(1)} %broadcast_in_dim.37), channel_id=1, source_target_pairs={{0,16},{8,24},{16,0},{24,8},{1,17},{9,25},{17,1},{25,9},{2,18},{10... | collective-permute-start | bytes 6152 | tf_op jit(solution)/shard_map/ppermute | solution.py:58
  52.0 1.3 collective-permute-start.7
  53.5 3.9 %collective-permute-start.8 = (f32[1,3,1,4096]{3,2,1,0:T(1,128)S(1)}, f32[1,3,1,4096]{3,2,1,0:T(1,128)S(1)}, u32[]{:S(2)}, u32[]{:S(2)}) collective-permute-start(f32[1,3,1,4096]{3,2,1,0:T(1,128)S(1)} %get-tuple-element.162), channel_id=1, source_target_pairs={{0,8},{8,16},{16,24},{1,9},{9,17},{17,25},{2,10},{10,18},{18,26},{... | collective-permute-start | bytes 147464 | tf_op jit(solution)/shard_map/ppermute | solution.py:247
  57.4 1.3 collective-permute-start.9
  59.6 3.8 %collective-permute-done.9 = f32[1,3,1,4096]{3,2,1,0:T(1,128)S(1)} collective-permute-done((f32[1,3,1,4096]{3,2,1,0:T(1,128)S(1)}, f32[1,3,1,4096]{3,2,1,0:T(1,128)S(1)}, u32[]{:S(2)}, u32[]{:S(2)}) %collective-permute-start.9) | collective-permute-done | bytes 49184 | tf_op jit(solution)/shard_map/ppermute | solution.py:248
  63.7 1.5 multiply_reduce_fusion.27
  65.2 2.6 %maximum_bitcast_fusion.1 = f32[4]{0:T(128)S(1)} fusion(f32[1,1]{1,0:T(1,128)} %bitcast.32, f32[1,1]{1,0:T(1,128)} %bitcast.31, f32[1,1]{1,0:T(1,128)} %bitcast.30, f32[1,1]{1,0:T(1,128)} %bitcast.29), kind=kLoop, calls=%fused_computation.272 | loop fusion | flops 12 | bytes 32 | tf_op jit(solution)/shard_map/broadcast_in_dim | solution.py:293
  67.9 1.3 collective-permute-start.11
  69.2 2.6 %collective-permute-start.12 = (f32[1,4,128]{2,1,0:T(4,128)S(1)}, f32[1,4,128]{2,1,0:T(4,128)S(1)}, u32[]{:S(2)}, u32[]{:S(2)}) collective-permute-start(f32[1,4,128]{2,1,0:T(4,128)S(1)} %broadcast_in_dim.39), channel_id=1, source_target_pairs={{0,24},{8,16},{16,8},{24,0},{1,25},{9,17},{17,9},{25,1},{2,26},{10... | collective-permute-start | bytes 6152 | tf_op jit(solution)/shard_map/ppermute | solution.py:58
  71.9 3.9 %collective-permute-start.13 = (f32[1,3,1,4096]{3,2,1,0:T(1,128)S(1)}, f32[1,3,1,4096]{3,2,1,0:T(1,128)S(1)}, u32[]{:S(2)}, u32[]{:S(2)}) collective-permute-start(f32[1,3,1,4096]{3,2,1,0:T(1,128)S(1)} %get-tuple-element.156), channel_id=1, source_target_pairs={{0,8},{8,16},{16,24},{1,9},{9,17},{17,25},{2,10},{10,18},{18,26},{... | collective-permute-start | bytes 147464 | tf_op jit(solution)/shard_map/ppermute | solution.py:247
  75.8 1.3 collective-permute-start.14
  78.0 3.8 %collective-permute-done.14 = f32[1,3,1,4096]{3,2,1,0:T(1,128)S(1)} collective-permute-done((f32[1,3,1,4096]{3,2,1,0:T(1,128)S(1)}, f32[1,3,1,4096]{3,2,1,0:T(1,128)S(1)}, u32[]{:S(2)}, u32[]{:S(2)}) %collective-permute-start.14) | collective-permute-done | bytes 49184 | tf_op jit(solution)/shard_map/ppermute | solution.py:248
  82.3 1.5 multiply_reduce_fusion.23
  83.8 2.6 %maximum_bitcast_fusion.2 = f32[4]{0:T(128)S(1)} fusion(f32[1,1]{1,0:T(1,128)} %bitcast.43, f32[1,1]{1,0:T(1,128)} %bitcast.42, f32[1,1]{1,0:T(1,128)} %bitcast.41, f32[1,1]{1,0:T(1,128)} %bitcast.40), kind=kLoop, calls=%fused_computation.273 | loop fusion | flops 12 | bytes 32 | tf_op jit(solution)/shard_map/broadcast_in_dim | solution.py:293
  86.5 2.6 %collective-permute-start.17 = (f32[1,4,128]{2,1,0:T(4,128)S(1)}, f32[1,4,128]{2,1,0:T(4,128)S(1)}, u32[]{:S(2)}, u32[]{:S(2)}) collective-permute-start(f32[1,4,128]{2,1,0:T(4,128)S(1)} %broadcast_in_dim.41), channel_id=1, source_target_pairs={{0,24},{8,16},{16,8},{24,0},{1,25},{9,17},{17,9},{25,1},{2,26},{10... | collective-permute-start | bytes 6152 | tf_op jit(solution)/shard_map/ppermute | solution.py:58
  90.0 3.1 %collective-permute-start.18 = (f32[1,3,1,4096]{3,2,1,0:T(1,128)S(1)}, f32[1,3,1,4096]{3,2,1,0:T(1,128)S(1)}, u32[]{:S(2)}, u32[]{:S(2)}) collective-permute-start(f32[1,3,1,4096]{3,2,1,0:T(1,128)S(1)} %get-tuple-element.150), channel_id=1, source_target_pairs={{0,8},{8,16},{16,24},{1,9},{9,17},{17,25},{2,10},{10,18},{18,26},{... | collective-permute-start | bytes 147464 | tf_op jit(solution)/shard_map/ppermute | solution.py:247
  93.1 1.3 collective-permute-start.19
  95.3 3.8 %collective-permute-done.19 = f32[1,3,1,4096]{3,2,1,0:T(1,128)S(1)} collective-permute-done((f32[1,3,1,4096]{3,2,1,0:T(1,128)S(1)}, f32[1,3,1,4096]{3,2,1,0:T(1,128)S(1)}, u32[]{:S(2)}, u32[]{:S(2)}) %collective-permute-start.19) | collective-permute-done | bytes 49184 | tf_op jit(solution)/shard_map/ppermute | solution.py:248
  99.7 1.5 multiply_reduce_fusion.19
  101.2 2.6 %maximum_bitcast_fusion.3 = f32[4]{0:T(128)S(1)} fusion(f32[1,1]{1,0:T(1,128)} %bitcast.54, f32[1,1]{1,0:T(1,128)} %bitcast.53, f32[1,1]{1,0:T(1,128)} %bitcast.52, f32[1,1]{1,0:T(1,128)} %bitcast.51), kind=kLoop, calls=%fused_computation.274 | loop fusion | flops 12 | bytes 32 | tf_op jit(solution)/shard_map/broadcast_in_dim | solution.py:293
  104.7 1.8 collective-permute-start.22
  107.4 3.1 %collective-permute-start.23 = (f32[1,3,1,4096]{3,2,1,0:T(1,128)S(1)}, f32[1,3,1,4096]{3,2,1,0:T(1,128)S(1)}, u32[]{:S(2)}, u32[]{:S(2)}) collective-permute-start(f32[1,3,1,4096]{3,2,1,0:T(1,128)S(1)} %get-tuple-element.144), channel_id=1, source_target_pairs={{0,8},{8,16},{16,24},{1,9},{9,17},{17,25},{2,10},{10,18},{18,26},{... | collective-permute-start | bytes 147464 | tf_op jit(solution)/shard_map/ppermute | solution.py:247
  110.5 1.3 collective-permute-start.24
  112.7 3.8 %collective-permute-done.24 = f32[1,3,1,4096]{3,2,1,0:T(1,128)S(1)} collective-permute-done((f32[1,3,1,4096]{3,2,1,0:T(1,128)S(1)}, f32[1,3,1,4096]{3,2,1,0:T(1,128)S(1)}, u32[]{:S(2)}, u32[]{:S(2)}) %collective-permute-start.24) | collective-permute-done | bytes 49184 | tf_op jit(solution)/shard_map/ppermute | solution.py:248
  116.8 1.5 multiply_reduce_fusion.15
  118.3 2.6 %maximum_bitcast_fusion.4 = f32[4]{0:T(128)S(1)} fusion(f32[1,1]{1,0:T(1,128)} %bitcast.65, f32[1,1]{1,0:T(1,128)} %bitcast.64, f32[1,1]{1,0:T(1,128)} %bitcast.63, f32[1,1]{1,0:T(1,128)} %bitcast.62), kind=kLoop, calls=%fused_computation.275 | loop fusion | flops 12 | bytes 32 | tf_op jit(solution)/shard_map/broadcast_in_dim | solution.py:293
  121.8 2.6 %collective-permute-start.27 = (f32[1,4,128]{2,1,0:T(4,128)S(1)}, f32[1,4,128]{2,1,0:T(4,128)S(1)}, u32[]{:S(2)}, u32[]{:S(2)}) collective-permute-start(f32[1,4,128]{2,1,0:T(4,128)S(1)} %broadcast_in_dim.45), channel_id=1, source_target_pairs={{0,24},{8,16},{16,8},{24,0},{1,25},{9,17},{17,9},{25,1},{2,26},{10... | collective-permute-start | bytes 6152 | tf_op jit(solution)/shard_map/ppermute | solution.py:58
  124.5 3.9 %collective-permute-start.28 = (f32[1,3,1,4096]{3,2,1,0:T(1,128)S(1)}, f32[1,3,1,4096]{3,2,1,0:T(1,128)S(1)}, u32[]{:S(2)}, u32[]{:S(2)}) collective-permute-start(f32[1,3,1,4096]{3,2,1,0:T(1,128)S(1)} %get-tuple-element.138), channel_id=1, source_target_pairs={{0,8},{8,16},{16,24},{1,9},{9,17},{17,25},{2,10},{10,18},{18,26},{... | collective-permute-start | bytes 147464 | tf_op jit(solution)/shard_map/ppermute | solution.py:247
  128.4 1.3 collective-permute-start.29
  130.6 3.8 %collective-permute-done.29 = f32[1,3,1,4096]{3,2,1,0:T(1,128)S(1)} collective-permute-done((f32[1,3,1,4096]{3,2,1,0:T(1,128)S(1)}, f32[1,3,1,4096]{3,2,1,0:T(1,128)S(1)}, u32[]{:S(2)}, u32[]{:S(2)}) %collective-permute-start.29) | collective-permute-done | bytes 49184 | tf_op jit(solution)/shard_map/ppermute | solution.py:248
  134.8 1.5 multiply_reduce_fusion.11
  136.3 2.6 %maximum_bitcast_fusion.5 = f32[4]{0:T(128)S(1)} fusion(f32[1,1]{1,0:T(1,128)} %bitcast.76, f32[1,1]{1,0:T(1,128)} %bitcast.75, f32[1,1]{1,0:T(1,128)} %bitcast.74, f32[1,1]{1,0:T(1,128)} %bitcast.73), kind=kLoop, calls=%fused_computation.276 | loop fusion | flops 12 | bytes 32 | tf_op jit(solution)/shard_map/broadcast_in_dim | solution.py:293
  139.0 2.6 %collective-permute-start.32 = (f32[1,4,128]{2,1,0:T(4,128)S(1)}, f32[1,4,128]{2,1,0:T(4,128)S(1)}, u32[]{:S(2)}, u32[]{:S(2)}) collective-permute-start(f32[1,4,128]{2,1,0:T(4,128)S(1)} %broadcast_in_dim.47), channel_id=1, source_target_pairs={{0,24},{8,16},{16,8},{24,0},{1,25},{9,17},{17,9},{25,1},{2,26},{10... | collective-permute-start | bytes 6152 | tf_op jit(solution)/shard_map/ppermute | solution.py:58
  142.5 3.1 %collective-permute-start.33 = (f32[1,3,1,4096]{3,2,1,0:T(1,128)S(1)}, f32[1,3,1,4096]{3,2,1,0:T(1,128)S(1)}, u32[]{:S(2)}, u32[]{:S(2)}) collective-permute-start(f32[1,3,1,4096]{3,2,1,0:T(1,128)S(1)} %get-tuple-element.132), channel_id=1, source_target_pairs={{0,8},{8,16},{16,24},{1,9},{9,17},{17,25},{2,10},{10,18},{18,26},{... | collective-permute-start | bytes 147464 | tf_op jit(solution)/shard_map/ppermute | solution.py:247
  145.7 1.3 collective-permute-start.34
  147.8 3.8 %collective-permute-done.34 = f32[1,3,1,4096]{3,2,1,0:T(1,128)S(1)} collective-permute-done((f32[1,3,1,4096]{3,2,1,0:T(1,128)S(1)}, f32[1,3,1,4096]{3,2,1,0:T(1,128)S(1)}, u32[]{:S(2)}, u32[]{:S(2)}) %collective-permute-start.34) | collective-permute-done | bytes 49184 | tf_op jit(solution)/shard_map/ppermute | solution.py:248
  151.9 1.5 multiply_reduce_fusion.7
  153.4 2.6 %maximum_bitcast_fusion.6 = f32[4]{0:T(128)S(1)} fusion(f32[1,1]{1,0:T(1,128)} %bitcast.87, f32[1,1]{1,0:T(1,128)} %bitcast.86, f32[1,1]{1,0:T(1,128)} %bitcast.85, f32[1,1]{1,0:T(1,128)} %bitcast.84), kind=kLoop, calls=%fused_computation.277 | loop fusion | flops 12 | bytes 32 | tf_op jit(solution)/shard_map/broadcast_in_dim | solution.py:293
  156.9 1.8 collective-permute-start.37
  159.6 3.4 %collective-permute-start.38 = (f32[1,3,1,4096]{3,2,1,0:T(1,128)S(1)}, f32[1,3,1,4096]{3,2,1,0:T(1,128)S(1)}, u32[]{:S(2)}, u32[]{:S(2)}) collective-permute-start(f32[1,3,1,4096]{3,2,1,0:T(1,128)S(1)} %get-tuple-element.130), channel_id=1, source_target_pairs={{0,8},{8,16},{16,24},{1,9},{9,17},{17,25},{2,10},{10,18},{18,26},{... | collective-permute-start | bytes 147464 | tf_op jit(solution)/shard_map/ppermute | solution.py:247
  163.0 1.3 collective-permute-start.39
  167.7 1.3 collective-permute-done.39
  169.3 1.6 multiply_reduce_fusion
  170.9 14.5 %stack.256 = f32[1,23]{1,0:T(1,128)S(1)} concatenate(f32[1,1]{1,0:T(1,128)} %bitcast.95, f32[1,1]{1,0:T(1,128)} %bitcast.96, f32[1,1]{1,0:T(1,128)} %bitcast.97, f32[1,1]{1,0:T(1,128)} %bitcast.98, f32[1,1]{1,0:T(1,128)} %bitcast.100, f32[1,1]{1,0:T(1,128)} %bitcast.101, f32[1,1]{1,0:T(1,128)} %bitcast.102, f32[1,1]{1,0:T(1,128)} %bitcast.104, f32[1,1]{1,0:T(1,128)} %bitcast.105, ...), dimensions={1} | concatenate | bytes 184 | tf_op jit(solution)/shard_map/stack | solution.py:287
  186.2 2.7 %collective-permute-start.41 = (f32[1,23]{1,0:T(1,128)S(1)}, f32[1,23]{1,0:T(1,128)S(1)}, u32[]{:S(2)}, u32[]{:S(2)}) collective-permute-start(f32[1,23]{1,0:T(1,128)S(1)} %stack.256), channel_id=1, source_target_pairs={{0,16},{8,24},{16,0},{24,8},{1,17},{9,25},{17,1},{25,9},{2,18},{10... | collective-permute-start | bytes 284 | tf_op jit(solution)/shard_map/ppermute | solution.py:58
  196.7 1.7 copy.51
  198.4 3.5 %all-to-all-start.1 = ((f32[1,3,16,4096]{3,0,1,2:T(1,128)}), f32[1,3,16,4096]{3,0,1,2:T(1,128)S(1)}, u32[]{:S(2)}, u32[]{:S(2)}) async-start(f32[1,3,16,4096]{3,0,1,2:T(1,128)} %copy.51), calls=%async_computation.1 | async-start | bytes 1572864 | tf_op jit(solution)/shard_map/all_to_all | solution.py:322
  202.1 3.2 %collective-permute-start.46 = (f32[8,6]{1,0:T(8,128)S(1)}, f32[8,6]{1,0:T(8,128)S(1)}, u32[]{:S(2)}, u32[]{:S(2)}) collective-permute-start(f32[8,6]{1,0:T(8,128)S(1)} %fusion.111), channel_id=1, source_target_pairs={{0,6},{1,7},{2,4},{3,5},{4,2},{5,3},{6,0},{7,1},{8,14},{9,15},{10,... | collective-permute-start | bytes 584 | tf_op jit(solution)/shard_map/ppermute | solution.py:58
  206.2 5.8 %collective-permute-done.46 = f32[8,6]{1,0:T(8,128)S(1)} collective-permute-done((f32[8,6]{1,0:T(8,128)S(1)}, f32[8,6]{1,0:T(8,128)S(1)}, u32[]{:S(2)}, u32[]{:S(2)}) %collective-permute-start.46) | collective-permute-done | bytes 224 | tf_op jit(solution)/shard_map/ppermute | solution.py:58
  212.0 3.2 %collective-permute-done.45 = f32[8,6]{1,0:T(8,128)S(1)} collective-permute-done((f32[8,6]{1,0:T(8,128)S(1)}, f32[8,6]{1,0:T(8,128)S(1)}, u32[]{:S(2)}, u32[]{:S(2)}) %collective-permute-start.45) | collective-permute-done | bytes 224 | tf_op jit(solution)/shard_map/ppermute | solution.py:58
  215.5 1.7 collective-permute-start.47
  217.2 2.5 %collective-permute-start.49 = (f32[4,6]{0,1:T(8,128)S(1)}, f32[4,6]{0,1:T(8,128)S(1)}, u32[]{:S(2)}, u32[]{:S(2)}) collective-permute-start(f32[4,6]{0,1:T(8,128)S(1)} %get-tuple-element.203), channel_id=1, source_target_pairs={{0,96},{32,64},{64,32},{96,0},{1,97},{33,65},{65,33},{97,1},{2,98}... | collective-permute-start | bytes 296 | tf_op jit(solution)/shard_map/ppermute | solution.py:83
  219.7 2.3 %collective-permute-done.49 = f32[4,6]{0,1:T(8,128)S(1)} collective-permute-done((f32[4,6]{0,1:T(8,128)S(1)}, f32[4,6]{0,1:T(8,128)S(1)}, u32[]{:S(2)}, u32[]{:S(2)}) %collective-permute-start.49) | collective-permute-done | bytes 128 | tf_op jit(solution)/shard_map/ppermute | solution.py:83
  222.0 2.8 %collective-permute-done.48 = f32[4,6]{0,1:T(8,128)S(1)} collective-permute-done((f32[4,6]{0,1:T(8,128)S(1)}, f32[4,6]{0,1:T(8,128)S(1)}, u32[]{:S(2)}, u32[]{:S(2)}) %collective-permute-start.48) | collective-permute-done | bytes 128 | tf_op jit(solution)/shard_map/ppermute | solution.py:83
  225.7 1.5 copy.57
  (171 shorter events, 33.0 us)
Async XLA Ops:
  0.6 25.8 %copy-start.1 = (s32[6]{0:T(128)S(1)}, s32[6]{0:T(128)}, u32[]{:S(2)}) copy-start(s32[6]{0:T(128)} %constant.189) | copy-start | bytes 76
  0.6 25.8 %copy-start.2 = (s32[6]{0:T(128)S(1)}, s32[6]{0:T(128)}, u32[]{:S(2)}) copy-start(s32[6]{0:T(128)} %constant.188) | copy-start | bytes 76
  0.7 25.8 %copy-start = (f32[4,6]{1,0:T(4,128)S(1)}, f32[4,6]{1,0:T(4,128)}, u32[]{:S(2)}) copy-start(f32[4,6]{1,0:T(4,128)} %param.10) | copy-start | bytes 292
  0.7 25.8 %copy-start.3 = (s32[8]{0:T(128)S(1)}, s32[8]{0:T(128)}, u32[]{:S(2)}) copy-start(s32[8]{0:T(128)} %param.15) | copy-start | bytes 100
  0.7 25.8 %collective-permute-start.3 = (f32[4,6]{1,0:T(4,128)}, f32[4,6]{1,0:T(4,128)S(1)}, u32[]{:S(2)}, u32[]{:S(2)}) collective-permute-start(f32[4,6]{1,0:T(4,128)} %param.10), channel_id=1, source_target_pairs={{0,64},{32,96},{64,0},{96,32},{1,65},{33,97},{65,1},{97,33},{2,66}... | collective-permute-start | bytes 296 | tf_op jit(solution)/shard_map/ppermute | solution.py:68
  4.7 21.7 %collective-permute-start.2 = (f32[4,6]{1,0:T(4,128)}, f32[4,6]{1,0:T(4,128)S(1)}, u32[]{:S(2)}, u32[]{:S(2)}) collective-permute-start(f32[4,6]{1,0:T(4,128)} %param.10), channel_id=1, source_target_pairs={{0,96},{32,64},{64,32},{96,0},{1,97},{33,65},{65,33},{97,1},{2,98}... | collective-permute-start | bytes 296 | tf_op jit(solution)/shard_map/ppermute | solution.py:68
  5.5 21.0 %collective-permute-start.4 = (f32[4,6]{1,0:T(4,128)}, f32[4,6]{1,0:T(4,128)S(1)}, u32[]{:S(2)}, u32[]{:S(2)}) collective-permute-start(f32[4,6]{1,0:T(4,128)} %param.10), channel_id=1, source_target_pairs={{0,32},{32,0},{64,96},{96,64},{1,33},{33,1},{65,97},{97,65},{2,34}... | collective-permute-start | bytes 296 | tf_op jit(solution)/shard_map/ppermute | solution.py:68
  22.1 11.8 %all-to-all-start = ((f32[8,2,4096]{2,1,0:T(2,128)}), f32[8,2,4096]{2,1,0:T(2,128)S(1)}, u32[]{:S(2)}, u32[]{:S(2)}) async-start(f32[8,2,4096]{2,1,0:T(2,128)} %shard_map.95), calls=%async_computation | async-start | bytes 524288 | tf_op jit(solution)/shard_map/all_to_all | solution.py:186
  34.1 5.8 %collective-permute-start.1 = (f32[1,2,4096]{2,1,0:T(2,128)S(1)}, f32[1,2,4096]{2,1,0:T(2,128)S(1)}, u32[]{:S(2)}, u32[]{:S(2)}) collective-permute-start(f32[1,2,4096]{2,1,0:T(2,128)S(1)} %get-tuple-element.179), channel_id=1, source_target_pairs={{0,8},{8,16},{16,24},{1,9},{9,17},{17,25},{2,10},{10,18},{18,26},{... | collective-permute-start | bytes 98312 | tf_op jit(solution)/shard_map/ppermute | solution.py:24
  37.6 5.8 %collective-permute-start = (f32[1,2,4096]{2,1,0:T(2,128)S(1)}, f32[1,2,4096]{2,1,0:T(2,128)S(1)}, u32[]{:S(2)}, u32[]{:S(2)}) collective-permute-start(f32[1,2,4096]{2,1,0:T(2,128)S(1)} %get-tuple-element.180), channel_id=1, source_target_pairs={{8,0},{16,8},{24,16},{9,1},{17,9},{25,17},{10,2},{18,10},{26,18},{... | collective-permute-start | bytes 98312 | tf_op jit(solution)/shard_map/ppermute | solution.py:25
  49.1 9.6 %collective-permute-start.6 = (f32[1,4,128]{2,1,0:T(4,128)S(1)}, f32[1,4,128]{2,1,0:T(4,128)S(1)}, u32[]{:S(2)}, u32[]{:S(2)}) collective-permute-start(f32[1,4,128]{2,1,0:T(4,128)S(1)} %broadcast_in_dim.37), channel_id=1, source_target_pairs={{0,16},{8,24},{16,0},{24,8},{1,17},{9,25},{17,1},{25,9},{2,18},{10... | collective-permute-start | bytes 6152 | tf_op jit(solution)/shard_map/ppermute | solution.py:58
  52.0 6.7 %collective-permute-start.7 = (f32[1,4,128]{2,1,0:T(4,128)S(1)}, f32[1,4,128]{2,1,0:T(4,128)S(1)}, u32[]{:S(2)}, u32[]{:S(2)}) collective-permute-start(f32[1,4,128]{2,1,0:T(4,128)S(1)} %broadcast_in_dim.37), channel_id=1, source_target_pairs={{0,24},{8,16},{16,8},{24,0},{1,25},{9,17},{17,9},{25,1},{2,26},{10... | collective-permute-start | bytes 6152 | tf_op jit(solution)/shard_map/ppermute | solution.py:58
  53.4 5.3 %collective-permute-start.5 = (f32[1,4,128]{2,1,0:T(4,128)S(1)}, f32[1,4,128]{2,1,0:T(4,128)S(1)}, u32[]{:S(2)}, u32[]{:S(2)}) collective-permute-start(f32[1,4,128]{2,1,0:T(4,128)S(1)} %broadcast_in_dim.37), channel_id=1, source_target_pairs={{0,8},{8,0},{16,24},{24,16},{1,9},{9,1},{17,25},{25,17},{2,10},{10... | collective-permute-start | bytes 6152 | tf_op jit(solution)/shard_map/ppermute | solution.py:58
  53.5 6.1 %collective-permute-start.8 = (f32[1,3,1,4096]{3,2,1,0:T(1,128)S(1)}, f32[1,3,1,4096]{3,2,1,0:T(1,128)S(1)}, u32[]{:S(2)}, u32[]{:S(2)}) collective-permute-start(f32[1,3,1,4096]{3,2,1,0:T(1,128)S(1)} %get-tuple-element.162), channel_id=1, source_target_pairs={{0,8},{8,16},{16,24},{1,9},{9,17},{17,25},{2,10},{10,18},{18,26},{... | collective-permute-start | bytes 147464 | tf_op jit(solution)/shard_map/ppermute | solution.py:247
  57.4 6.0 %collective-permute-start.9 = (f32[1,3,1,4096]{3,2,1,0:T(1,128)S(1)}, f32[1,3,1,4096]{3,2,1,0:T(1,128)S(1)}, u32[]{:S(2)}, u32[]{:S(2)}) collective-permute-start(f32[1,3,1,4096]{3,2,1,0:T(1,128)S(1)} %get-tuple-element.163), channel_id=1, source_target_pairs={{8,0},{16,8},{24,16},{9,1},{17,9},{25,17},{10,2},{18,10},{26,18},{... | collective-permute-start | bytes 147464 | tf_op jit(solution)/shard_map/ppermute | solution.py:248
  67.9 9.3 %collective-permute-start.11 = (f32[1,4,128]{2,1,0:T(4,128)S(1)}, f32[1,4,128]{2,1,0:T(4,128)S(1)}, u32[]{:S(2)}, u32[]{:S(2)}) collective-permute-start(f32[1,4,128]{2,1,0:T(4,128)S(1)} %broadcast_in_dim.39), channel_id=1, source_target_pairs={{0,16},{8,24},{16,0},{24,8},{1,17},{9,25},{17,1},{25,9},{2,18},{10... | collective-permute-start | bytes 6152 | tf_op jit(solution)/shard_map/ppermute | solution.py:58
  69.2 7.9 %collective-permute-start.12 = (f32[1,4,128]{2,1,0:T(4,128)S(1)}, f32[1,4,128]{2,1,0:T(4,128)S(1)}, u32[]{:S(2)}, u32[]{:S(2)}) collective-permute-start(f32[1,4,128]{2,1,0:T(4,128)S(1)} %broadcast_in_dim.39), channel_id=1, source_target_pairs={{0,24},{8,16},{16,8},{24,0},{1,25},{9,17},{17,9},{25,1},{2,26},{10... | collective-permute-start | bytes 6152 | tf_op jit(solution)/shard_map/ppermute | solution.py:58
  71.8 5.3 %collective-permute-start.10 = (f32[1,4,128]{2,1,0:T(4,128)S(1)}, f32[1,4,128]{2,1,0:T(4,128)S(1)}, u32[]{:S(2)}, u32[]{:S(2)}) collective-permute-start(f32[1,4,128]{2,1,0:T(4,128)S(1)} %broadcast_in_dim.39), channel_id=1, source_target_pairs={{0,8},{8,0},{16,24},{24,16},{1,9},{9,1},{17,25},{25,17},{2,10},{10... | collective-permute-start | bytes 6152 | tf_op jit(solution)/shard_map/ppermute | solution.py:58
  71.9 6.1 %collective-permute-start.13 = (f32[1,3,1,4096]{3,2,1,0:T(1,128)S(1)}, f32[1,3,1,4096]{3,2,1,0:T(1,128)S(1)}, u32[]{:S(2)}, u32[]{:S(2)}) collective-permute-start(f32[1,3,1,4096]{3,2,1,0:T(1,128)S(1)} %get-tuple-element.156), channel_id=1, source_target_pairs={{0,8},{8,16},{16,24},{1,9},{9,17},{17,25},{2,10},{10,18},{18,26},{... | collective-permute-start | bytes 147464 | tf_op jit(solution)/shard_map/ppermute | solution.py:247
  75.8 6.0 %collective-permute-start.14 = (f32[1,3,1,4096]{3,2,1,0:T(1,128)S(1)}, f32[1,3,1,4096]{3,2,1,0:T(1,128)S(1)}, u32[]{:S(2)}, u32[]{:S(2)}) collective-permute-start(f32[1,3,1,4096]{3,2,1,0:T(1,128)S(1)} %get-tuple-element.157), channel_id=1, source_target_pairs={{8,0},{16,8},{24,16},{9,1},{17,9},{25,17},{10,2},{18,10},{26,18},{... | collective-permute-start | bytes 147464 | tf_op jit(solution)/shard_map/ppermute | solution.py:248
  86.4 8.0 %collective-permute-start.16 = (f32[1,4,128]{2,1,0:T(4,128)S(1)}, f32[1,4,128]{2,1,0:T(4,128)S(1)}, u32[]{:S(2)}, u32[]{:S(2)}) collective-permute-start(f32[1,4,128]{2,1,0:T(4,128)S(1)} %broadcast_in_dim.41), channel_id=1, source_target_pairs={{0,16},{8,24},{16,0},{24,8},{1,17},{9,25},{17,1},{25,9},{2,18},{10... | collective-permute-start | bytes 6152 | tf_op jit(solution)/shard_map/ppermute | solution.py:58
  86.5 7.9 %collective-permute-start.17 = (f32[1,4,128]{2,1,0:T(4,128)S(1)}, f32[1,4,128]{2,1,0:T(4,128)S(1)}, u32[]{:S(2)}, u32[]{:S(2)}) collective-permute-start(f32[1,4,128]{2,1,0:T(4,128)S(1)} %broadcast_in_dim.41), channel_id=1, source_target_pairs={{0,24},{8,16},{16,8},{24,0},{1,25},{9,17},{17,9},{25,1},{2,26},{10... | collective-permute-start | bytes 6152 | tf_op jit(solution)/shard_map/ppermute | solution.py:58
  89.1 5.3 %collective-permute-start.15 = (f32[1,4,128]{2,1,0:T(4,128)S(1)}, f32[1,4,128]{2,1,0:T(4,128)S(1)}, u32[]{:S(2)}, u32[]{:S(2)}) collective-permute-start(f32[1,4,128]{2,1,0:T(4,128)S(1)} %broadcast_in_dim.41), channel_id=1, source_target_pairs={{0,8},{8,0},{16,24},{24,16},{1,9},{9,1},{17,25},{25,17},{2,10},{10... | collective-permute-start | bytes 6152 | tf_op jit(solution)/shard_map/ppermute | solution.py:58
  90.0 5.3 %collective-permute-start.18 = (f32[1,3,1,4096]{3,2,1,0:T(1,128)S(1)}, f32[1,3,1,4096]{3,2,1,0:T(1,128)S(1)}, u32[]{:S(2)}, u32[]{:S(2)}) collective-permute-start(f32[1,3,1,4096]{3,2,1,0:T(1,128)S(1)} %get-tuple-element.150), channel_id=1, source_target_pairs={{0,8},{8,16},{16,24},{1,9},{9,17},{17,25},{2,10},{10,18},{18,26},{... | collective-permute-start | bytes 147464 | tf_op jit(solution)/shard_map/ppermute | solution.py:247
  93.1 6.0 %collective-permute-start.19 = (f32[1,3,1,4096]{3,2,1,0:T(1,128)S(1)}, f32[1,3,1,4096]{3,2,1,0:T(1,128)S(1)}, u32[]{:S(2)}, u32[]{:S(2)}) collective-permute-start(f32[1,3,1,4096]{3,2,1,0:T(1,128)S(1)} %get-tuple-element.151), channel_id=1, source_target_pairs={{8,0},{16,8},{24,16},{9,1},{17,9},{25,17},{10,2},{18,10},{26,18},{... | collective-permute-start | bytes 147464 | tf_op jit(solution)/shard_map/ppermute | solution.py:248
  103.8 8.0 %collective-permute-start.21 = (f32[1,4,128]{2,1,0:T(4,128)S(1)}, f32[1,4,128]{2,1,0:T(4,128)S(1)}, u32[]{:S(2)}, u32[]{:S(2)}) collective-permute-start(f32[1,4,128]{2,1,0:T(4,128)S(1)} %broadcast_in_dim.43), channel_id=1, source_target_pairs={{0,16},{8,24},{16,0},{24,8},{1,17},{9,25},{17,1},{25,9},{2,18},{10... | collective-permute-start | bytes 6152 | tf_op jit(solution)/shard_map/ppermute | solution.py:58
  104.7 7.2 %collective-permute-start.22 = (f32[1,4,128]{2,1,0:T(4,128)S(1)}, f32[1,4,128]{2,1,0:T(4,128)S(1)}, u32[]{:S(2)}, u32[]{:S(2)}) collective-permute-start(f32[1,4,128]{2,1,0:T(4,128)S(1)} %broadcast_in_dim.43), channel_id=1, source_target_pairs={{0,24},{8,16},{16,8},{24,0},{1,25},{9,17},{17,9},{25,1},{2,26},{10... | collective-permute-start | bytes 6152 | tf_op jit(solution)/shard_map/ppermute | solution.py:58
  106.5 5.3 %collective-permute-start.20 = (f32[1,4,128]{2,1,0:T(4,128)S(1)}, f32[1,4,128]{2,1,0:T(4,128)S(1)}, u32[]{:S(2)}, u32[]{:S(2)}) collective-permute-start(f32[1,4,128]{2,1,0:T(4,128)S(1)} %broadcast_in_dim.43), channel_id=1, source_target_pairs={{0,8},{8,0},{16,24},{24,16},{1,9},{9,1},{17,25},{25,17},{2,10},{10... | collective-permute-start | bytes 6152 | tf_op jit(solution)/shard_map/ppermute | solution.py:58
  107.4 5.3 %collective-permute-start.23 = (f32[1,3,1,4096]{3,2,1,0:T(1,128)S(1)}, f32[1,3,1,4096]{3,2,1,0:T(1,128)S(1)}, u32[]{:S(2)}, u32[]{:S(2)}) collective-permute-start(f32[1,3,1,4096]{3,2,1,0:T(1,128)S(1)} %get-tuple-element.144), channel_id=1, source_target_pairs={{0,8},{8,16},{16,24},{1,9},{9,17},{17,25},{2,10},{10,18},{18,26},{... | collective-permute-start | bytes 147464 | tf_op jit(solution)/shard_map/ppermute | solution.py:247
  110.5 6.0 %collective-permute-start.24 = (f32[1,3,1,4096]{3,2,1,0:T(1,128)S(1)}, f32[1,3,1,4096]{3,2,1,0:T(1,128)S(1)}, u32[]{:S(2)}, u32[]{:S(2)}) collective-permute-start(f32[1,3,1,4096]{3,2,1,0:T(1,128)S(1)} %get-tuple-element.145), channel_id=1, source_target_pairs={{8,0},{16,8},{24,16},{9,1},{17,9},{25,17},{10,2},{18,10},{26,18},{... | collective-permute-start | bytes 147464 | tf_op jit(solution)/shard_map/ppermute | solution.py:248
  121.0 8.8 %collective-permute-start.26 = (f32[1,4,128]{2,1,0:T(4,128)S(1)}, f32[1,4,128]{2,1,0:T(4,128)S(1)}, u32[]{:S(2)}, u32[]{:S(2)}) collective-permute-start(f32[1,4,128]{2,1,0:T(4,128)S(1)} %broadcast_in_dim.45), channel_id=1, source_target_pairs={{0,16},{8,24},{16,0},{24,8},{1,17},{9,25},{17,1},{25,9},{2,18},{10... | collective-permute-start | bytes 6152 | tf_op jit(solution)/shard_map/ppermute | solution.py:58
  121.8 7.9 %collective-permute-start.27 = (f32[1,4,128]{2,1,0:T(4,128)S(1)}, f32[1,4,128]{2,1,0:T(4,128)S(1)}, u32[]{:S(2)}, u32[]{:S(2)}) collective-permute-start(f32[1,4,128]{2,1,0:T(4,128)S(1)} %broadcast_in_dim.45), channel_id=1, source_target_pairs={{0,24},{8,16},{16,8},{24,0},{1,25},{9,17},{17,9},{25,1},{2,26},{10... | collective-permute-start | bytes 6152 | tf_op jit(solution)/shard_map/ppermute | solution.py:58
  124.4 5.3 %collective-permute-start.25 = (f32[1,4,128]{2,1,0:T(4,128)S(1)}, f32[1,4,128]{2,1,0:T(4,128)S(1)}, u32[]{:S(2)}, u32[]{:S(2)}) collective-permute-start(f32[1,4,128]{2,1,0:T(4,128)S(1)} %broadcast_in_dim.45), channel_id=1, source_target_pairs={{0,8},{8,0},{16,24},{24,16},{1,9},{9,1},{17,25},{25,17},{2,10},{10... | collective-permute-start | bytes 6152 | tf_op jit(solution)/shard_map/ppermute | solution.py:58
  124.5 6.1 %collective-permute-start.28 = (f32[1,3,1,4096]{3,2,1,0:T(1,128)S(1)}, f32[1,3,1,4096]{3,2,1,0:T(1,128)S(1)}, u32[]{:S(2)}, u32[]{:S(2)}) collective-permute-start(f32[1,3,1,4096]{3,2,1,0:T(1,128)S(1)} %get-tuple-element.138), channel_id=1, source_target_pairs={{0,8},{8,16},{16,24},{1,9},{9,17},{17,25},{2,10},{10,18},{18,26},{... | collective-permute-start | bytes 147464 | tf_op jit(solution)/shard_map/ppermute | solution.py:247
  128.4 6.0 %collective-permute-start.29 = (f32[1,3,1,4096]{3,2,1,0:T(1,128)S(1)}, f32[1,3,1,4096]{3,2,1,0:T(1,128)S(1)}, u32[]{:S(2)}, u32[]{:S(2)}) collective-permute-start(f32[1,3,1,4096]{3,2,1,0:T(1,128)S(1)} %get-tuple-element.139), channel_id=1, source_target_pairs={{8,0},{16,8},{24,16},{9,1},{17,9},{25,17},{10,2},{18,10},{26,18},{... | collective-permute-start | bytes 147464 | tf_op jit(solution)/shard_map/ppermute | solution.py:248
  138.9 8.0 %collective-permute-start.31 = (f32[1,4,128]{2,1,0:T(4,128)S(1)}, f32[1,4,128]{2,1,0:T(4,128)S(1)}, u32[]{:S(2)}, u32[]{:S(2)}) collective-permute-start(f32[1,4,128]{2,1,0:T(4,128)S(1)} %broadcast_in_dim.47), channel_id=1, source_target_pairs={{0,16},{8,24},{16,0},{24,8},{1,17},{9,25},{17,1},{25,9},{2,18},{10... | collective-permute-start | bytes 6152 | tf_op jit(solution)/shard_map/ppermute | solution.py:58
  139.0 7.9 %collective-permute-start.32 = (f32[1,4,128]{2,1,0:T(4,128)S(1)}, f32[1,4,128]{2,1,0:T(4,128)S(1)}, u32[]{:S(2)}, u32[]{:S(2)}) collective-permute-start(f32[1,4,128]{2,1,0:T(4,128)S(1)} %broadcast_in_dim.47), channel_id=1, source_target_pairs={{0,24},{8,16},{16,8},{24,0},{1,25},{9,17},{17,9},{25,1},{2,26},{10... | collective-permute-start | bytes 6152 | tf_op jit(solution)/shard_map/ppermute | solution.py:58
  141.6 5.3 %collective-permute-start.30 = (f32[1,4,128]{2,1,0:T(4,128)S(1)}, f32[1,4,128]{2,1,0:T(4,128)S(1)}, u32[]{:S(2)}, u32[]{:S(2)}) collective-permute-start(f32[1,4,128]{2,1,0:T(4,128)S(1)} %broadcast_in_dim.47), channel_id=1, source_target_pairs={{0,8},{8,0},{16,24},{24,16},{1,9},{9,1},{17,25},{25,17},{2,10},{10... | collective-permute-start | bytes 6152 | tf_op jit(solution)/shard_map/ppermute | solution.py:58
  142.5 5.3 %collective-permute-start.33 = (f32[1,3,1,4096]{3,2,1,0:T(1,128)S(1)}, f32[1,3,1,4096]{3,2,1,0:T(1,128)S(1)}, u32[]{:S(2)}, u32[]{:S(2)}) collective-permute-start(f32[1,3,1,4096]{3,2,1,0:T(1,128)S(1)} %get-tuple-element.132), channel_id=1, source_target_pairs={{0,8},{8,16},{16,24},{1,9},{9,17},{17,25},{2,10},{10,18},{18,26},{... | collective-permute-start | bytes 147464 | tf_op jit(solution)/shard_map/ppermute | solution.py:247
  145.7 6.0 %collective-permute-start.34 = (f32[1,3,1,4096]{3,2,1,0:T(1,128)S(1)}, f32[1,3,1,4096]{3,2,1,0:T(1,128)S(1)}, u32[]{:S(2)}, u32[]{:S(2)}) collective-permute-start(f32[1,3,1,4096]{3,2,1,0:T(1,128)S(1)} %get-tuple-element.133), channel_id=1, source_target_pairs={{8,0},{16,8},{24,16},{9,1},{17,9},{25,17},{10,2},{18,10},{26,18},{... | collective-permute-start | bytes 147464 | tf_op jit(solution)/shard_map/ppermute | solution.py:248
  156.1 8.2 %collective-permute-start.36 = (f32[1,4,128]{2,1,0:T(4,128)S(1)}, f32[1,4,128]{2,1,0:T(4,128)S(1)}, u32[]{:S(2)}, u32[]{:S(2)}) collective-permute-start(f32[1,4,128]{2,1,0:T(4,128)S(1)} %broadcast_in_dim.49), channel_id=1, source_target_pairs={{0,16},{8,24},{16,0},{24,8},{1,17},{9,25},{17,1},{25,9},{2,18},{10... | collective-permute-start | bytes 6152 | tf_op jit(solution)/shard_map/ppermute | solution.py:58
  156.9 7.4 %collective-permute-start.37 = (f32[1,4,128]{2,1,0:T(4,128)S(1)}, f32[1,4,128]{2,1,0:T(4,128)S(1)}, u32[]{:S(2)}, u32[]{:S(2)}) collective-permute-start(f32[1,4,128]{2,1,0:T(4,128)S(1)} %broadcast_in_dim.49), channel_id=1, source_target_pairs={{0,24},{8,16},{16,8},{24,0},{1,25},{9,17},{17,9},{25,1},{2,26},{10... | collective-permute-start | bytes 6152 | tf_op jit(solution)/shard_map/ppermute | solution.py:58
  158.8 5.6 %collective-permute-start.35 = (f32[1,4,128]{2,1,0:T(4,128)S(1)}, f32[1,4,128]{2,1,0:T(4,128)S(1)}, u32[]{:S(2)}, u32[]{:S(2)}) collective-permute-start(f32[1,4,128]{2,1,0:T(4,128)S(1)} %broadcast_in_dim.49), channel_id=1, source_target_pairs={{0,8},{8,0},{16,24},{24,16},{1,9},{9,1},{17,25},{25,17},{2,10},{10... | collective-permute-start | bytes 6152 | tf_op jit(solution)/shard_map/ppermute | solution.py:58
  159.6 8.1 %collective-permute-start.38 = (f32[1,3,1,4096]{3,2,1,0:T(1,128)S(1)}, f32[1,3,1,4096]{3,2,1,0:T(1,128)S(1)}, u32[]{:S(2)}, u32[]{:S(2)}) collective-permute-start(f32[1,3,1,4096]{3,2,1,0:T(1,128)S(1)} %get-tuple-element.130), channel_id=1, source_target_pairs={{0,8},{8,16},{16,24},{1,9},{9,17},{17,25},{2,10},{10,18},{18,26},{... | collective-permute-start | bytes 147464 | tf_op jit(solution)/shard_map/ppermute | solution.py:247
  163.0 6.0 %collective-permute-start.39 = (f32[1,3,1,4096]{3,2,1,0:T(1,128)S(1)}, f32[1,3,1,4096]{3,2,1,0:T(1,128)S(1)}, u32[]{:S(2)}, u32[]{:S(2)}) collective-permute-start(f32[1,3,1,4096]{3,2,1,0:T(1,128)S(1)} %get-tuple-element.131), channel_id=1, source_target_pairs={{8,0},{16,8},{24,16},{9,1},{17,9},{25,17},{10,2},{18,10},{26,18},{... | collective-permute-start | bytes 147464 | tf_op jit(solution)/shard_map/ppermute | solution.py:248
  185.4 4.9 %collective-permute-start.42 = (f32[1,23]{1,0:T(1,128)S(1)}, f32[1,23]{1,0:T(1,128)S(1)}, u32[]{:S(2)}, u32[]{:S(2)}) collective-permute-start(f32[1,23]{1,0:T(1,128)S(1)} %stack.256), channel_id=1, source_target_pairs={{0,24},{8,16},{16,8},{24,0},{1,25},{9,17},{17,9},{25,1},{2,26},{10... | collective-permute-start | bytes 284 | tf_op jit(solution)/shard_map/ppermute | solution.py:58
  186.2 5.1 %collective-permute-start.41 = (f32[1,23]{1,0:T(1,128)S(1)}, f32[1,23]{1,0:T(1,128)S(1)}, u32[]{:S(2)}, u32[]{:S(2)}) collective-permute-start(f32[1,23]{1,0:T(1,128)S(1)} %stack.256), channel_id=1, source_target_pairs={{0,16},{8,24},{16,0},{24,8},{1,17},{9,25},{17,1},{25,9},{2,18},{10... | collective-permute-start | bytes 284 | tf_op jit(solution)/shard_map/ppermute | solution.py:58
  188.9 3.6 %collective-permute-start.40 = (f32[1,23]{1,0:T(1,128)S(1)}, f32[1,23]{1,0:T(1,128)S(1)}, u32[]{:S(2)}, u32[]{:S(2)}) collective-permute-start(f32[1,23]{1,0:T(1,128)S(1)} %stack.256), channel_id=1, source_target_pairs={{0,8},{8,0},{16,24},{24,16},{1,9},{9,1},{17,25},{25,17},{2,10},{10... | collective-permute-start | bytes 284 | tf_op jit(solution)/shard_map/ppermute | solution.py:58
  196.6 5.4 %collective-permute-start.43 = (f32[8,6]{1,0:T(8,128)S(1)}, f32[8,6]{1,0:T(8,128)S(1)}, u32[]{:S(2)}, u32[]{:S(2)}) collective-permute-start(f32[8,6]{1,0:T(8,128)S(1)} %broadcast_multiply_fusion), channel_id=1, source_target_pairs={{0,1},{1,0},{2,3},{3,2},{4,5},{5,4},{6,7},{7,6},{8,9},{9,8},{10,11... | collective-permute-start | bytes 584 | tf_op jit(solution)/shard_map/ppermute | solution.py:58
  198.4 27.2 %all-to-all-start.1 = ((f32[1,3,16,4096]{3,0,1,2:T(1,128)}), f32[1,3,16,4096]{3,0,1,2:T(1,128)S(1)}, u32[]{:S(2)}, u32[]{:S(2)}) async-start(f32[1,3,16,4096]{3,0,1,2:T(1,128)} %copy.51), calls=%async_computation.1 | async-start | bytes 1572864 | tf_op jit(solution)/shard_map/all_to_all | solution.py:322
  202.1 9.9 %collective-permute-start.46 = (f32[8,6]{1,0:T(8,128)S(1)}, f32[8,6]{1,0:T(8,128)S(1)}, u32[]{:S(2)}, u32[]{:S(2)}) collective-permute-start(f32[8,6]{1,0:T(8,128)S(1)} %fusion.111), channel_id=1, source_target_pairs={{0,6},{1,7},{2,4},{3,5},{4,2},{5,3},{6,0},{7,1},{8,14},{9,15},{10,... | collective-permute-start | bytes 584 | tf_op jit(solution)/shard_map/ppermute | solution.py:58
  205.2 9.9 %collective-permute-start.45 = (f32[8,6]{1,0:T(8,128)S(1)}, f32[8,6]{1,0:T(8,128)S(1)}, u32[]{:S(2)}, u32[]{:S(2)}) collective-permute-start(f32[8,6]{1,0:T(8,128)S(1)} %fusion.111), channel_id=1, source_target_pairs={{0,4},{1,5},{2,6},{3,7},{4,0},{5,1},{6,2},{7,3},{8,12},{9,13},{10,... | collective-permute-start | bytes 584 | tf_op jit(solution)/shard_map/ppermute | solution.py:58
  206.1 9.1 %collective-permute-start.44 = (f32[8,6]{1,0:T(8,128)S(1)}, f32[8,6]{1,0:T(8,128)S(1)}, u32[]{:S(2)}, u32[]{:S(2)}) collective-permute-start(f32[8,6]{1,0:T(8,128)S(1)} %fusion.111), channel_id=1, source_target_pairs={{0,2},{1,3},{2,0},{3,1},{4,6},{5,7},{6,4},{7,5},{8,10},{9,11},{10,... | collective-permute-start | bytes 584 | tf_op jit(solution)/shard_map/ppermute | solution.py:58
  215.5 4.3 %collective-permute-start.47 = (f32[4,6]{0,1:T(8,128)S(1)}, f32[4,6]{0,1:T(8,128)S(1)}, u32[]{:S(2)}, u32[]{:S(2)}) collective-permute-start(f32[4,6]{0,1:T(8,128)S(1)} %get-tuple-element.202), channel_id=1, source_target_pairs={{0,32},{32,0},{64,96},{96,64},{1,33},{33,1},{65,97},{97,65},{2,34}... | collective-permute-start | bytes 296 | tf_op jit(solution)/shard_map/ppermute | solution.py:83
  217.2 4.8 %collective-permute-start.49 = (f32[4,6]{0,1:T(8,128)S(1)}, f32[4,6]{0,1:T(8,128)S(1)}, u32[]{:S(2)}, u32[]{:S(2)}) collective-permute-start(f32[4,6]{0,1:T(8,128)S(1)} %get-tuple-element.203), channel_id=1, source_target_pairs={{0,96},{32,64},{64,32},{96,0},{1,97},{33,65},{65,33},{97,1},{2,98}... | collective-permute-start | bytes 296 | tf_op jit(solution)/shard_map/ppermute | solution.py:83
  219.7 5.1 %collective-permute-start.48 = (f32[4,6]{0,1:T(8,128)S(1)}, f32[4,6]{0,1:T(8,128)S(1)}, u32[]{:S(2)}, u32[]{:S(2)}) collective-permute-start(f32[4,6]{0,1:T(8,128)S(1)} %get-tuple-element.204), channel_id=1, source_target_pairs={{0,64},{32,96},{64,0},{96,32},{1,65},{33,97},{65,1},{97,33},{2,66}... | collective-permute-start | bytes 296 | tf_op jit(solution)/shard_map/ppermute | solution.py:83

commit v4 on v3

--- a/solution.py
+++ b/solution.py
@@ -147,20 +147,6 @@
     upper_mask = (column != RES - 1).astype(jnp.float32)
     lower_mask = (column != 0).astype(jnp.float32)
     table = jnp.concatenate([grain_modulus[None, :], slip_softening.T], 0)
-
-    def stiff_one(inputs):
-        codes, grain_cells = inputs
-        flat_codes = codes.reshape(-1)
-        flat_grains = grain_cells.reshape(-1)
-        onehot = (jnp.arange(GRAINS)[:, None] == flat_grains[None, :]).astype(jnp.float32)
-        looked = jnp.dot(
-            table, onehot, precision=lax.Precision.HIGHEST, preferred_element_type=jnp.float32
-        )
-        softening = jnp.zeros(flat_codes.shape, jnp.float32)
-        for slip in range(SLIPS):
-            active = (flat_codes // 2**slip % 2).astype(jnp.float32)
-            softening = softening + active * looked[1 + slip]
-        return (looked[0] / (1.0 + softening)).reshape(codes.shape)
 
     spot_onehot = (rve_spot[:, None] == jnp.arange(spot_count)[None, :]).astype(jnp.float32)
     parts, hot_me = axis_gather(macro_adjoint, "hot")

time: 228 us -> 228 us (level)
  no operation moved by 1% of the time
where the time goes in v4:
time: 228 us; the launch traced here: 227 us
  starting transfers between devices  89.5 us (39%)
  waiting for transfers between devices  47.4 us (21%)
  other arithmetic  39.7 us (17%)
  local copies, waits for them, and re-layouts  27.8 us (12%)
  Pallas kernels  15 us (7%)
  between operations  7.35 us (3%)
    ppermute x28, starting transfers between devices, axis_sum(): vals[o] = lax.ppermute(value, axis, [(i, i ^ mask) for i in range(size)])  34 us
    ppermute x7, starting transfers between devices, boundary_planes(): before = lax.ppermute(value[:, :, -1:], 'yb', up)  24.5 us
    ppermute x7, waiting for transfers between devices, boundary_planes(): after = lax.ppermute(value[:, :, :1], 'yb', down)  24.2 us
    broadcast_in_dim x7, other arithmetic, shards(): jnp.broadcast_to(local[:, :, None], local.shape + (128,))  17.3 us
    pallas_call x1, Pallas kernels, stiffness(): pl.pallas_call(stiffness_kernel, grid=(rves,), in_specs=[pl.BlockSpec(pie...  15 us
    another operation x1, local copies, waits for them, and re-layouts, shards(): local = jnp.stack(terms, -1)  14.5 us
    reduce_sum x8, other arithmetic, local_dot(): return jnp.sum(first * second, axis=(1, 2, 3))  12.3 us
    ppermute x28, waiting for transfers between devices, axis_sum(): vals[o] = lax.ppermute(value, axis, [(i, i ^ mask) for i in range(size)])  11.9 us
  transfers between devices with their start and end apart: 52, of which 16 were waited for; matrix products, arithmetic and copies ran while one was open for 7% of the time, Pallas kernels for 7%

profile of v4, /device:TPU:0, one launch (start us, length us, event | category | flops | bytes accessed | tf_op | source)
XLA Modules:
  0.0 227.1 jit_solution(6325243595513324504)
XLA Ops:
  0.7 4.1 %collective-permute-start.3 = (f32[4,6]{1,0:T(4,128)}, f32[4,6]{1,0:T(4,128)S(1)}, u32[]{:S(2)}, u32[]{:S(2)}) collective-permute-start(f32[4,6]{1,0:T(4,128)} %param.10), channel_id=1, source_target_pairs={{0,64},{32,96},{64,0},{96,32},{1,65},{33,97},{65,1},{97,33},{2,66}... | collective-permute-start | bytes 296 | tf_op jit(solution)/shard_map/ppermute | solution.py:68
  7.1 15.0 %shard_map.95 = f32[8,2,4096]{2,1,0:T(2,128)} custom-call(bf16[3,16,64]{2,1,0:T(8,128)(2,1)} %fusion.95.pieces_ref, s32[8,2,4096]{2,1,0:T(2,128)} %codes_ref.1, s32[8,2,4096]{2,1,0:T(2,128)} %grains_ref.1), custom_call_target="tpu_custom_call" | custom-call | tf_op jit(solution)/shard_map/pallas_call | solution.py:122
  22.1 4.3 %all-to-all-start = ((f32[8,2,4096]{2,1,0:T(2,128)}), f32[8,2,4096]{2,1,0:T(2,128)S(1)}, u32[]{:S(2)}, u32[]{:S(2)}) async-start(f32[8,2,4096]{2,1,0:T(2,128)} %shard_map.95), calls=%async_computation | async-start | bytes 524288 | tf_op jit(solution)/shard_map/all_to_all | solution.py:172
  31.2 2.7 %all-to-all-done = f32[8,2,4096]{2,1,0:T(2,128)S(1)} async-done(((f32[8,2,4096]{2,1,0:T(2,128)}), f32[8,2,4096]{2,1,0:T(2,128)S(1)}, u32[]{:S(2)}, u32[]{:S(2)}) %all-to-all-start) | async-done | bytes 262176 | tf_op jit(solution)/shard_map/all_to_all | solution.py:172
  34.1 3.5 %collective-permute-start.1 = (f32[1,2,4096]{2,1,0:T(2,128)S(1)}, f32[1,2,4096]{2,1,0:T(2,128)S(1)}, u32[]{:S(2)}, u32[]{:S(2)}) collective-permute-start(f32[1,2,4096]{2,1,0:T(2,128)S(1)} %get-tuple-element.179), channel_id=1, source_target_pairs={{0,8},{8,16},{16,24},{1,9},{9,17},{17,25},{2,10},{10,18},{18,26},{... | collective-permute-start | bytes 98312 | tf_op jit(solution)/shard_map/ppermute | solution.py:24
  37.6 1.3 collective-permute-start
  39.9 3.5 %collective-permute-done = f32[1,2,4096]{2,1,0:T(2,128)S(1)} collective-permute-done((f32[1,2,4096]{2,1,0:T(2,128)S(1)}, f32[1,2,4096]{2,1,0:T(2,128)S(1)}, u32[]{:S(2)}, u32[]{:S(2)}) %collective-permute-start) | collective-permute-done | bytes 32800 | tf_op jit(solution)/shard_map/ppermute | solution.py:25
  45.6 1.5 multiply_reduce_fusion.29
  47.1 1.9 maximum_bitcast_fusion
  49.1 2.9 %collective-permute-start.6 = (f32[1,4,128]{2,1,0:T(4,128)S(1)}, f32[1,4,128]{2,1,0:T(4,128)S(1)}, u32[]{:S(2)}, u32[]{:S(2)}) collective-permute-start(f32[1,4,128]{2,1,0:T(4,128)S(1)} %broadcast_in_dim.37), channel_id=1, source_target_pairs={{0,16},{8,24},{16,0},{24,8},{1,17},{9,25},{17,1},{25,9},{2,18},{10... | collective-permute-start | bytes 6152 | tf_op jit(solution)/shard_map/ppermute | solution.py:58
  52.0 1.3 collective-permute-start.7
  53.5 3.9 %collective-permute-start.8 = (f32[1,3,1,4096]{3,2,1,0:T(1,128)S(1)}, f32[1,3,1,4096]{3,2,1,0:T(1,128)S(1)}, u32[]{:S(2)}, u32[]{:S(2)}) collective-permute-start(f32[1,3,1,4096]{3,2,1,0:T(1,128)S(1)} %get-tuple-element.162), channel_id=1, source_target_pairs={{0,8},{8,16},{16,24},{1,9},{9,17},{17,25},{2,10},{10,18},{18,26},{... | collective-permute-start | bytes 147464 | tf_op jit(solution)/shard_map/ppermute | solution.py:233
  57.4 1.3 collective-permute-start.9
  59.6 3.8 %collective-permute-done.9 = f32[1,3,1,4096]{3,2,1,0:T(1,128)S(1)} collective-permute-done((f32[1,3,1,4096]{3,2,1,0:T(1,128)S(1)}, f32[1,3,1,4096]{3,2,1,0:T(1,128)S(1)}, u32[]{:S(2)}, u32[]{:S(2)}) %collective-permute-start.9) | collective-permute-done | bytes 49184 | tf_op jit(solution)/shard_map/ppermute | solution.py:234
  63.7 1.5 multiply_reduce_fusion.27
  65.2 2.6 %maximum_bitcast_fusion.1 = f32[4]{0:T(128)S(1)} fusion(f32[1,1]{1,0:T(1,128)} %bitcast.32, f32[1,1]{1,0:T(1,128)} %bitcast.31, f32[1,1]{1,0:T(1,128)} %bitcast.30, f32[1,1]{1,0:T(1,128)} %bitcast.29), kind=kLoop, calls=%fused_computation.272 | loop fusion | flops 12 | bytes 32 | tf_op jit(solution)/shard_map/broadcast_in_dim | solution.py:279
  67.9 1.3 collective-permute-start.11
  69.2 2.6 %collective-permute-start.12 = (f32[1,4,128]{2,1,0:T(4,128)S(1)}, f32[1,4,128]{2,1,0:T(4,128)S(1)}, u32[]{:S(2)}, u32[]{:S(2)}) collective-permute-start(f32[1,4,128]{2,1,0:T(4,128)S(1)} %broadcast_in_dim.39), channel_id=1, source_target_pairs={{0,24},{8,16},{16,8},{24,0},{1,25},{9,17},{17,9},{25,1},{2,26},{10... | collective-permute-start | bytes 6152 | tf_op jit(solution)/shard_map/ppermute | solution.py:58
  71.9 3.9 %collective-permute-start.13 = (f32[1,3,1,4096]{3,2,1,0:T(1,128)S(1)}, f32[1,3,1,4096]{3,2,1,0:T(1,128)S(1)}, u32[]{:S(2)}, u32[]{:S(2)}) collective-permute-start(f32[1,3,1,4096]{3,2,1,0:T(1,128)S(1)} %get-tuple-element.156), channel_id=1, source_target_pairs={{0,8},{8,16},{16,24},{1,9},{9,17},{17,25},{2,10},{10,18},{18,26},{... | collective-permute-start | bytes 147464 | tf_op jit(solution)/shard_map/ppermute | solution.py:233
  75.8 1.3 collective-permute-start.14
  78.0 3.8 %collective-permute-done.14 = f32[1,3,1,4096]{3,2,1,0:T(1,128)S(1)} collective-permute-done((f32[1,3,1,4096]{3,2,1,0:T(1,128)S(1)}, f32[1,3,1,4096]{3,2,1,0:T(1,128)S(1)}, u32[]{:S(2)}, u32[]{:S(2)}) %collective-permute-start.14) | collective-permute-done | bytes 49184 | tf_op jit(solution)/shard_map/ppermute | solution.py:234
  82.3 1.5 multiply_reduce_fusion.23
  83.8 2.6 %maximum_bitcast_fusion.2 = f32[4]{0:T(128)S(1)} fusion(f32[1,1]{1,0:T(1,128)} %bitcast.43, f32[1,1]{1,0:T(1,128)} %bitcast.42, f32[1,1]{1,0:T(1,128)} %bitcast.41, f32[1,1]{1,0:T(1,128)} %bitcast.40), kind=kLoop, calls=%fused_computation.273 | loop fusion | flops 12 | bytes 32 | tf_op jit(solution)/shard_map/broadcast_in_dim | solution.py:279
  86.5 2.6 %collective-permute-start.17 = (f32[1,4,128]{2,1,0:T(4,128)S(1)}, f32[1,4,128]{2,1,0:T(4,128)S(1)}, u32[]{:S(2)}, u32[]{:S(2)}) collective-permute-start(f32[1,4,128]{2,1,0:T(4,128)S(1)} %broadcast_in_dim.41), channel_id=1, source_target_pairs={{0,24},{8,16},{16,8},{24,0},{1,25},{9,17},{17,9},{25,1},{2,26},{10... | collective-permute-start | bytes 6152 | tf_op jit(solution)/shard_map/ppermute | solution.py:58
  90.0 3.1 %collective-permute-start.18 = (f32[1,3,1,4096]{3,2,1,0:T(1,128)S(1)}, f32[1,3,1,4096]{3,2,1,0:T(1,128)S(1)}, u32[]{:S(2)}, u32[]{:S(2)}) collective-permute-start(f32[1,3,1,4096]{3,2,1,0:T(1,128)S(1)} %get-tuple-element.150), channel_id=1, source_target_pairs={{0,8},{8,16},{16,24},{1,9},{9,17},{17,25},{2,10},{10,18},{18,26},{... | collective-permute-start | bytes 147464 | tf_op jit(solution)/shard_map/ppermute | solution.py:233
  93.1 1.3 collective-permute-start.19
  95.3 3.8 %collective-permute-done.19 = f32[1,3,1,4096]{3,2,1,0:T(1,128)S(1)} collective-permute-done((f32[1,3,1,4096]{3,2,1,0:T(1,128)S(1)}, f32[1,3,1,4096]{3,2,1,0:T(1,128)S(1)}, u32[]{:S(2)}, u32[]{:S(2)}) %collective-permute-start.19) | collective-permute-done | bytes 49184 | tf_op jit(solution)/shard_map/ppermute | solution.py:234
  99.7 1.5 multiply_reduce_fusion.19
  101.2 2.6 %maximum_bitcast_fusion.3 = f32[4]{0:T(128)S(1)} fusion(f32[1,1]{1,0:T(1,128)} %bitcast.54, f32[1,1]{1,0:T(1,128)} %bitcast.53, f32[1,1]{1,0:T(1,128)} %bitcast.52, f32[1,1]{1,0:T(1,128)} %bitcast.51), kind=kLoop, calls=%fused_computation.274 | loop fusion | flops 12 | bytes 32 | tf_op jit(solution)/shard_map/broadcast_in_dim | solution.py:279
  104.7 1.8 collective-permute-start.22
  107.4 3.1 %collective-permute-start.23 = (f32[1,3,1,4096]{3,2,1,0:T(1,128)S(1)}, f32[1,3,1,4096]{3,2,1,0:T(1,128)S(1)}, u32[]{:S(2)}, u32[]{:S(2)}) collective-permute-start(f32[1,3,1,4096]{3,2,1,0:T(1,128)S(1)} %get-tuple-element.144), channel_id=1, source_target_pairs={{0,8},{8,16},{16,24},{1,9},{9,17},{17,25},{2,10},{10,18},{18,26},{... | collective-permute-start | bytes 147464 | tf_op jit(solution)/shard_map/ppermute | solution.py:233
  110.5 1.3 collective-permute-start.24
  112.7 3.8 %collective-permute-done.24 = f32[1,3,1,4096]{3,2,1,0:T(1,128)S(1)} collective-permute-done((f32[1,3,1,4096]{3,2,1,0:T(1,128)S(1)}, f32[1,3,1,4096]{3,2,1,0:T(1,128)S(1)}, u32[]{:S(2)}, u32[]{:S(2)}) %collective-permute-start.24) | collective-permute-done | bytes 49184 | tf_op jit(solution)/shard_map/ppermute | solution.py:234
  116.8 1.5 multiply_reduce_fusion.15
  118.3 2.6 %maximum_bitcast_fusion.4 = f32[4]{0:T(128)S(1)} fusion(f32[1,1]{1,0:T(1,128)} %bitcast.65, f32[1,1]{1,0:T(1,128)} %bitcast.64, f32[1,1]{1,0:T(1,128)} %bitcast.63, f32[1,1]{1,0:T(1,128)} %bitcast.62), kind=kLoop, calls=%fused_computation.275 | loop fusion | flops 12 | bytes 32 | tf_op jit(solution)/shard_map/broadcast_in_dim | solution.py:279
  121.8 2.6 %collective-permute-start.27 = (f32[1,4,128]{2,1,0:T(4,128)S(1)}, f32[1,4,128]{2,1,0:T(4,128)S(1)}, u32[]{:S(2)}, u32[]{:S(2)}) collective-permute-start(f32[1,4,128]{2,1,0:T(4,128)S(1)} %broadcast_in_dim.45), channel_id=1, source_target_pairs={{0,24},{8,16},{16,8},{24,0},{1,25},{9,17},{17,9},{25,1},{2,26},{10... | collective-permute-start | bytes 6152 | tf_op jit(solution)/shard_map/ppermute | solution.py:58
  124.5 3.9 %collective-permute-start.28 = (f32[1,3,1,4096]{3,2,1,0:T(1,128)S(1)}, f32[1,3,1,4096]{3,2,1,0:T(1,128)S(1)}, u32[]{:S(2)}, u32[]{:S(2)}) collective-permute-start(f32[1,3,1,4096]{3,2,1,0:T(1,128)S(1)} %get-tuple-element.138), channel_id=1, source_target_pairs={{0,8},{8,16},{16,24},{1,9},{9,17},{17,25},{2,10},{10,18},{18,26},{... | collective-permute-start | bytes 147464 | tf_op jit(solution)/shard_map/ppermute | solution.py:233
  128.4 1.3 collective-permute-start.29
  130.6 3.8 %collective-permute-done.29 = f32[1,3,1,4096]{3,2,1,0:T(1,128)S(1)} collective-permute-done((f32[1,3,1,4096]{3,2,1,0:T(1,128)S(1)}, f32[1,3,1,4096]{3,2,1,0:T(1,128)S(1)}, u32[]{:S(2)}, u32[]{:S(2)}) %collective-permute-start.29) | collective-permute-done | bytes 49184 | tf_op jit(solution)/shard_map/ppermute | solution.py:234
  134.8 1.5 multiply_reduce_fusion.11
  136.3 2.6 %maximum_bitcast_fusion.5 = f32[4]{0:T(128)S(1)} fusion(f32[1,1]{1,0:T(1,128)} %bitcast.76, f32[1,1]{1,0:T(1,128)} %bitcast.75, f32[1,1]{1,0:T(1,128)} %bitcast.74, f32[1,1]{1,0:T(1,128)} %bitcast.73), kind=kLoop, calls=%fused_computation.276 | loop fusion | flops 12 | bytes 32 | tf_op jit(solution)/shard_map/broadcast_in_dim | solution.py:279
  139.0 2.6 %collective-permute-start.32 = (f32[1,4,128]{2,1,0:T(4,128)S(1)}, f32[1,4,128]{2,1,0:T(4,128)S(1)}, u32[]{:S(2)}, u32[]{:S(2)}) collective-permute-start(f32[1,4,128]{2,1,0:T(4,128)S(1)} %broadcast_in_dim.47), channel_id=1, source_target_pairs={{0,24},{8,16},{16,8},{24,0},{1,25},{9,17},{17,9},{25,1},{2,26},{10... | collective-permute-start | bytes 6152 | tf_op jit(solution)/shard_map/ppermute | solution.py:58
  142.5 3.1 %collective-permute-start.33 = (f32[1,3,1,4096]{3,2,1,0:T(1,128)S(1)}, f32[1,3,1,4096]{3,2,1,0:T(1,128)S(1)}, u32[]{:S(2)}, u32[]{:S(2)}) collective-permute-start(f32[1,3,1,4096]{3,2,1,0:T(1,128)S(1)} %get-tuple-element.132), channel_id=1, source_target_pairs={{0,8},{8,16},{16,24},{1,9},{9,17},{17,25},{2,10},{10,18},{18,26},{... | collective-permute-start | bytes 147464 | tf_op jit(solution)/shard_map/ppermute | solution.py:233
  145.7 1.3 collective-permute-start.34
  147.8 3.8 %collective-permute-done.34 = f32[1,3,1,4096]{3,2,1,0:T(1,128)S(1)} collective-permute-done((f32[1,3,1,4096]{3,2,1,0:T(1,128)S(1)}, f32[1,3,1,4096]{3,2,1,0:T(1,128)S(1)}, u32[]{:S(2)}, u32[]{:S(2)}) %collective-permute-start.34) | collective-permute-done | bytes 49184 | tf_op jit(solution)/shard_map/ppermute | solution.py:234
  151.9 1.5 multiply_reduce_fusion.7
  153.4 2.6 %maximum_bitcast_fusion.6 = f32[4]{0:T(128)S(1)} fusion(f32[1,1]{1,0:T(1,128)} %bitcast.87, f32[1,1]{1,0:T(1,128)} %bitcast.86, f32[1,1]{1,0:T(1,128)} %bitcast.85, f32[1,1]{1,0:T(1,128)} %bitcast.84), kind=kLoop, calls=%fused_computation.277 | loop fusion | flops 12 | bytes 32 | tf_op jit(solution)/shard_map/broadcast_in_dim | solution.py:279
  156.9 1.8 collective-permute-start.37
  159.6 3.4 %collective-permute-start.38 = (f32[1,3,1,4096]{3,2,1,0:T(1,128)S(1)}, f32[1,3,1,4096]{3,2,1,0:T(1,128)S(1)}, u32[]{:S(2)}, u32[]{:S(2)}) collective-permute-start(f32[1,3,1,4096]{3,2,1,0:T(1,128)S(1)} %get-tuple-element.130), channel_id=1, source_target_pairs={{0,8},{8,16},{16,24},{1,9},{9,17},{17,25},{2,10},{10,18},{18,26},{... | collective-permute-start | bytes 147464 | tf_op jit(solution)/shard_map/ppermute | solution.py:233
  163.0 1.3 collective-permute-start.39
  167.7 1.3 collective-permute-done.39
  169.3 1.6 multiply_reduce_fusion
  170.9 14.5 %stack.256 = f32[1,23]{1,0:T(1,128)S(1)} concatenate(f32[1,1]{1,0:T(1,128)} %bitcast.95, f32[1,1]{1,0:T(1,128)} %bitcast.96, f32[1,1]{1,0:T(1,128)} %bitcast.97, f32[1,1]{1,0:T(1,128)} %bitcast.98, f32[1,1]{1,0:T(1,128)} %bitcast.100, f32[1,1]{1,0:T(1,128)} %bitcast.101, f32[1,1]{1,0:T(1,128)} %bitcast.102, f32[1,1]{1,0:T(1,128)} %bitcast.104, f32[1,1]{1,0:T(1,128)} %bitcast.105, ...), dimensions={1} | concatenate | bytes 184 | tf_op jit(solution)/shard_map/stack | solution.py:273
  186.2 2.7 %collective-permute-start.41 = (f32[1,23]{1,0:T(1,128)S(1)}, f32[1,23]{1,0:T(1,128)S(1)}, u32[]{:S(2)}, u32[]{:S(2)}) collective-permute-start(f32[1,23]{1,0:T(1,128)S(1)} %stack.256), channel_id=1, source_target_pairs={{0,16},{8,24},{16,0},{24,8},{1,17},{9,25},{17,1},{25,9},{2,18},{10... | collective-permute-start | bytes 284 | tf_op jit(solution)/shard_map/ppermute | solution.py:58
  196.7 1.7 copy.51
  198.4 3.5 %all-to-all-start.1 = ((f32[1,3,16,4096]{3,0,1,2:T(1,128)}), f32[1,3,16,4096]{3,0,1,2:T(1,128)S(1)}, u32[]{:S(2)}, u32[]{:S(2)}) async-start(f32[1,3,16,4096]{3,0,1,2:T(1,128)} %copy.51), calls=%async_computation.1 | async-start | bytes 1572864 | tf_op jit(solution)/shard_map/all_to_all | solution.py:308
  202.1 3.2 %collective-permute-start.46 = (f32[8,6]{1,0:T(8,128)S(1)}, f32[8,6]{1,0:T(8,128)S(1)}, u32[]{:S(2)}, u32[]{:S(2)}) collective-permute-start(f32[8,6]{1,0:T(8,128)S(1)} %fusion.111), channel_id=1, source_target_pairs={{0,6},{1,7},{2,4},{3,5},{4,2},{5,3},{6,0},{7,1},{8,14},{9,15},{10,... | collective-permute-start | bytes 584 | tf_op jit(solution)/shard_map/ppermute | solution.py:58
  206.2 5.8 %collective-permute-done.46 = f32[8,6]{1,0:T(8,128)S(1)} collective-permute-done((f32[8,6]{1,0:T(8,128)S(1)}, f32[8,6]{1,0:T(8,128)S(1)}, u32[]{:S(2)}, u32[]{:S(2)}) %collective-permute-start.46) | collective-permute-done | bytes 224 | tf_op jit(solution)/shard_map/ppermute | solution.py:58
  212.0 3.2 %collective-permute-done.45 = f32[8,6]{1,0:T(8,128)S(1)} collective-permute-done((f32[8,6]{1,0:T(8,128)S(1)}, f32[8,6]{1,0:T(8,128)S(1)}, u32[]{:S(2)}, u32[]{:S(2)}) %collective-permute-start.45) | collective-permute-done | bytes 224 | tf_op jit(solution)/shard_map/ppermute | solution.py:58
  215.5 1.7 collective-permute-start.47
  217.2 2.5 %collective-permute-start.49 = (f32[4,6]{0,1:T(8,128)S(1)}, f32[4,6]{0,1:T(8,128)S(1)}, u32[]{:S(2)}, u32[]{:S(2)}) collective-permute-start(f32[4,6]{0,1:T(8,128)S(1)} %get-tuple-element.203), channel_id=1, source_target_pairs={{0,96},{32,64},{64,32},{96,0},{1,97},{33,65},{65,33},{97,1},{2,98}... | collective-permute-start | bytes 296 | tf_op jit(solution)/shard_map/ppermute | solution.py:83
  219.7 2.3 %collective-permute-done.49 = f32[4,6]{0,1:T(8,128)S(1)} collective-permute-done((f32[4,6]{0,1:T(8,128)S(1)}, f32[4,6]{0,1:T(8,128)S(1)}, u32[]{:S(2)}, u32[]{:S(2)}) %collective-permute-start.49) | collective-permute-done | bytes 128 | tf_op jit(solution)/shard_map/ppermute | solution.py:83
  222.0 2.8 %collective-permute-done.48 = f32[4,6]{0,1:T(8,128)S(1)} collective-permute-done((f32[4,6]{0,1:T(8,128)S(1)}, f32[4,6]{0,1:T(8,128)S(1)}, u32[]{:S(2)}, u32[]{:S(2)}) %collective-permute-start.48) | collective-permute-done | bytes 128 | tf_op jit(solution)/shard_map/ppermute | solution.py:83
  225.7 1.5 copy.57
  (171 shorter events, 33.0 us)
Async XLA Ops:
  0.6 25.8 %copy-start.1 = (s32[6]{0:T(128)S(1)}, s32[6]{0:T(128)}, u32[]{:S(2)}) copy-start(s32[6]{0:T(128)} %constant.189) | copy-start | bytes 76
  0.6 25.8 %copy-start.2 = (s32[6]{0:T(128)S(1)}, s32[6]{0:T(128)}, u32[]{:S(2)}) copy-start(s32[6]{0:T(128)} %constant.188) | copy-start | bytes 76
  0.7 25.8 %copy-start = (f32[4,6]{1,0:T(4,128)S(1)}, f32[4,6]{1,0:T(4,128)}, u32[]{:S(2)}) copy-start(f32[4,6]{1,0:T(4,128)} %param.10) | copy-start | bytes 292
  0.7 25.8 %copy-start.3 = (s32[8]{0:T(128)S(1)}, s32[8]{0:T(128)}, u32[]{:S(2)}) copy-start(s32[8]{0:T(128)} %param.15) | copy-start | bytes 100
  0.7 25.8 %collective-permute-start.3 = (f32[4,6]{1,0:T(4,128)}, f32[4,6]{1,0:T(4,128)S(1)}, u32[]{:S(2)}, u32[]{:S(2)}) collective-permute-start(f32[4,6]{1,0:T(4,128)} %param.10), channel_id=1, source_target_pairs={{0,64},{32,96},{64,0},{96,32},{1,65},{33,97},{65,1},{97,33},{2,66}... | collective-permute-start | bytes 296 | tf_op jit(solution)/shard_map/ppermute | solution.py:68
  4.7 21.7 %collective-permute-start.2 = (f32[4,6]{1,0:T(4,128)}, f32[4,6]{1,0:T(4,128)S(1)}, u32[]{:S(2)}, u32[]{:S(2)}) collective-permute-start(f32[4,6]{1,0:T(4,128)} %param.10), channel_id=1, source_target_pairs={{0,96},{32,64},{64,32},{96,0},{1,97},{33,65},{65,33},{97,1},{2,98}... | collective-permute-start | bytes 296 | tf_op jit(solution)/shard_map/ppermute | solution.py:68
  5.5 21.0 %collective-permute-start.4 = (f32[4,6]{1,0:T(4,128)}, f32[4,6]{1,0:T(4,128)S(1)}, u32[]{:S(2)}, u32[]{:S(2)}) collective-permute-start(f32[4,6]{1,0:T(4,128)} %param.10), channel_id=1, source_target_pairs={{0,32},{32,0},{64,96},{96,64},{1,33},{33,1},{65,97},{97,65},{2,34}... | collective-permute-start | bytes 296 | tf_op jit(solution)/shard_map/ppermute | solution.py:68
  22.1 11.8 %all-to-all-start = ((f32[8,2,4096]{2,1,0:T(2,128)}), f32[8,2,4096]{2,1,0:T(2,128)S(1)}, u32[]{:S(2)}, u32[]{:S(2)}) async-start(f32[8,2,4096]{2,1,0:T(2,128)} %shard_map.95), calls=%async_computation | async-start | bytes 524288 | tf_op jit(solution)/shard_map/all_to_all | solution.py:172
  34.1 5.8 %collective-permute-start.1 = (f32[1,2,4096]{2,1,0:T(2,128)S(1)}, f32[1,2,4096]{2,1,0:T(2,128)S(1)}, u32[]{:S(2)}, u32[]{:S(2)}) collective-permute-start(f32[1,2,4096]{2,1,0:T(2,128)S(1)} %get-tuple-element.179), channel_id=1, source_target_pairs={{0,8},{8,16},{16,24},{1,9},{9,17},{17,25},{2,10},{10,18},{18,26},{... | collective-permute-start | bytes 98312 | tf_op jit(solution)/shard_map/ppermute | solution.py:24
  37.6 5.8 %collective-permute-start = (f32[1,2,4096]{2,1,0:T(2,128)S(1)}, f32[1,2,4096]{2,1,0:T(2,128)S(1)}, u32[]{:S(2)}, u32[]{:S(2)}) collective-permute-start(f32[1,2,4096]{2,1,0:T(2,128)S(1)} %get-tuple-element.180), channel_id=1, source_target_pairs={{8,0},{16,8},{24,16},{9,1},{17,9},{25,17},{10,2},{18,10},{26,18},{... | collective-permute-start | bytes 98312 | tf_op jit(solution)/shard_map/ppermute | solution.py:25
  49.1 9.6 %collective-permute-start.6 = (f32[1,4,128]{2,1,0:T(4,128)S(1)}, f32[1,4,128]{2,1,0:T(4,128)S(1)}, u32[]{:S(2)}, u32[]{:S(2)}) collective-permute-start(f32[1,4,128]{2,1,0:T(4,128)S(1)} %broadcast_in_dim.37), channel_id=1, source_target_pairs={{0,16},{8,24},{16,0},{24,8},{1,17},{9,25},{17,1},{25,9},{2,18},{10... | collective-permute-start | bytes 6152 | tf_op jit(solution)/shard_map/ppermute | solution.py:58
  52.0 6.7 %collective-permute-start.7 = (f32[1,4,128]{2,1,0:T(4,128)S(1)}, f32[1,4,128]{2,1,0:T(4,128)S(1)}, u32[]{:S(2)}, u32[]{:S(2)}) collective-permute-start(f32[1,4,128]{2,1,0:T(4,128)S(1)} %broadcast_in_dim.37), channel_id=1, source_target_pairs={{0,24},{8,16},{16,8},{24,0},{1,25},{9,17},{17,9},{25,1},{2,26},{10... | collective-permute-start | bytes 6152 | tf_op jit(solution)/shard_map/ppermute | solution.py:58
  53.4 5.3 %collective-permute-start.5 = (f32[1,4,128]{2,1,0:T(4,128)S(1)}, f32[1,4,128]{2,1,0:T(4,128)S(1)}, u32[]{:S(2)}, u32[]{:S(2)}) collective-permute-start(f32[1,4,128]{2,1,0:T(4,128)S(1)} %broadcast_in_dim.37), channel_id=1, source_target_pairs={{0,8},{8,0},{16,24},{24,16},{1,9},{9,1},{17,25},{25,17},{2,10},{10... | collective-permute-start | bytes 6152 | tf_op jit(solution)/shard_map/ppermute | solution.py:58
  53.5 6.1 %collective-permute-start.8 = (f32[1,3,1,4096]{3,2,1,0:T(1,128)S(1)}, f32[1,3,1,4096]{3,2,1,0:T(1,128)S(1)}, u32[]{:S(2)}, u32[]{:S(2)}) collective-permute-start(f32[1,3,1,4096]{3,2,1,0:T(1,128)S(1)} %get-tuple-element.162), channel_id=1, source_target_pairs={{0,8},{8,16},{16,24},{1,9},{9,17},{17,25},{2,10},{10,18},{18,26},{... | collective-permute-start | bytes 147464 | tf_op jit(solution)/shard_map/ppermute | solution.py:233
  57.4 6.0 %collective-permute-start.9 = (f32[1,3,1,4096]{3,2,1,0:T(1,128)S(1)}, f32[1,3,1,4096]{3,2,1,0:T(1,128)S(1)}, u32[]{:S(2)}, u32[]{:S(2)}) collective-permute-start(f32[1,3,1,4096]{3,2,1,0:T(1,128)S(1)} %get-tuple-element.163), channel_id=1, source_target_pairs={{8,0},{16,8},{24,16},{9,1},{17,9},{25,17},{10,2},{18,10},{26,18},{... | collective-permute-start | bytes 147464 | tf_op jit(solution)/shard_map/ppermute | solution.py:234
  67.9 9.3 %collective-permute-start.11 = (f32[1,4,128]{2,1,0:T(4,128)S(1)}, f32[1,4,128]{2,1,0:T(4,128)S(1)}, u32[]{:S(2)}, u32[]{:S(2)}) collective-permute-start(f32[1,4,128]{2,1,0:T(4,128)S(1)} %broadcast_in_dim.39), channel_id=1, source_target_pairs={{0,16},{8,24},{16,0},{24,8},{1,17},{9,25},{17,1},{25,9},{2,18},{10... | collective-permute-start | bytes 6152 | tf_op jit(solution)/shard_map/ppermute | solution.py:58
  69.2 7.9 %collective-permute-start.12 = (f32[1,4,128]{2,1,0:T(4,128)S(1)}, f32[1,4,128]{2,1,0:T(4,128)S(1)}, u32[]{:S(2)}, u32[]{:S(2)}) collective-permute-start(f32[1,4,128]{2,1,0:T(4,128)S(1)} %broadcast_in_dim.39), channel_id=1, source_target_pairs={{0,24},{8,16},{16,8},{24,0},{1,25},{9,17},{17,9},{25,1},{2,26},{10... | collective-permute-start | bytes 6152 | tf_op jit(solution)/shard_map/ppermute | solution.py:58
  71.8 5.3 %collective-permute-start.10 = (f32[1,4,128]{2,1,0:T(4,128)S(1)}, f32[1,4,128]{2,1,0:T(4,128)S(1)}, u32[]{:S(2)}, u32[]{:S(2)}) collective-permute-start(f32[1,4,128]{2,1,0:T(4,128)S(1)} %broadcast_in_dim.39), channel_id=1, source_target_pairs={{0,8},{8,0},{16,24},{24,16},{1,9},{9,1},{17,25},{25,17},{2,10},{10... | collective-permute-start | bytes 6152 | tf_op jit(solution)/shard_map/ppermute | solution.py:58
  71.9 6.1 %collective-permute-start.13 = (f32[1,3,1,4096]{3,2,1,0:T(1,128)S(1)}, f32[1,3,1,4096]{3,2,1,0:T(1,128)S(1)}, u32[]{:S(2)}, u32[]{:S(2)}) collective-permute-start(f32[1,3,1,4096]{3,2,1,0:T(1,128)S(1)} %get-tuple-element.156), channel_id=1, source_target_pairs={{0,8},{8,16},{16,24},{1,9},{9,17},{17,25},{2,10},{10,18},{18,26},{... | collective-permute-start | bytes 147464 | tf_op jit(solution)/shard_map/ppermute | solution.py:233
  75.8 6.0 %collective-permute-start.14 = (f32[1,3,1,4096]{3,2,1,0:T(1,128)S(1)}, f32[1,3,1,4096]{3,2,1,0:T(1,128)S(1)}, u32[]{:S(2)}, u32[]{:S(2)}) collective-permute-start(f32[1,3,1,4096]{3,2,1,0:T(1,128)S(1)} %get-tuple-element.157), channel_id=1, source_target_pairs={{8,0},{16,8},{24,16},{9,1},{17,9},{25,17},{10,2},{18,10},{26,18},{... | collective-permute-start | bytes 147464 | tf_op jit(solution)/shard_map/ppermute | solution.py:234
  86.4 8.0 %collective-permute-start.16 = (f32[1,4,128]{2,1,0:T(4,128)S(1)}, f32[1,4,128]{2,1,0:T(4,128)S(1)}, u32[]{:S(2)}, u32[]{:S(2)}) collective-permute-start(f32[1,4,128]{2,1,0:T(4,128)S(1)} %broadcast_in_dim.41), channel_id=1, source_target_pairs={{0,16},{8,24},{16,0},{24,8},{1,17},{9,25},{17,1},{25,9},{2,18},{10... | collective-permute-start | bytes 6152 | tf_op jit(solution)/shard_map/ppermute | solution.py:58
  86.5 7.9 %collective-permute-start.17 = (f32[1,4,128]{2,1,0:T(4,128)S(1)}, f32[1,4,128]{2,1,0:T(4,128)S(1)}, u32[]{:S(2)}, u32[]{:S(2)}) collective-permute-start(f32[1,4,128]{2,1,0:T(4,128)S(1)} %broadcast_in_dim.41), channel_id=1, source_target_pairs={{0,24},{8,16},{16,8},{24,0},{1,25},{9,17},{17,9},{25,1},{2,26},{10... | collective-permute-start | bytes 6152 | tf_op jit(solution)/shard_map/ppermute | solution.py:58
  89.1 5.3 %collective-permute-start.15 = (f32[1,4,128]{2,1,0:T(4,128)S(1)}, f32[1,4,128]{2,1,0:T(4,128)S(1)}, u32[]{:S(2)}, u32[]{:S(2)}) collective-permute-start(f32[1,4,128]{2,1,0:T(4,128)S(1)} %broadcast_in_dim.41), channel_id=1, source_target_pairs={{0,8},{8,0},{16,24},{24,16},{1,9},{9,1},{17,25},{25,17},{2,10},{10... | collective-permute-start | bytes 6152 | tf_op jit(solution)/shard_map/ppermute | solution.py:58
  90.0 5.3 %collective-permute-start.18 = (f32[1,3,1,4096]{3,2,1,0:T(1,128)S(1)}, f32[1,3,1,4096]{3,2,1,0:T(1,128)S(1)}, u32[]{:S(2)}, u32[]{:S(2)}) collective-permute-start(f32[1,3,1,4096]{3,2,1,0:T(1,128)S(1)} %get-tuple-element.150), channel_id=1, source_target_pairs={{0,8},{8,16},{16,24},{1,9},{9,17},{17,25},{2,10},{10,18},{18,26},{... | collective-permute-start | bytes 147464 | tf_op jit(solution)/shard_map/ppermute | solution.py:233
  93.1 6.0 %collective-permute-start.19 = (f32[1,3,1,4096]{3,2,1,0:T(1,128)S(1)}, f32[1,3,1,4096]{3,2,1,0:T(1,128)S(1)}, u32[]{:S(2)}, u32[]{:S(2)}) collective-permute-start(f32[1,3,1,4096]{3,2,1,0:T(1,128)S(1)} %get-tuple-element.151), channel_id=1, source_target_pairs={{8,0},{16,8},{24,16},{9,1},{17,9},{25,17},{10,2},{18,10},{26,18},{... | collective-permute-start | bytes 147464 | tf_op jit(solution)/shard_map/ppermute | solution.py:234
  103.8 8.0 %collective-permute-start.21 = (f32[1,4,128]{2,1,0:T(4,128)S(1)}, f32[1,4,128]{2,1,0:T(4,128)S(1)}, u32[]{:S(2)}, u32[]{:S(2)}) collective-permute-start(f32[1,4,128]{2,1,0:T(4,128)S(1)} %broadcast_in_dim.43), channel_id=1, source_target_pairs={{0,16},{8,24},{16,0},{24,8},{1,17},{9,25},{17,1},{25,9},{2,18},{10... | collective-permute-start | bytes 6152 | tf_op jit(solution)/shard_map/ppermute | solution.py:58
  104.7 7.2 %collective-permute-start.22 = (f32[1,4,128]{2,1,0:T(4,128)S(1)}, f32[1,4,128]{2,1,0:T(4,128)S(1)}, u32[]{:S(2)}, u32[]{:S(2)}) collective-permute-start(f32[1,4,128]{2,1,0:T(4,128)S(1)} %broadcast_in_dim.43), channel_id=1, source_target_pairs={{0,24},{8,16},{16,8},{24,0},{1,25},{9,17},{17,9},{25,1},{2,26},{10... | collective-permute-start | bytes 6152 | tf_op jit(solution)/shard_map/ppermute | solution.py:58
  106.5 5.3 %collective-permute-start.20 = (f32[1,4,128]{2,1,0:T(4,128)S(1)}, f32[1,4,128]{2,1,0:T(4,128)S(1)}, u32[]{:S(2)}, u32[]{:S(2)}) collective-permute-start(f32[1,4,128]{2,1,0:T(4,128)S(1)} %broadcast_in_dim.43), channel_id=1, source_target_pairs={{0,8},{8,0},{16,24},{24,16},{1,9},{9,1},{17,25},{25,17},{2,10},{10... | collective-permute-start | bytes 6152 | tf_op jit(solution)/shard_map/ppermute | solution.py:58
  107.4 5.3 %collective-permute-start.23 = (f32[1,3,1,4096]{3,2,1,0:T(1,128)S(1)}, f32[1,3,1,4096]{3,2,1,0:T(1,128)S(1)}, u32[]{:S(2)}, u32[]{:S(2)}) collective-permute-start(f32[1,3,1,4096]{3,2,1,0:T(1,128)S(1)} %get-tuple-element.144), channel_id=1, source_target_pairs={{0,8},{8,16},{16,24},{1,9},{9,17},{17,25},{2,10},{10,18},{18,26},{... | collective-permute-start | bytes 147464 | tf_op jit(solution)/shard_map/ppermute | solution.py:233
  110.5 6.0 %collective-permute-start.24 = (f32[1,3,1,4096]{3,2,1,0:T(1,128)S(1)}, f32[1,3,1,4096]{3,2,1,0:T(1,128)S(1)}, u32[]{:S(2)}, u32[]{:S(2)}) collective-permute-start(f32[1,3,1,4096]{3,2,1,0:T(1,128)S(1)} %get-tuple-element.145), channel_id=1, source_target_pairs={{8,0},{16,8},{24,16},{9,1},{17,9},{25,17},{10,2},{18,10},{26,18},{... | collective-permute-start | bytes 147464 | tf_op jit(solution)/shard_map/ppermute | solution.py:234
  121.0 8.8 %collective-permute-start.26 = (f32[1,4,128]{2,1,0:T(4,128)S(1)}, f32[1,4,128]{2,1,0:T(4,128)S(1)}, u32[]{:S(2)}, u32[]{:S(2)}) collective-permute-start(f32[1,4,128]{2,1,0:T(4,128)S(1)} %broadcast_in_dim.45), channel_id=1, source_target_pairs={{0,16},{8,24},{16,0},{24,8},{1,17},{9,25},{17,1},{25,9},{2,18},{10... | collective-permute-start | bytes 6152 | tf_op jit(solution)/shard_map/ppermute | solution.py:58
  121.8 7.9 %collective-permute-start.27 = (f32[1,4,128]{2,1,0:T(4,128)S(1)}, f32[1,4,128]{2,1,0:T(4,128)S(1)}, u32[]{:S(2)}, u32[]{:S(2)}) collective-permute-start(f32[1,4,128]{2,1,0:T(4,128)S(1)} %broadcast_in_dim.45), channel_id=1, source_target_pairs={{0,24},{8,16},{16,8},{24,0},{1,25},{9,17},{17,9},{25,1},{2,26},{10... | collective-permute-start | bytes 6152 | tf_op jit(solution)/shard_map/ppermute | solution.py:58
  124.4 5.3 %collective-permute-start.25 = (f32[1,4,128]{2,1,0:T(4,128)S(1)}, f32[1,4,128]{2,1,0:T(4,128)S(1)}, u32[]{:S(2)}, u32[]{:S(2)}) collective-permute-start(f32[1,4,128]{2,1,0:T(4,128)S(1)} %broadcast_in_dim.45), channel_id=1, source_target_pairs={{0,8},{8,0},{16,24},{24,16},{1,9},{9,1},{17,25},{25,17},{2,10},{10... | collective-permute-start | bytes 6152 | tf_op jit(solution)/shard_map/ppermute | solution.py:58
  124.5 6.1 %collective-permute-start.28 = (f32[1,3,1,4096]{3,2,1,0:T(1,128)S(1)}, f32[1,3,1,4096]{3,2,1,0:T(1,128)S(1)}, u32[]{:S(2)}, u32[]{:S(2)}) collective-permute-start(f32[1,3,1,4096]{3,2,1,0:T(1,128)S(1)} %get-tuple-element.138), channel_id=1, source_target_pairs={{0,8},{8,16},{16,24},{1,9},{9,17},{17,25},{2,10},{10,18},{18,26},{... | collective-permute-start | bytes 147464 | tf_op jit(solution)/shard_map/ppermute | solution.py:233
  128.4 6.0 %collective-permute-start.29 = (f32[1,3,1,4096]{3,2,1,0:T(1,128)S(1)}, f32[1,3,1,4096]{3,2,1,0:T(1,128)S(1)}, u32[]{:S(2)}, u32[]{:S(2)}) collective-permute-start(f32[1,3,1,4096]{3,2,1,0:T(1,128)S(1)} %get-tuple-element.139), channel_id=1, source_target_pairs={{8,0},{16,8},{24,16},{9,1},{17,9},{25,17},{10,2},{18,10},{26,18},{... | collective-permute-start | bytes 147464 | tf_op jit(solution)/shard_map/ppermute | solution.py:234
  138.9 8.0 %collective-permute-start.31 = (f32[1,4,128]{2,1,0:T(4,128)S(1)}, f32[1,4,128]{2,1,0:T(4,128)S(1)}, u32[]{:S(2)}, u32[]{:S(2)}) collective-permute-start(f32[1,4,128]{2,1,0:T(4,128)S(1)} %broadcast_in_dim.47), channel_id=1, source_target_pairs={{0,16},{8,24},{16,0},{24,8},{1,17},{9,25},{17,1},{25,9},{2,18},{10... | collective-permute-start | bytes 6152 | tf_op jit(solution)/shard_map/ppermute | solution.py:58
  139.0 7.9 %collective-permute-start.32 = (f32[1,4,128]{2,1,0:T(4,128)S(1)}, f32[1,4,128]{2,1,0:T(4,128)S(1)}, u32[]{:S(2)}, u32[]{:S(2)}) collective-permute-start(f32[1,4,128]{2,1,0:T(4,128)S(1)} %broadcast_in_dim.47), channel_id=1, source_target_pairs={{0,24},{8,16},{16,8},{24,0},{1,25},{9,17},{17,9},{25,1},{2,26},{10... | collective-permute-start | bytes 6152 | tf_op jit(solution)/shard_map/ppermute | solution.py:58
  141.6 5.3 %collective-permute-start.30 = (f32[1,4,128]{2,1,0:T(4,128)S(1)}, f32[1,4,128]{2,1,0:T(4,128)S(1)}, u32[]{:S(2)}, u32[]{:S(2)}) collective-permute-start(f32[1,4,128]{2,1,0:T(4,128)S(1)} %broadcast_in_dim.47), channel_id=1, source_target_pairs={{0,8},{8,0},{16,24},{24,16},{1,9},{9,1},{17,25},{25,17},{2,10},{10... | collective-permute-start | bytes 6152 | tf_op jit(solution)/shard_map/ppermute | solution.py:58
  142.5 5.3 %collective-permute-start.33 = (f32[1,3,1,4096]{3,2,1,0:T(1,128)S(1)}, f32[1,3,1,4096]{3,2,1,0:T(1,128)S(1)}, u32[]{:S(2)}, u32[]{:S(2)}) collective-permute-start(f32[1,3,1,4096]{3,2,1,0:T(1,128)S(1)} %get-tuple-element.132), channel_id=1, source_target_pairs={{0,8},{8,16},{16,24},{1,9},{9,17},{17,25},{2,10},{10,18},{18,26},{... | collective-permute-start | bytes 147464 | tf_op jit(solution)/shard_map/ppermute | solution.py:233
  145.7 6.0 %collective-permute-start.34 = (f32[1,3,1,4096]{3,2,1,0:T(1,128)S(1)}, f32[1,3,1,4096]{3,2,1,0:T(1,128)S(1)}, u32[]{:S(2)}, u32[]{:S(2)}) collective-permute-start(f32[1,3,1,4096]{3,2,1,0:T(1,128)S(1)} %get-tuple-element.133), channel_id=1, source_target_pairs={{8,0},{16,8},{24,16},{9,1},{17,9},{25,17},{10,2},{18,10},{26,18},{... | collective-permute-start | bytes 147464 | tf_op jit(solution)/shard_map/ppermute | solution.py:234
  156.1 8.2 %collective-permute-start.36 = (f32[1,4,128]{2,1,0:T(4,128)S(1)}, f32[1,4,128]{2,1,0:T(4,128)S(1)}, u32[]{:S(2)}, u32[]{:S(2)}) collective-permute-start(f32[1,4,128]{2,1,0:T(4,128)S(1)} %broadcast_in_dim.49), channel_id=1, source_target_pairs={{0,16},{8,24},{16,0},{24,8},{1,17},{9,25},{17,1},{25,9},{2,18},{10... | collective-permute-start | bytes 6152 | tf_op jit(solution)/shard_map/ppermute | solution.py:58
  156.9 7.4 %collective-permute-start.37 = (f32[1,4,128]{2,1,0:T(4,128)S(1)}, f32[1,4,128]{2,1,0:T(4,128)S(1)}, u32[]{:S(2)}, u32[]{:S(2)}) collective-permute-start(f32[1,4,128]{2,1,0:T(4,128)S(1)} %broadcast_in_dim.49), channel_id=1, source_target_pairs={{0,24},{8,16},{16,8},{24,0},{1,25},{9,17},{17,9},{25,1},{2,26},{10... | collective-permute-start | bytes 6152 | tf_op jit(solution)/shard_map/ppermute | solution.py:58
  158.8 5.6 %collective-permute-start.35 = (f32[1,4,128]{2,1,0:T(4,128)S(1)}, f32[1,4,128]{2,1,0:T(4,128)S(1)}, u32[]{:S(2)}, u32[]{:S(2)}) collective-permute-start(f32[1,4,128]{2,1,0:T(4,128)S(1)} %broadcast_in_dim.49), channel_id=1, source_target_pairs={{0,8},{8,0},{16,24},{24,16},{1,9},{9,1},{17,25},{25,17},{2,10},{10... | collective-permute-start | bytes 6152 | tf_op jit(solution)/shard_map/ppermute | solution.py:58
  159.6 8.1 %collective-permute-start.38 = (f32[1,3,1,4096]{3,2,1,0:T(1,128)S(1)}, f32[1,3,1,4096]{3,2,1,0:T(1,128)S(1)}, u32[]{:S(2)}, u32[]{:S(2)}) collective-permute-start(f32[1,3,1,4096]{3,2,1,0:T(1,128)S(1)} %get-tuple-element.130), channel_id=1, source_target_pairs={{0,8},{8,16},{16,24},{1,9},{9,17},{17,25},{2,10},{10,18},{18,26},{... | collective-permute-start | bytes 147464 | tf_op jit(solution)/shard_map/ppermute | solution.py:233
  163.0 6.0 %collective-permute-start.39 = (f32[1,3,1,4096]{3,2,1,0:T(1,128)S(1)}, f32[1,3,1,4096]{3,2,1,0:T(1,128)S(1)}, u32[]{:S(2)}, u32[]{:S(2)}) collective-permute-start(f32[1,3,1,4096]{3,2,1,0:T(1,128)S(1)} %get-tuple-element.131), channel_id=1, source_target_pairs={{8,0},{16,8},{24,16},{9,1},{17,9},{25,17},{10,2},{18,10},{26,18},{... | collective-permute-start | bytes 147464 | tf_op jit(solution)/shard_map/ppermute | solution.py:234
  185.4 4.9 %collective-permute-start.42 = (f32[1,23]{1,0:T(1,128)S(1)}, f32[1,23]{1,0:T(1,128)S(1)}, u32[]{:S(2)}, u32[]{:S(2)}) collective-permute-start(f32[1,23]{1,0:T(1,128)S(1)} %stack.256), channel_id=1, source_target_pairs={{0,24},{8,16},{16,8},{24,0},{1,25},{9,17},{17,9},{25,1},{2,26},{10... | collective-permute-start | bytes 284 | tf_op jit(solution)/shard_map/ppermute | solution.py:58
  186.2 5.1 %collective-permute-start.41 = (f32[1,23]{1,0:T(1,128)S(1)}, f32[1,23]{1,0:T(1,128)S(1)}, u32[]{:S(2)}, u32[]{:S(2)}) collective-permute-start(f32[1,23]{1,0:T(1,128)S(1)} %stack.256), channel_id=1, source_target_pairs={{0,16},{8,24},{16,0},{24,8},{1,17},{9,25},{17,1},{25,9},{2,18},{10... | collective-permute-start | bytes 284 | tf_op jit(solution)/shard_map/ppermute | solution.py:58
  188.9 3.6 %collective-permute-start.40 = (f32[1,23]{1,0:T(1,128)S(1)}, f32[1,23]{1,0:T(1,128)S(1)}, u32[]{:S(2)}, u32[]{:S(2)}) collective-permute-start(f32[1,23]{1,0:T(1,128)S(1)} %stack.256), channel_id=1, source_target_pairs={{0,8},{8,0},{16,24},{24,16},{1,9},{9,1},{17,25},{25,17},{2,10},{10... | collective-permute-start | bytes 284 | tf_op jit(solution)/shard_map/ppermute | solution.py:58
  196.6 5.4 %collective-permute-start.43 = (f32[8,6]{1,0:T(8,128)S(1)}, f32[8,6]{1,0:T(8,128)S(1)}, u32[]{:S(2)}, u32[]{:S(2)}) collective-permute-start(f32[8,6]{1,0:T(8,128)S(1)} %broadcast_multiply_fusion), channel_id=1, source_target_pairs={{0,1},{1,0},{2,3},{3,2},{4,5},{5,4},{6,7},{7,6},{8,9},{9,8},{10,11... | collective-permute-start | bytes 584 | tf_op jit(solution)/shard_map/ppermute | solution.py:58
  198.4 27.2 %all-to-all-start.1 = ((f32[1,3,16,4096]{3,0,1,2:T(1,128)}), f32[1,3,16,4096]{3,0,1,2:T(1,128)S(1)}, u32[]{:S(2)}, u32[]{:S(2)}) async-start(f32[1,3,16,4096]{3,0,1,2:T(1,128)} %copy.51), calls=%async_computation.1 | async-start | bytes 1572864 | tf_op jit(solution)/shard_map/all_to_all | solution.py:308
  202.1 9.9 %collective-permute-start.46 = (f32[8,6]{1,0:T(8,128)S(1)}, f32[8,6]{1,0:T(8,128)S(1)}, u32[]{:S(2)}, u32[]{:S(2)}) collective-permute-start(f32[8,6]{1,0:T(8,128)S(1)} %fusion.111), channel_id=1, source_target_pairs={{0,6},{1,7},{2,4},{3,5},{4,2},{5,3},{6,0},{7,1},{8,14},{9,15},{10,... | collective-permute-start | bytes 584 | tf_op jit(solution)/shard_map/ppermute | solution.py:58
  205.2 9.9 %collective-permute-start.45 = (f32[8,6]{1,0:T(8,128)S(1)}, f32[8,6]{1,0:T(8,128)S(1)}, u32[]{:S(2)}, u32[]{:S(2)}) collective-permute-start(f32[8,6]{1,0:T(8,128)S(1)} %fusion.111), channel_id=1, source_target_pairs={{0,4},{1,5},{2,6},{3,7},{4,0},{5,1},{6,2},{7,3},{8,12},{9,13},{10,... | collective-permute-start | bytes 584 | tf_op jit(solution)/shard_map/ppermute | solution.py:58
  206.1 9.1 %collective-permute-start.44 = (f32[8,6]{1,0:T(8,128)S(1)}, f32[8,6]{1,0:T(8,128)S(1)}, u32[]{:S(2)}, u32[]{:S(2)}) collective-permute-start(f32[8,6]{1,0:T(8,128)S(1)} %fusion.111), channel_id=1, source_target_pairs={{0,2},{1,3},{2,0},{3,1},{4,6},{5,7},{6,4},{7,5},{8,10},{9,11},{10,... | collective-permute-start | bytes 584 | tf_op jit(solution)/shard_map/ppermute | solution.py:58
  215.5 4.3 %collective-permute-start.47 = (f32[4,6]{0,1:T(8,128)S(1)}, f32[4,6]{0,1:T(8,128)S(1)}, u32[]{:S(2)}, u32[]{:S(2)}) collective-permute-start(f32[4,6]{0,1:T(8,128)S(1)} %get-tuple-element.202), channel_id=1, source_target_pairs={{0,32},{32,0},{64,96},{96,64},{1,33},{33,1},{65,97},{97,65},{2,34}... | collective-permute-start | bytes 296 | tf_op jit(solution)/shard_map/ppermute | solution.py:83
  217.2 4.8 %collective-permute-start.49 = (f32[4,6]{0,1:T(8,128)S(1)}, f32[4,6]{0,1:T(8,128)S(1)}, u32[]{:S(2)}, u32[]{:S(2)}) collective-permute-start(f32[4,6]{0,1:T(8,128)S(1)} %get-tuple-element.203), channel_id=1, source_target_pairs={{0,96},{32,64},{64,32},{96,0},{1,97},{33,65},{65,33},{97,1},{2,98}... | collective-permute-start | bytes 296 | tf_op jit(solution)/shard_map/ppermute | solution.py:83
  219.7 5.1 %collective-permute-start.48 = (f32[4,6]{0,1:T(8,128)S(1)}, f32[4,6]{0,1:T(8,128)S(1)}, u32[]{:S(2)}, u32[]{:S(2)}) collective-permute-start(f32[4,6]{0,1:T(8,128)S(1)} %get-tuple-element.204), channel_id=1, source_target_pairs={{0,64},{32,96},{64,0},{96,32},{1,65},{33,97},{65,1},{97,33},{2,66}... | collective-permute-start | bytes 296 | tf_op jit(solution)/shard_map/ppermute | solution.py:83

commit v5 on v3

--- a/solution.py
+++ b/solution.py
@@ -286,9 +286,10 @@
             terms.append(jnp.sum(stiff, axis=(1, 2)))
         local = jnp.stack(terms, -1)
         if last:
-            sums = axis_sum(local, "yb")
-            norm_now = sums[:, 1]
-            alpha = norm_now / sums[:, 0]
+            lanes = axis_sum(jnp.broadcast_to(local[:, :, None], local.shape + (128,)), "yb")
+            lane_alpha = lanes[:, 1] / lanes[:, 0]
+            sums = lanes[:, :, 0]
+            alpha = lane_alpha[:, 0]
         else:
             lanes = axis_sum(jnp.broadcast_to(local[:, :, None], local.shape + (128,)), "yb")
             lane_alpha = lanes[:, 1] / lanes[:, 0]

time: 228 us -> 228 us (level)
  no operation moved by 1% of the time
where the time goes in v5:
time: 228 us; the launch traced here: 227 us
  starting transfers between devices  89.4 us (39%)
  waiting for transfers between devices  48.2 us (21%)
  other arithmetic  40 us (18%)
  local copies, waits for them, and re-layouts  27.9 us (12%)
  Pallas kernels  15 us (7%)
  between operations  5.95 us (3%)
    ppermute x28, starting transfers between devices, axis_sum(): vals[o] = lax.ppermute(value, axis, [(i, i ^ mask) for i in range(size)])  33.9 us
    ppermute x7, starting transfers between devices, boundary_planes(): before = lax.ppermute(value[:, :, -1:], 'yb', up)  24.5 us
    ppermute x7, waiting for transfers between devices, boundary_planes(): after = lax.ppermute(value[:, :, :1], 'yb', down)  24.2 us
    broadcast_in_dim x7, other arithmetic, shards(): jnp.broadcast_to(local[:, :, None], local.shape + (128,))  17.3 us
    pallas_call x1, Pallas kernels, stiffness(): pl.pallas_call(stiffness_kernel, grid=(rves,), in_specs=[pl.BlockSpec(pie...  15 us
    another operation x1, local copies, waits for them, and re-layouts, shards(): local = jnp.stack(terms, -1)  14.5 us
    ppermute x28, waiting for transfers between devices, axis_sum(): vals[o] = lax.ppermute(value, axis, [(i, i ^ mask) for i in range(size)])  12.7 us
    reduce_sum x8, other arithmetic, local_dot(): return jnp.sum(first * second, axis=(1, 2, 3))  12.5 us
  transfers between devices with their start and end apart: 52, of which 16 were waited for; matrix products, arithmetic and copies ran while one was open for 7% of the time, Pallas kernels for 7%

profile of v5, /device:TPU:0, one launch (start us, length us, event | category | flops | bytes accessed | tf_op | source)
XLA Modules:
  0.0 226.8 jit_solution(18034942972903737168)
XLA Ops:
  0.7 4.1 %collective-permute-start.3 = (f32[4,6]{1,0:T(4,128)}, f32[4,6]{1,0:T(4,128)S(1)}, u32[]{:S(2)}, u32[]{:S(2)}) collective-permute-start(f32[4,6]{1,0:T(4,128)} %param.10), channel_id=1, source_target_pairs={{0,64},{32,96},{64,0},{96,32},{1,65},{33,97},{65,1},{97,33},{2,66}... | collective-permute-start | bytes 296 | tf_op jit(solution)/shard_map/ppermute | solution.py:68
  7.1 15.0 %shard_map.95 = f32[8,2,4096]{2,1,0:T(2,128)} custom-call(bf16[3,16,64]{2,1,0:T(8,128)(2,1)} %fusion.95.pieces_ref, s32[8,2,4096]{2,1,0:T(2,128)} %codes_ref.1, s32[8,2,4096]{2,1,0:T(2,128)} %grains_ref.1), custom_call_target="tpu_custom_call" | custom-call | tf_op jit(solution)/shard_map/pallas_call | solution.py:122
  22.1 4.3 %all-to-all-start = ((f32[8,2,4096]{2,1,0:T(2,128)}), f32[8,2,4096]{2,1,0:T(2,128)S(1)}, u32[]{:S(2)}, u32[]{:S(2)}) async-start(f32[8,2,4096]{2,1,0:T(2,128)} %shard_map.95), calls=%async_computation | async-start | bytes 524288 | tf_op jit(solution)/shard_map/all_to_all | solution.py:186
  31.2 2.7 %all-to-all-done = f32[8,2,4096]{2,1,0:T(2,128)S(1)} async-done(((f32[8,2,4096]{2,1,0:T(2,128)}), f32[8,2,4096]{2,1,0:T(2,128)S(1)}, u32[]{:S(2)}, u32[]{:S(2)}) %all-to-all-start) | async-done | bytes 262176 | tf_op jit(solution)/shard_map/all_to_all | solution.py:186
  34.1 3.5 %collective-permute-start.1 = (f32[1,2,4096]{2,1,0:T(2,128)S(1)}, f32[1,2,4096]{2,1,0:T(2,128)S(1)}, u32[]{:S(2)}, u32[]{:S(2)}) collective-permute-start(f32[1,2,4096]{2,1,0:T(2,128)S(1)} %get-tuple-element.179), channel_id=1, source_target_pairs={{0,8},{8,16},{16,24},{1,9},{9,17},{17,25},{2,10},{10,18},{18,26},{... | collective-permute-start | bytes 98312 | tf_op jit(solution)/shard_map/ppermute | solution.py:24
  37.6 1.3 collective-permute-start
  39.9 3.5 %collective-permute-done = f32[1,2,4096]{2,1,0:T(2,128)S(1)} collective-permute-done((f32[1,2,4096]{2,1,0:T(2,128)S(1)}, f32[1,2,4096]{2,1,0:T(2,128)S(1)}, u32[]{:S(2)}, u32[]{:S(2)}) %collective-permute-start) | collective-permute-done | bytes 32800 | tf_op jit(solution)/shard_map/ppermute | solution.py:25
  45.6 1.5 multiply_reduce_fusion.29
  47.1 1.9 maximum_bitcast_fusion
  49.1 2.9 %collective-permute-start.6 = (f32[1,4,128]{2,1,0:T(4,128)S(1)}, f32[1,4,128]{2,1,0:T(4,128)S(1)}, u32[]{:S(2)}, u32[]{:S(2)}) collective-permute-start(f32[1,4,128]{2,1,0:T(4,128)S(1)} %broadcast_in_dim.41), channel_id=1, source_target_pairs={{0,16},{8,24},{16,0},{24,8},{1,17},{9,25},{17,1},{25,9},{2,18},{10... | collective-permute-start | bytes 6152 | tf_op jit(solution)/shard_map/ppermute | solution.py:58
  52.1 1.3 collective-permute-start.7
  53.5 3.9 %collective-permute-start.8 = (f32[1,3,1,4096]{3,2,1,0:T(1,128)S(1)}, f32[1,3,1,4096]{3,2,1,0:T(1,128)S(1)}, u32[]{:S(2)}, u32[]{:S(2)}) collective-permute-start(f32[1,3,1,4096]{3,2,1,0:T(1,128)S(1)} %get-tuple-element.162), channel_id=1, source_target_pairs={{0,8},{8,16},{16,24},{1,9},{9,17},{17,25},{2,10},{10,18},{18,26},{... | collective-permute-start | bytes 147464 | tf_op jit(solution)/shard_map/ppermute | solution.py:247
  57.4 1.3 collective-permute-start.9
  59.6 3.8 %collective-permute-done.9 = f32[1,3,1,4096]{3,2,1,0:T(1,128)S(1)} collective-permute-done((f32[1,3,1,4096]{3,2,1,0:T(1,128)S(1)}, f32[1,3,1,4096]{3,2,1,0:T(1,128)S(1)}, u32[]{:S(2)}, u32[]{:S(2)}) %collective-permute-start.9) | collective-permute-done | bytes 49184 | tf_op jit(solution)/shard_map/ppermute | solution.py:248
  63.7 1.6 multiply_reduce_fusion.27
  65.3 2.6 %maximum_bitcast_fusion.1 = f32[4]{0:T(128)S(1)} fusion(f32[1,1]{1,0:T(1,128)} %bitcast.32, f32[1,1]{1,0:T(1,128)} %bitcast.31, f32[1,1]{1,0:T(1,128)} %bitcast.30, f32[1,1]{1,0:T(1,128)} %bitcast.29), kind=kLoop, calls=%fused_computation.275 | loop fusion | flops 12 | bytes 32 | tf_op jit(solution)/shard_map/broadcast_in_dim | solution.py:294
  67.9 1.3 collective-permute-start.11
  69.3 2.6 %collective-permute-start.12 = (f32[1,4,128]{2,1,0:T(4,128)S(1)}, f32[1,4,128]{2,1,0:T(4,128)S(1)}, u32[]{:S(2)}, u32[]{:S(2)}) collective-permute-start(f32[1,4,128]{2,1,0:T(4,128)S(1)} %broadcast_in_dim.43), channel_id=1, source_target_pairs={{0,24},{8,16},{16,8},{24,0},{1,25},{9,17},{17,9},{25,1},{2,26},{10... | collective-permute-start | bytes 6152 | tf_op jit(solution)/shard_map/ppermute | solution.py:58
  72.0 3.9 %collective-permute-start.13 = (f32[1,3,1,4096]{3,2,1,0:T(1,128)S(1)}, f32[1,3,1,4096]{3,2,1,0:T(1,128)S(1)}, u32[]{:S(2)}, u32[]{:S(2)}) collective-permute-start(f32[1,3,1,4096]{3,2,1,0:T(1,128)S(1)} %get-tuple-element.156), channel_id=1, source_target_pairs={{0,8},{8,16},{16,24},{1,9},{9,17},{17,25},{2,10},{10,18},{18,26},{... | collective-permute-start | bytes 147464 | tf_op jit(solution)/shard_map/ppermute | solution.py:247
  75.9 1.3 collective-permute-start.14
  78.1 3.8 %collective-permute-done.14 = f32[1,3,1,4096]{3,2,1,0:T(1,128)S(1)} collective-permute-done((f32[1,3,1,4096]{3,2,1,0:T(1,128)S(1)}, f32[1,3,1,4096]{3,2,1,0:T(1,128)S(1)}, u32[]{:S(2)}, u32[]{:S(2)}) %collective-permute-start.14) | collective-permute-done | bytes 49184 | tf_op jit(solution)/shard_map/ppermute | solution.py:248
  82.3 1.6 multiply_reduce_fusion.23
  83.9 2.6 %maximum_bitcast_fusion.2 = f32[4]{0:T(128)S(1)} fusion(f32[1,1]{1,0:T(1,128)} %bitcast.43, f32[1,1]{1,0:T(1,128)} %bitcast.42, f32[1,1]{1,0:T(1,128)} %bitcast.41, f32[1,1]{1,0:T(1,128)} %bitcast.40), kind=kLoop, calls=%fused_computation.276 | loop fusion | flops 12 | bytes 32 | tf_op jit(solution)/shard_map/broadcast_in_dim | solution.py:294
  86.6 2.6 %collective-permute-start.17 = (f32[1,4,128]{2,1,0:T(4,128)S(1)}, f32[1,4,128]{2,1,0:T(4,128)S(1)}, u32[]{:S(2)}, u32[]{:S(2)}) collective-permute-start(f32[1,4,128]{2,1,0:T(4,128)S(1)} %broadcast_in_dim.45), channel_id=1, source_target_pairs={{0,24},{8,16},{16,8},{24,0},{1,25},{9,17},{17,9},{25,1},{2,26},{10... | collective-permute-start | bytes 6152 | tf_op jit(solution)/shard_map/ppermute | solution.py:58
  90.1 3.1 %collective-permute-start.18 = (f32[1,3,1,4096]{3,2,1,0:T(1,128)S(1)}, f32[1,3,1,4096]{3,2,1,0:T(1,128)S(1)}, u32[]{:S(2)}, u32[]{:S(2)}) collective-permute-start(f32[1,3,1,4096]{3,2,1,0:T(1,128)S(1)} %get-tuple-element.150), channel_id=1, source_target_pairs={{0,8},{8,16},{16,24},{1,9},{9,17},{17,25},{2,10},{10,18},{18,26},{... | collective-permute-start | bytes 147464 | tf_op jit(solution)/shard_map/ppermute | solution.py:247
  93.2 1.3 collective-permute-start.19
  95.4 3.8 %collective-permute-done.19 = f32[1,3,1,4096]{3,2,1,0:T(1,128)S(1)} collective-permute-done((f32[1,3,1,4096]{3,2,1,0:T(1,128)S(1)}, f32[1,3,1,4096]{3,2,1,0:T(1,128)S(1)}, u32[]{:S(2)}, u32[]{:S(2)}) %collective-permute-start.19) | collective-permute-done | bytes 49184 | tf_op jit(solution)/shard_map/ppermute | solution.py:248
  99.7 1.6 multiply_reduce_fusion.19
  101.3 2.6 %maximum_bitcast_fusion.3 = f32[4]{0:T(128)S(1)} fusion(f32[1,1]{1,0:T(1,128)} %bitcast.54, f32[1,1]{1,0:T(1,128)} %bitcast.53, f32[1,1]{1,0:T(1,128)} %bitcast.52, f32[1,1]{1,0:T(1,128)} %bitcast.51), kind=kLoop, calls=%fused_computation.277 | loop fusion | flops 12 | bytes 32 | tf_op jit(solution)/shard_map/broadcast_in_dim | solution.py:294
  104.8 1.8 collective-permute-start.22
  107.5 3.1 %collective-permute-start.23 = (f32[1,3,1,4096]{3,2,1,0:T(1,128)S(1)}, f32[1,3,1,4096]{3,2,1,0:T(1,128)S(1)}, u32[]{:S(2)}, u32[]{:S(2)}) collective-permute-start(f32[1,3,1,4096]{3,2,1,0:T(1,128)S(1)} %get-tuple-element.144), channel_id=1, source_target_pairs={{0,8},{8,16},{16,24},{1,9},{9,17},{17,25},{2,10},{10,18},{18,26},{... | collective-permute-start | bytes 147464 | tf_op jit(solution)/shard_map/ppermute | solution.py:247
  110.6 1.3 collective-permute-start.24
  112.8 3.8 %collective-permute-done.24 = f32[1,3,1,4096]{3,2,1,0:T(1,128)S(1)} collective-permute-done((f32[1,3,1,4096]{3,2,1,0:T(1,128)S(1)}, f32[1,3,1,4096]{3,2,1,0:T(1,128)S(1)}, u32[]{:S(2)}, u32[]{:S(2)}) %collective-permute-start.24) | collective-permute-done | bytes 49184 | tf_op jit(solution)/shard_map/ppermute | solution.py:248
  116.9 1.6 multiply_reduce_fusion.15
  118.5 2.6 %maximum_bitcast_fusion.4 = f32[4]{0:T(128)S(1)} fusion(f32[1,1]{1,0:T(1,128)} %bitcast.65, f32[1,1]{1,0:T(1,128)} %bitcast.64, f32[1,1]{1,0:T(1,128)} %bitcast.63, f32[1,1]{1,0:T(1,128)} %bitcast.62), kind=kLoop, calls=%fused_computation.278 | loop fusion | flops 12 | bytes 32 | tf_op jit(solution)/shard_map/broadcast_in_dim | solution.py:294
  121.9 2.6 %collective-permute-start.27 = (f32[1,4,128]{2,1,0:T(4,128)S(1)}, f32[1,4,128]{2,1,0:T(4,128)S(1)}, u32[]{:S(2)}, u32[]{:S(2)}) collective-permute-start(f32[1,4,128]{2,1,0:T(4,128)S(1)} %broadcast_in_dim.49), channel_id=1, source_target_pairs={{0,24},{8,16},{16,8},{24,0},{1,25},{9,17},{17,9},{25,1},{2,26},{10... | collective-permute-start | bytes 6152 | tf_op jit(solution)/shard_map/ppermute | solution.py:58
  124.6 3.9 %collective-permute-start.28 = (f32[1,3,1,4096]{3,2,1,0:T(1,128)S(1)}, f32[1,3,1,4096]{3,2,1,0:T(1,128)S(1)}, u32[]{:S(2)}, u32[]{:S(2)}) collective-permute-start(f32[1,3,1,4096]{3,2,1,0:T(1,128)S(1)} %get-tuple-element.138), channel_id=1, source_target_pairs={{0,8},{8,16},{16,24},{1,9},{9,17},{17,25},{2,10},{10,18},{18,26},{... | collective-permute-start | bytes 147464 | tf_op jit(solution)/shard_map/ppermute | solution.py:247
  128.6 1.3 collective-permute-start.29
  130.7 3.8 %collective-permute-done.29 = f32[1,3,1,4096]{3,2,1,0:T(1,128)S(1)} collective-permute-done((f32[1,3,1,4096]{3,2,1,0:T(1,128)S(1)}, f32[1,3,1,4096]{3,2,1,0:T(1,128)S(1)}, u32[]{:S(2)}, u32[]{:S(2)}) %collective-permute-start.29) | collective-permute-done | bytes 49184 | tf_op jit(solution)/shard_map/ppermute | solution.py:248
  134.9 1.6 multiply_reduce_fusion.11
  136.5 2.6 %maximum_bitcast_fusion.5 = f32[4]{0:T(128)S(1)} fusion(f32[1,1]{1,0:T(1,128)} %bitcast.76, f32[1,1]{1,0:T(1,128)} %bitcast.75, f32[1,1]{1,0:T(1,128)} %bitcast.74, f32[1,1]{1,0:T(1,128)} %bitcast.73), kind=kLoop, calls=%fused_computation.279 | loop fusion | flops 12 | bytes 32 | tf_op jit(solution)/shard_map/broadcast_in_dim | solution.py:294
  139.2 2.6 %collective-permute-start.32 = (f32[1,4,128]{2,1,0:T(4,128)S(1)}, f32[1,4,128]{2,1,0:T(4,128)S(1)}, u32[]{:S(2)}, u32[]{:S(2)}) collective-permute-start(f32[1,4,128]{2,1,0:T(4,128)S(1)} %broadcast_in_dim.51), channel_id=1, source_target_pairs={{0,24},{8,16},{16,8},{24,0},{1,25},{9,17},{17,9},{25,1},{2,26},{10... | collective-permute-start | bytes 6152 | tf_op jit(solution)/shard_map/ppermute | solution.py:58
  142.6 3.1 %collective-permute-start.33 = (f32[1,3,1,4096]{3,2,1,0:T(1,128)S(1)}, f32[1,3,1,4096]{3,2,1,0:T(1,128)S(1)}, u32[]{:S(2)}, u32[]{:S(2)}) collective-permute-start(f32[1,3,1,4096]{3,2,1,0:T(1,128)S(1)} %get-tuple-element.132), channel_id=1, source_target_pairs={{0,8},{8,16},{16,24},{1,9},{9,17},{17,25},{2,10},{10,18},{18,26},{... | collective-permute-start | bytes 147464 | tf_op jit(solution)/shard_map/ppermute | solution.py:247
  147.9 3.8 %collective-permute-done.34 = f32[1,3,1,4096]{3,2,1,0:T(1,128)S(1)} collective-permute-done((f32[1,3,1,4096]{3,2,1,0:T(1,128)S(1)}, f32[1,3,1,4096]{3,2,1,0:T(1,128)S(1)}, u32[]{:S(2)}, u32[]{:S(2)}) %collective-permute-start.34) | collective-permute-done | bytes 49184 | tf_op jit(solution)/shard_map/ppermute | solution.py:248
  152.0 1.6 multiply_reduce_fusion.7
  153.6 2.6 %maximum_bitcast_fusion.6 = f32[4]{0:T(128)S(1)} fusion(f32[1,1]{1,0:T(1,128)} %bitcast.87, f32[1,1]{1,0:T(1,128)} %bitcast.86, f32[1,1]{1,0:T(1,128)} %bitcast.85, f32[1,1]{1,0:T(1,128)} %bitcast.84), kind=kLoop, calls=%fused_computation.280 | loop fusion | flops 12 | bytes 32 | tf_op jit(solution)/shard_map/broadcast_in_dim | solution.py:294
  157.1 1.8 collective-permute-start.37
  159.8 3.4 %collective-permute-start.38 = (f32[1,3,1,4096]{3,2,1,0:T(1,128)S(1)}, f32[1,3,1,4096]{3,2,1,0:T(1,128)S(1)}, u32[]{:S(2)}, u32[]{:S(2)}) collective-permute-start(f32[1,3,1,4096]{3,2,1,0:T(1,128)S(1)} %get-tuple-element.130), channel_id=1, source_target_pairs={{0,8},{8,16},{16,24},{1,9},{9,17},{17,25},{2,10},{10,18},{18,26},{... | collective-permute-start | bytes 147464 | tf_op jit(solution)/shard_map/ppermute | solution.py:247
  163.1 1.3 collective-permute-start.39
  169.5 1.5 multiply_reduce_fusion
  171.0 14.5 %stack.256 = f32[1,23]{1,0:T(1,128)S(1)} concatenate(f32[1,1]{1,0:T(1,128)} %bitcast.95, f32[1,1]{1,0:T(1,128)} %bitcast.96, f32[1,1]{1,0:T(1,128)} %bitcast.97, f32[1,1]{1,0:T(1,128)} %bitcast.98, f32[1,1]{1,0:T(1,128)} %bitcast.100, f32[1,1]{1,0:T(1,128)} %bitcast.101, f32[1,1]{1,0:T(1,128)} %bitcast.102, f32[1,1]{1,0:T(1,128)} %bitcast.104, f32[1,1]{1,0:T(1,128)} %bitcast.105, ...), dimensions={1} | concatenate | bytes 184 | tf_op jit(solution)/shard_map/stack | solution.py:287
  185.6 2.2 collective-permute-start.41
  187.8 1.8 collective-permute-start.42
  190.8 1.9 collective-permute-done.42
  196.4 1.7 copy.51
  198.1 3.5 %all-to-all-start.1 = ((f32[1,3,16,4096]{3,0,1,2:T(1,128)}), f32[1,3,16,4096]{3,0,1,2:T(1,128)S(1)}, u32[]{:S(2)}, u32[]{:S(2)}) async-start(f32[1,3,16,4096]{3,0,1,2:T(1,128)} %copy.51), calls=%async_computation.1 | async-start | bytes 1572864 | tf_op jit(solution)/shard_map/all_to_all | solution.py:323
  201.7 3.2 %collective-permute-start.46 = (f32[8,6]{1,0:T(8,128)S(1)}, f32[8,6]{1,0:T(8,128)S(1)}, u32[]{:S(2)}, u32[]{:S(2)}) collective-permute-start(f32[8,6]{1,0:T(8,128)S(1)} %fusion.111), channel_id=1, source_target_pairs={{0,6},{1,7},{2,4},{3,5},{4,2},{5,3},{6,0},{7,1},{8,14},{9,15},{10,... | collective-permute-start | bytes 584 | tf_op jit(solution)/shard_map/ppermute | solution.py:58
  205.9 5.8 %collective-permute-done.46 = f32[8,6]{1,0:T(8,128)S(1)} collective-permute-done((f32[8,6]{1,0:T(8,128)S(1)}, f32[8,6]{1,0:T(8,128)S(1)}, u32[]{:S(2)}, u32[]{:S(2)}) %collective-permute-start.46) | collective-permute-done | bytes 224 | tf_op jit(solution)/shard_map/ppermute | solution.py:58
  211.6 3.2 %collective-permute-done.45 = f32[8,6]{1,0:T(8,128)S(1)} collective-permute-done((f32[8,6]{1,0:T(8,128)S(1)}, f32[8,6]{1,0:T(8,128)S(1)}, u32[]{:S(2)}, u32[]{:S(2)}) %collective-permute-start.45) | collective-permute-done | bytes 224 | tf_op jit(solution)/shard_map/ppermute | solution.py:58
  215.1 1.7 collective-permute-start.47
  216.9 2.5 %collective-permute-start.49 = (f32[4,6]{0,1:T(8,128)S(1)}, f32[4,6]{0,1:T(8,128)S(1)}, u32[]{:S(2)}, u32[]{:S(2)}) collective-permute-start(f32[4,6]{0,1:T(8,128)S(1)} %get-tuple-element.203), channel_id=1, source_target_pairs={{0,96},{32,64},{64,32},{96,0},{1,97},{33,65},{65,33},{97,1},{2,98}... | collective-permute-start | bytes 296 | tf_op jit(solution)/shard_map/ppermute | solution.py:83
  219.4 2.3 %collective-permute-done.49 = f32[4,6]{0,1:T(8,128)S(1)} collective-permute-done((f32[4,6]{0,1:T(8,128)S(1)}, f32[4,6]{0,1:T(8,128)S(1)}, u32[]{:S(2)}, u32[]{:S(2)}) %collective-permute-start.49) | collective-permute-done | bytes 128 | tf_op jit(solution)/shard_map/ppermute | solution.py:83
  221.7 2.8 %collective-permute-done.48 = f32[4,6]{0,1:T(8,128)S(1)} collective-permute-done((f32[4,6]{0,1:T(8,128)S(1)}, f32[4,6]{0,1:T(8,128)S(1)}, u32[]{:S(2)}, u32[]{:S(2)}) %collective-permute-start.48) | collective-permute-done | bytes 128 | tf_op jit(solution)/shard_map/ppermute | solution.py:83
  225.3 1.5 copy.57
  (174 shorter events, 33.2 us)
Async XLA Ops:
  0.6 25.7 %copy-start.1 = (s32[6]{0:T(128)S(1)}, s32[6]{0:T(128)}, u32[]{:S(2)}) copy-start(s32[6]{0:T(128)} %constant.189) | copy-start | bytes 76
  0.6 25.7 %copy-start.2 = (s32[6]{0:T(128)S(1)}, s32[6]{0:T(128)}, u32[]{:S(2)}) copy-start(s32[6]{0:T(128)} %constant.188) | copy-start | bytes 76
  0.7 25.8 %copy-start = (f32[4,6]{1,0:T(4,128)S(1)}, f32[4,6]{1,0:T(4,128)}, u32[]{:S(2)}) copy-start(f32[4,6]{1,0:T(4,128)} %param.10) | copy-start | bytes 292
  0.7 25.8 %copy-start.3 = (s32[8]{0:T(128)S(1)}, s32[8]{0:T(128)}, u32[]{:S(2)}) copy-start(s32[8]{0:T(128)} %param.15) | copy-start | bytes 100
  0.7 25.7 %collective-permute-start.3 = (f32[4,6]{1,0:T(4,128)}, f32[4,6]{1,0:T(4,128)S(1)}, u32[]{:S(2)}, u32[]{:S(2)}) collective-permute-start(f32[4,6]{1,0:T(4,128)} %param.10), channel_id=1, source_target_pairs={{0,64},{32,96},{64,0},{96,32},{1,65},{33,97},{65,1},{97,33},{2,66}... | collective-permute-start | bytes 296 | tf_op jit(solution)/shard_map/ppermute | solution.py:68
  4.7 21.7 %collective-permute-start.2 = (f32[4,6]{1,0:T(4,128)}, f32[4,6]{1,0:T(4,128)S(1)}, u32[]{:S(2)}, u32[]{:S(2)}) collective-permute-start(f32[4,6]{1,0:T(4,128)} %param.10), channel_id=1, source_target_pairs={{0,96},{32,64},{64,32},{96,0},{1,97},{33,65},{65,33},{97,1},{2,98}... | collective-permute-start | bytes 296 | tf_op jit(solution)/shard_map/ppermute | solution.py:68
  5.5 21.0 %collective-permute-start.4 = (f32[4,6]{1,0:T(4,128)}, f32[4,6]{1,0:T(4,128)S(1)}, u32[]{:S(2)}, u32[]{:S(2)}) collective-permute-start(f32[4,6]{1,0:T(4,128)} %param.10), channel_id=1, source_target_pairs={{0,32},{32,0},{64,96},{96,64},{1,33},{33,1},{65,97},{97,65},{2,34}... | collective-permute-start | bytes 296 | tf_op jit(solution)/shard_map/ppermute | solution.py:68
  22.1 11.8 %all-to-all-start = ((f32[8,2,4096]{2,1,0:T(2,128)}), f32[8,2,4096]{2,1,0:T(2,128)S(1)}, u32[]{:S(2)}, u32[]{:S(2)}) async-start(f32[8,2,4096]{2,1,0:T(2,128)} %shard_map.95), calls=%async_computation | async-start | bytes 524288 | tf_op jit(solution)/shard_map/all_to_all | solution.py:186
  34.1 5.8 %collective-permute-start.1 = (f32[1,2,4096]{2,1,0:T(2,128)S(1)}, f32[1,2,4096]{2,1,0:T(2,128)S(1)}, u32[]{:S(2)}, u32[]{:S(2)}) collective-permute-start(f32[1,2,4096]{2,1,0:T(2,128)S(1)} %get-tuple-element.179), channel_id=1, source_target_pairs={{0,8},{8,16},{16,24},{1,9},{9,17},{17,25},{2,10},{10,18},{18,26},{... | collective-permute-start | bytes 98312 | tf_op jit(solution)/shard_map/ppermute | solution.py:24
  37.6 5.8 %collective-permute-start = (f32[1,2,4096]{2,1,0:T(2,128)S(1)}, f32[1,2,4096]{2,1,0:T(2,128)S(1)}, u32[]{:S(2)}, u32[]{:S(2)}) collective-permute-start(f32[1,2,4096]{2,1,0:T(2,128)S(1)} %get-tuple-element.180), channel_id=1, source_target_pairs={{8,0},{16,8},{24,16},{9,1},{17,9},{25,17},{10,2},{18,10},{26,18},{... | collective-permute-start | bytes 98312 | tf_op jit(solution)/shard_map/ppermute | solution.py:25
  49.1 9.6 %collective-permute-start.6 = (f32[1,4,128]{2,1,0:T(4,128)S(1)}, f32[1,4,128]{2,1,0:T(4,128)S(1)}, u32[]{:S(2)}, u32[]{:S(2)}) collective-permute-start(f32[1,4,128]{2,1,0:T(4,128)S(1)} %broadcast_in_dim.41), channel_id=1, source_target_pairs={{0,16},{8,24},{16,0},{24,8},{1,17},{9,25},{17,1},{25,9},{2,18},{10... | collective-permute-start | bytes 6152 | tf_op jit(solution)/shard_map/ppermute | solution.py:58
  52.1 6.7 %collective-permute-start.7 = (f32[1,4,128]{2,1,0:T(4,128)S(1)}, f32[1,4,128]{2,1,0:T(4,128)S(1)}, u32[]{:S(2)}, u32[]{:S(2)}) collective-permute-start(f32[1,4,128]{2,1,0:T(4,128)S(1)} %broadcast_in_dim.41), channel_id=1, source_target_pairs={{0,24},{8,16},{16,8},{24,0},{1,25},{9,17},{17,9},{25,1},{2,26},{10... | collective-permute-start | bytes 6152 | tf_op jit(solution)/shard_map/ppermute | solution.py:58
  53.4 5.3 %collective-permute-start.5 = (f32[1,4,128]{2,1,0:T(4,128)S(1)}, f32[1,4,128]{2,1,0:T(4,128)S(1)}, u32[]{:S(2)}, u32[]{:S(2)}) collective-permute-start(f32[1,4,128]{2,1,0:T(4,128)S(1)} %broadcast_in_dim.41), channel_id=1, source_target_pairs={{0,8},{8,0},{16,24},{24,16},{1,9},{9,1},{17,25},{25,17},{2,10},{10... | collective-permute-start | bytes 6152 | tf_op jit(solution)/shard_map/ppermute | solution.py:58
  53.5 6.1 %collective-permute-start.8 = (f32[1,3,1,4096]{3,2,1,0:T(1,128)S(1)}, f32[1,3,1,4096]{3,2,1,0:T(1,128)S(1)}, u32[]{:S(2)}, u32[]{:S(2)}) collective-permute-start(f32[1,3,1,4096]{3,2,1,0:T(1,128)S(1)} %get-tuple-element.162), channel_id=1, source_target_pairs={{0,8},{8,16},{16,24},{1,9},{9,17},{17,25},{2,10},{10,18},{18,26},{... | collective-permute-start | bytes 147464 | tf_op jit(solution)/shard_map/ppermute | solution.py:247
  57.4 6.0 %collective-permute-start.9 = (f32[1,3,1,4096]{3,2,1,0:T(1,128)S(1)}, f32[1,3,1,4096]{3,2,1,0:T(1,128)S(1)}, u32[]{:S(2)}, u32[]{:S(2)}) collective-permute-start(f32[1,3,1,4096]{3,2,1,0:T(1,128)S(1)} %get-tuple-element.163), channel_id=1, source_target_pairs={{8,0},{16,8},{24,16},{9,1},{17,9},{25,17},{10,2},{18,10},{26,18},{... | collective-permute-start | bytes 147464 | tf_op jit(solution)/shard_map/ppermute | solution.py:248
  67.9 9.3 %collective-permute-start.11 = (f32[1,4,128]{2,1,0:T(4,128)S(1)}, f32[1,4,128]{2,1,0:T(4,128)S(1)}, u32[]{:S(2)}, u32[]{:S(2)}) collective-permute-start(f32[1,4,128]{2,1,0:T(4,128)S(1)} %broadcast_in_dim.43), channel_id=1, source_target_pairs={{0,16},{8,24},{16,0},{24,8},{1,17},{9,25},{17,1},{25,9},{2,18},{10... | collective-permute-start | bytes 6152 | tf_op jit(solution)/shard_map/ppermute | solution.py:58
  69.3 7.9 %collective-permute-start.12 = (f32[1,4,128]{2,1,0:T(4,128)S(1)}, f32[1,4,128]{2,1,0:T(4,128)S(1)}, u32[]{:S(2)}, u32[]{:S(2)}) collective-permute-start(f32[1,4,128]{2,1,0:T(4,128)S(1)} %broadcast_in_dim.43), channel_id=1, source_target_pairs={{0,24},{8,16},{16,8},{24,0},{1,25},{9,17},{17,9},{25,1},{2,26},{10... | collective-permute-start | bytes 6152 | tf_op jit(solution)/shard_map/ppermute | solution.py:58
  71.9 5.3 %collective-permute-start.10 = (f32[1,4,128]{2,1,0:T(4,128)S(1)}, f32[1,4,128]{2,1,0:T(4,128)S(1)}, u32[]{:S(2)}, u32[]{:S(2)}) collective-permute-start(f32[1,4,128]{2,1,0:T(4,128)S(1)} %broadcast_in_dim.43), channel_id=1, source_target_pairs={{0,8},{8,0},{16,24},{24,16},{1,9},{9,1},{17,25},{25,17},{2,10},{10... | collective-permute-start | bytes 6152 | tf_op jit(solution)/shard_map/ppermute | solution.py:58
  72.0 6.1 %collective-permute-start.13 = (f32[1,3,1,4096]{3,2,1,0:T(1,128)S(1)}, f32[1,3,1,4096]{3,2,1,0:T(1,128)S(1)}, u32[]{:S(2)}, u32[]{:S(2)}) collective-permute-start(f32[1,3,1,4096]{3,2,1,0:T(1,128)S(1)} %get-tuple-element.156), channel_id=1, source_target_pairs={{0,8},{8,16},{16,24},{1,9},{9,17},{17,25},{2,10},{10,18},{18,26},{... | collective-permute-start | bytes 147464 | tf_op jit(solution)/shard_map/ppermute | solution.py:247
  75.9 6.0 %collective-permute-start.14 = (f32[1,3,1,4096]{3,2,1,0:T(1,128)S(1)}, f32[1,3,1,4096]{3,2,1,0:T(1,128)S(1)}, u32[]{:S(2)}, u32[]{:S(2)}) collective-permute-start(f32[1,3,1,4096]{3,2,1,0:T(1,128)S(1)} %get-tuple-element.157), channel_id=1, source_target_pairs={{8,0},{16,8},{24,16},{9,1},{17,9},{25,17},{10,2},{18,10},{26,18},{... | collective-permute-start | bytes 147464 | tf_op jit(solution)/shard_map/ppermute | solution.py:248
  86.5 8.0 %collective-permute-start.16 = (f32[1,4,128]{2,1,0:T(4,128)S(1)}, f32[1,4,128]{2,1,0:T(4,128)S(1)}, u32[]{:S(2)}, u32[]{:S(2)}) collective-permute-start(f32[1,4,128]{2,1,0:T(4,128)S(1)} %broadcast_in_dim.45), channel_id=1, source_target_pairs={{0,16},{8,24},{16,0},{24,8},{1,17},{9,25},{17,1},{25,9},{2,18},{10... | collective-permute-start | bytes 6152 | tf_op jit(solution)/shard_map/ppermute | solution.py:58
  86.6 7.9 %collective-permute-start.17 = (f32[1,4,128]{2,1,0:T(4,128)S(1)}, f32[1,4,128]{2,1,0:T(4,128)S(1)}, u32[]{:S(2)}, u32[]{:S(2)}) collective-permute-start(f32[1,4,128]{2,1,0:T(4,128)S(1)} %broadcast_in_dim.45), channel_id=1, source_target_pairs={{0,24},{8,16},{16,8},{24,0},{1,25},{9,17},{17,9},{25,1},{2,26},{10... | collective-permute-start | bytes 6152 | tf_op jit(solution)/shard_map/ppermute | solution.py:58
  89.2 5.3 %collective-permute-start.15 = (f32[1,4,128]{2,1,0:T(4,128)S(1)}, f32[1,4,128]{2,1,0:T(4,128)S(1)}, u32[]{:S(2)}, u32[]{:S(2)}) collective-permute-start(f32[1,4,128]{2,1,0:T(4,128)S(1)} %broadcast_in_dim.45), channel_id=1, source_target_pairs={{0,8},{8,0},{16,24},{24,16},{1,9},{9,1},{17,25},{25,17},{2,10},{10... | collective-permute-start | bytes 6152 | tf_op jit(solution)/shard_map/ppermute | solution.py:58
  90.1 5.3 %collective-permute-start.18 = (f32[1,3,1,4096]{3,2,1,0:T(1,128)S(1)}, f32[1,3,1,4096]{3,2,1,0:T(1,128)S(1)}, u32[]{:S(2)}, u32[]{:S(2)}) collective-permute-start(f32[1,3,1,4096]{3,2,1,0:T(1,128)S(1)} %get-tuple-element.150), channel_id=1, source_target_pairs={{0,8},{8,16},{16,24},{1,9},{9,17},{17,25},{2,10},{10,18},{18,26},{... | collective-permute-start | bytes 147464 | tf_op jit(solution)/shard_map/ppermute | solution.py:247
  93.2 6.0 %collective-permute-start.19 = (f32[1,3,1,4096]{3,2,1,0:T(1,128)S(1)}, f32[1,3,1,4096]{3,2,1,0:T(1,128)S(1)}, u32[]{:S(2)}, u32[]{:S(2)}) collective-permute-start(f32[1,3,1,4096]{3,2,1,0:T(1,128)S(1)} %get-tuple-element.151), channel_id=1, source_target_pairs={{8,0},{16,8},{24,16},{9,1},{17,9},{25,17},{10,2},{18,10},{26,18},{... | collective-permute-start | bytes 147464 | tf_op jit(solution)/shard_map/ppermute | solution.py:248
  103.9 8.0 %collective-permute-start.21 = (f32[1,4,128]{2,1,0:T(4,128)S(1)}, f32[1,4,128]{2,1,0:T(4,128)S(1)}, u32[]{:S(2)}, u32[]{:S(2)}) collective-permute-start(f32[1,4,128]{2,1,0:T(4,128)S(1)} %broadcast_in_dim.47), channel_id=1, source_target_pairs={{0,16},{8,24},{16,0},{24,8},{1,17},{9,25},{17,1},{25,9},{2,18},{10... | collective-permute-start | bytes 6152 | tf_op jit(solution)/shard_map/ppermute | solution.py:58
  104.8 7.2 %collective-permute-start.22 = (f32[1,4,128]{2,1,0:T(4,128)S(1)}, f32[1,4,128]{2,1,0:T(4,128)S(1)}, u32[]{:S(2)}, u32[]{:S(2)}) collective-permute-start(f32[1,4,128]{2,1,0:T(4,128)S(1)} %broadcast_in_dim.47), channel_id=1, source_target_pairs={{0,24},{8,16},{16,8},{24,0},{1,25},{9,17},{17,9},{25,1},{2,26},{10... | collective-permute-start | bytes 6152 | tf_op jit(solution)/shard_map/ppermute | solution.py:58
  106.6 5.3 %collective-permute-start.20 = (f32[1,4,128]{2,1,0:T(4,128)S(1)}, f32[1,4,128]{2,1,0:T(4,128)S(1)}, u32[]{:S(2)}, u32[]{:S(2)}) collective-permute-start(f32[1,4,128]{2,1,0:T(4,128)S(1)} %broadcast_in_dim.47), channel_id=1, source_target_pairs={{0,8},{8,0},{16,24},{24,16},{1,9},{9,1},{17,25},{25,17},{2,10},{10... | collective-permute-start | bytes 6152 | tf_op jit(solution)/shard_map/ppermute | solution.py:58
  107.5 5.3 %collective-permute-start.23 = (f32[1,3,1,4096]{3,2,1,0:T(1,128)S(1)}, f32[1,3,1,4096]{3,2,1,0:T(1,128)S(1)}, u32[]{:S(2)}, u32[]{:S(2)}) collective-permute-start(f32[1,3,1,4096]{3,2,1,0:T(1,128)S(1)} %get-tuple-element.144), channel_id=1, source_target_pairs={{0,8},{8,16},{16,24},{1,9},{9,17},{17,25},{2,10},{10,18},{18,26},{... | collective-permute-start | bytes 147464 | tf_op jit(solution)/shard_map/ppermute | solution.py:247
  110.6 6.0 %collective-permute-start.24 = (f32[1,3,1,4096]{3,2,1,0:T(1,128)S(1)}, f32[1,3,1,4096]{3,2,1,0:T(1,128)S(1)}, u32[]{:S(2)}, u32[]{:S(2)}) collective-permute-start(f32[1,3,1,4096]{3,2,1,0:T(1,128)S(1)} %get-tuple-element.145), channel_id=1, source_target_pairs={{8,0},{16,8},{24,16},{9,1},{17,9},{25,17},{10,2},{18,10},{26,18},{... | collective-permute-start | bytes 147464 | tf_op jit(solution)/shard_map/ppermute | solution.py:248
  121.1 8.8 %collective-permute-start.26 = (f32[1,4,128]{2,1,0:T(4,128)S(1)}, f32[1,4,128]{2,1,0:T(4,128)S(1)}, u32[]{:S(2)}, u32[]{:S(2)}) collective-permute-start(f32[1,4,128]{2,1,0:T(4,128)S(1)} %broadcast_in_dim.49), channel_id=1, source_target_pairs={{0,16},{8,24},{16,0},{24,8},{1,17},{9,25},{17,1},{25,9},{2,18},{10... | collective-permute-start | bytes 6152 | tf_op jit(solution)/shard_map/ppermute | solution.py:58
  121.9 7.9 %collective-permute-start.27 = (f32[1,4,128]{2,1,0:T(4,128)S(1)}, f32[1,4,128]{2,1,0:T(4,128)S(1)}, u32[]{:S(2)}, u32[]{:S(2)}) collective-permute-start(f32[1,4,128]{2,1,0:T(4,128)S(1)} %broadcast_in_dim.49), channel_id=1, source_target_pairs={{0,24},{8,16},{16,8},{24,0},{1,25},{9,17},{17,9},{25,1},{2,26},{10... | collective-permute-start | bytes 6152 | tf_op jit(solution)/shard_map/ppermute | solution.py:58
  124.6 5.3 %collective-permute-start.25 = (f32[1,4,128]{2,1,0:T(4,128)S(1)}, f32[1,4,128]{2,1,0:T(4,128)S(1)}, u32[]{:S(2)}, u32[]{:S(2)}) collective-permute-start(f32[1,4,128]{2,1,0:T(4,128)S(1)} %broadcast_in_dim.49), channel_id=1, source_target_pairs={{0,8},{8,0},{16,24},{24,16},{1,9},{9,1},{17,25},{25,17},{2,10},{10... | collective-permute-start | bytes 6152 | tf_op jit(solution)/shard_map/ppermute | solution.py:58
  124.6 6.1 %collective-permute-start.28 = (f32[1,3,1,4096]{3,2,1,0:T(1,128)S(1)}, f32[1,3,1,4096]{3,2,1,0:T(1,128)S(1)}, u32[]{:S(2)}, u32[]{:S(2)}) collective-permute-start(f32[1,3,1,4096]{3,2,1,0:T(1,128)S(1)} %get-tuple-element.138), channel_id=1, source_target_pairs={{0,8},{8,16},{16,24},{1,9},{9,17},{17,25},{2,10},{10,18},{18,26},{... | collective-permute-start | bytes 147464 | tf_op jit(solution)/shard_map/ppermute | solution.py:247
  128.6 6.0 %collective-permute-start.29 = (f32[1,3,1,4096]{3,2,1,0:T(1,128)S(1)}, f32[1,3,1,4096]{3,2,1,0:T(1,128)S(1)}, u32[]{:S(2)}, u32[]{:S(2)}) collective-permute-start(f32[1,3,1,4096]{3,2,1,0:T(1,128)S(1)} %get-tuple-element.139), channel_id=1, source_target_pairs={{8,0},{16,8},{24,16},{9,1},{17,9},{25,17},{10,2},{18,10},{26,18},{... | collective-permute-start | bytes 147464 | tf_op jit(solution)/shard_map/ppermute | solution.py:248
  139.1 8.0 %collective-permute-start.31 = (f32[1,4,128]{2,1,0:T(4,128)S(1)}, f32[1,4,128]{2,1,0:T(4,128)S(1)}, u32[]{:S(2)}, u32[]{:S(2)}) collective-permute-start(f32[1,4,128]{2,1,0:T(4,128)S(1)} %broadcast_in_dim.51), channel_id=1, source_target_pairs={{0,16},{8,24},{16,0},{24,8},{1,17},{9,25},{17,1},{25,9},{2,18},{10... | collective-permute-start | bytes 6152 | tf_op jit(solution)/shard_map/ppermute | solution.py:58
  139.2 7.9 %collective-permute-start.32 = (f32[1,4,128]{2,1,0:T(4,128)S(1)}, f32[1,4,128]{2,1,0:T(4,128)S(1)}, u32[]{:S(2)}, u32[]{:S(2)}) collective-permute-start(f32[1,4,128]{2,1,0:T(4,128)S(1)} %broadcast_in_dim.51), channel_id=1, source_target_pairs={{0,24},{8,16},{16,8},{24,0},{1,25},{9,17},{17,9},{25,1},{2,26},{10... | collective-permute-start | bytes 6152 | tf_op jit(solution)/shard_map/ppermute | solution.py:58
  141.8 5.3 %collective-permute-start.30 = (f32[1,4,128]{2,1,0:T(4,128)S(1)}, f32[1,4,128]{2,1,0:T(4,128)S(1)}, u32[]{:S(2)}, u32[]{:S(2)}) collective-permute-start(f32[1,4,128]{2,1,0:T(4,128)S(1)} %broadcast_in_dim.51), channel_id=1, source_target_pairs={{0,8},{8,0},{16,24},{24,16},{1,9},{9,1},{17,25},{25,17},{2,10},{10... | collective-permute-start | bytes 6152 | tf_op jit(solution)/shard_map/ppermute | solution.py:58
  142.6 5.3 %collective-permute-start.33 = (f32[1,3,1,4096]{3,2,1,0:T(1,128)S(1)}, f32[1,3,1,4096]{3,2,1,0:T(1,128)S(1)}, u32[]{:S(2)}, u32[]{:S(2)}) collective-permute-start(f32[1,3,1,4096]{3,2,1,0:T(1,128)S(1)} %get-tuple-element.132), channel_id=1, source_target_pairs={{0,8},{8,16},{16,24},{1,9},{9,17},{17,25},{2,10},{10,18},{18,26},{... | collective-permute-start | bytes 147464 | tf_op jit(solution)/shard_map/ppermute | solution.py:247
  145.8 6.0 %collective-permute-start.34 = (f32[1,3,1,4096]{3,2,1,0:T(1,128)S(1)}, f32[1,3,1,4096]{3,2,1,0:T(1,128)S(1)}, u32[]{:S(2)}, u32[]{:S(2)}) collective-permute-start(f32[1,3,1,4096]{3,2,1,0:T(1,128)S(1)} %get-tuple-element.133), channel_id=1, source_target_pairs={{8,0},{16,8},{24,16},{9,1},{17,9},{25,17},{10,2},{18,10},{26,18},{... | collective-permute-start | bytes 147464 | tf_op jit(solution)/shard_map/ppermute | solution.py:248
  156.2 8.2 %collective-permute-start.36 = (f32[1,4,128]{2,1,0:T(4,128)S(1)}, f32[1,4,128]{2,1,0:T(4,128)S(1)}, u32[]{:S(2)}, u32[]{:S(2)}) collective-permute-start(f32[1,4,128]{2,1,0:T(4,128)S(1)} %broadcast_in_dim.53), channel_id=1, source_target_pairs={{0,16},{8,24},{16,0},{24,8},{1,17},{9,25},{17,1},{25,9},{2,18},{10... | collective-permute-start | bytes 6152 | tf_op jit(solution)/shard_map/ppermute | solution.py:58
  157.1 7.4 %collective-permute-start.37 = (f32[1,4,128]{2,1,0:T(4,128)S(1)}, f32[1,4,128]{2,1,0:T(4,128)S(1)}, u32[]{:S(2)}, u32[]{:S(2)}) collective-permute-start(f32[1,4,128]{2,1,0:T(4,128)S(1)} %broadcast_in_dim.53), channel_id=1, source_target_pairs={{0,24},{8,16},{16,8},{24,0},{1,25},{9,17},{17,9},{25,1},{2,26},{10... | collective-permute-start | bytes 6152 | tf_op jit(solution)/shard_map/ppermute | solution.py:58
  158.9 5.6 %collective-permute-start.35 = (f32[1,4,128]{2,1,0:T(4,128)S(1)}, f32[1,4,128]{2,1,0:T(4,128)S(1)}, u32[]{:S(2)}, u32[]{:S(2)}) collective-permute-start(f32[1,4,128]{2,1,0:T(4,128)S(1)} %broadcast_in_dim.53), channel_id=1, source_target_pairs={{0,8},{8,0},{16,24},{24,16},{1,9},{9,1},{17,25},{25,17},{2,10},{10... | collective-permute-start | bytes 6152 | tf_op jit(solution)/shard_map/ppermute | solution.py:58
  159.8 8.1 %collective-permute-start.38 = (f32[1,3,1,4096]{3,2,1,0:T(1,128)S(1)}, f32[1,3,1,4096]{3,2,1,0:T(1,128)S(1)}, u32[]{:S(2)}, u32[]{:S(2)}) collective-permute-start(f32[1,3,1,4096]{3,2,1,0:T(1,128)S(1)} %get-tuple-element.130), channel_id=1, source_target_pairs={{0,8},{8,16},{16,24},{1,9},{9,17},{17,25},{2,10},{10,18},{18,26},{... | collective-permute-start | bytes 147464 | tf_op jit(solution)/shard_map/ppermute | solution.py:247
  163.1 6.0 %collective-permute-start.39 = (f32[1,3,1,4096]{3,2,1,0:T(1,128)S(1)}, f32[1,3,1,4096]{3,2,1,0:T(1,128)S(1)}, u32[]{:S(2)}, u32[]{:S(2)}) collective-permute-start(f32[1,3,1,4096]{3,2,1,0:T(1,128)S(1)} %get-tuple-element.131), channel_id=1, source_target_pairs={{8,0},{16,8},{24,16},{9,1},{17,9},{25,17},{10,2},{18,10},{26,18},{... | collective-permute-start | bytes 147464 | tf_op jit(solution)/shard_map/ppermute | solution.py:248
  185.6 5.2 %collective-permute-start.41 = (f32[1,23,128]{2,1,0:T(8,128)S(1)}, f32[1,23,128]{2,1,0:T(8,128)S(1)}, u32[]{:S(2)}, u32[]{:S(2)}) collective-permute-start(f32[1,23,128]{2,1,0:T(8,128)S(1)} %broadcast_in_dim.55), channel_id=1, source_target_pairs={{0,16},{8,24},{16,0},{24,8},{1,17},{9,25},{17,1},{25,9},{2,18},{10... | collective-permute-start | bytes 35336 | tf_op jit(solution)/shard_map/ppermute | solution.py:58
  187.8 4.9 %collective-permute-start.42 = (f32[1,23,128]{2,1,0:T(8,128)S(1)}, f32[1,23,128]{2,1,0:T(8,128)S(1)}, u32[]{:S(2)}, u32[]{:S(2)}) collective-permute-start(f32[1,23,128]{2,1,0:T(8,128)S(1)} %broadcast_in_dim.55), channel_id=1, source_target_pairs={{0,24},{8,16},{16,8},{24,0},{1,25},{9,17},{17,9},{25,1},{2,26},{10... | collective-permute-start | bytes 35336 | tf_op jit(solution)/shard_map/ppermute | solution.py:58
  189.6 3.7 %collective-permute-start.40 = (f32[1,23,128]{2,1,0:T(8,128)S(1)}, f32[1,23,128]{2,1,0:T(8,128)S(1)}, u32[]{:S(2)}, u32[]{:S(2)}) collective-permute-start(f32[1,23,128]{2,1,0:T(8,128)S(1)} %broadcast_in_dim.55), channel_id=1, source_target_pairs={{0,8},{8,0},{16,24},{24,16},{1,9},{9,1},{17,25},{25,17},{2,10},{10... | collective-permute-start | bytes 35336 | tf_op jit(solution)/shard_map/ppermute | solution.py:58
  196.3 5.4 %collective-permute-start.43 = (f32[8,6]{1,0:T(8,128)S(1)}, f32[8,6]{1,0:T(8,128)S(1)}, u32[]{:S(2)}, u32[]{:S(2)}) collective-permute-start(f32[8,6]{1,0:T(8,128)S(1)} %broadcast_multiply_fusion), channel_id=1, source_target_pairs={{0,1},{1,0},{2,3},{3,2},{4,5},{5,4},{6,7},{7,6},{8,9},{9,8},{10,11... | collective-permute-start | bytes 584 | tf_op jit(solution)/shard_map/ppermute | solution.py:58
  198.1 27.2 %all-to-all-start.1 = ((f32[1,3,16,4096]{3,0,1,2:T(1,128)}), f32[1,3,16,4096]{3,0,1,2:T(1,128)S(1)}, u32[]{:S(2)}, u32[]{:S(2)}) async-start(f32[1,3,16,4096]{3,0,1,2:T(1,128)} %copy.51), calls=%async_computation.1 | async-start | bytes 1572864 | tf_op jit(solution)/shard_map/all_to_all | solution.py:323
  201.7 9.9 %collective-permute-start.46 = (f32[8,6]{1,0:T(8,128)S(1)}, f32[8,6]{1,0:T(8,128)S(1)}, u32[]{:S(2)}, u32[]{:S(2)}) collective-permute-start(f32[8,6]{1,0:T(8,128)S(1)} %fusion.111), channel_id=1, source_target_pairs={{0,6},{1,7},{2,4},{3,5},{4,2},{5,3},{6,0},{7,1},{8,14},{9,15},{10,... | collective-permute-start | bytes 584 | tf_op jit(solution)/shard_map/ppermute | solution.py:58
  204.9 9.9 %collective-permute-start.45 = (f32[8,6]{1,0:T(8,128)S(1)}, f32[8,6]{1,0:T(8,128)S(1)}, u32[]{:S(2)}, u32[]{:S(2)}) collective-permute-start(f32[8,6]{1,0:T(8,128)S(1)} %fusion.111), channel_id=1, source_target_pairs={{0,4},{1,5},{2,6},{3,7},{4,0},{5,1},{6,2},{7,3},{8,12},{9,13},{10,... | collective-permute-start | bytes 584 | tf_op jit(solution)/shard_map/ppermute | solution.py:58
  205.7 9.1 %collective-permute-start.44 = (f32[8,6]{1,0:T(8,128)S(1)}, f32[8,6]{1,0:T(8,128)S(1)}, u32[]{:S(2)}, u32[]{:S(2)}) collective-permute-start(f32[8,6]{1,0:T(8,128)S(1)} %fusion.111), channel_id=1, source_target_pairs={{0,2},{1,3},{2,0},{3,1},{4,6},{5,7},{6,4},{7,5},{8,10},{9,11},{10,... | collective-permute-start | bytes 584 | tf_op jit(solution)/shard_map/ppermute | solution.py:58
  215.1 4.3 %collective-permute-start.47 = (f32[4,6]{0,1:T(8,128)S(1)}, f32[4,6]{0,1:T(8,128)S(1)}, u32[]{:S(2)}, u32[]{:S(2)}) collective-permute-start(f32[4,6]{0,1:T(8,128)S(1)} %get-tuple-element.202), channel_id=1, source_target_pairs={{0,32},{32,0},{64,96},{96,64},{1,33},{33,1},{65,97},{97,65},{2,34}... | collective-permute-start | bytes 296 | tf_op jit(solution)/shard_map/ppermute | solution.py:83
  216.9 4.8 %collective-permute-start.49 = (f32[4,6]{0,1:T(8,128)S(1)}, f32[4,6]{0,1:T(8,128)S(1)}, u32[]{:S(2)}, u32[]{:S(2)}) collective-permute-start(f32[4,6]{0,1:T(8,128)S(1)} %get-tuple-element.203), channel_id=1, source_target_pairs={{0,96},{32,64},{64,32},{96,0},{1,97},{33,65},{65,33},{97,1},{2,98}... | collective-permute-start | bytes 296 | tf_op jit(solution)/shard_map/ppermute | solution.py:83
  219.4 5.1 %collective-permute-start.48 = (f32[4,6]{0,1:T(8,128)S(1)}, f32[4,6]{0,1:T(8,128)S(1)}, u32[]{:S(2)}, u32[]{:S(2)}) collective-permute-start(f32[4,6]{0,1:T(8,128)S(1)} %get-tuple-element.204), channel_id=1, source_target_pairs={{0,64},{32,96},{64,0},{96,32},{1,65},{33,97},{65,1},{97,33},{2,66}... | collective-permute-start | bytes 296 | tf_op jit(solution)/shard_map/ppermute | solution.py:83
